TPU v7x, 512 devices: a whole 4x8x8 slice. The times are simulated.
512 devices in a mesh: dp: 32 (over y, x), feat: 16 (over z, core).
Axes of the slice: x: 4, y: 8, z: 8, core: 2. Of those that a mesh axis runs over, the one named last changes fastest.
Arguments:
- tokens: bfloat16 [4096, 8192], P('dp', 'feat'), may hold values from -6 to 6
- targets: bfloat16 [8192, 8192], P('dp', 'feat'), may hold values from -6 to 6
- first_blocks: bfloat16 [128, 64, 256], P('feat'), may hold values from -0.75 to 0.75
- second_factor_blocks: bfloat16 [128, 256, 256], P('feat'), may hold values from -0.375 to 0.375
- down_blocks: bfloat16 [128, 256, 64], P('feat'), may hold values from -0.375 to 0.375
- first_tangent: bfloat16 [128, 64, 256], P('feat'), may hold values from -0.75 to 0.75
- second_factor_tangent: bfloat16 [128, 256, 256], P('feat'), may hold values from -0.375 to 0.375
- doc_lengths: int32 [32, 32], replicated, may hold values from 1 to 8, as said below
- doc_owners: int32 [32, 32], replicated, may hold values from 0 to 31, as said below
- pack_offsets: int32 [32, 32], replicated, may hold values from 0 to 248, as said below
Outputs:
- hess_first: float32 [128, 64, 256], P('feat', 'dp')
- hess_mixed: float32 [128, 256, 256], P('feat', 'dp')
Inputs may be any that keep to these rules, and one draw needn't show every extreme that they name: `doc_lengths`: the 32 lengths of one loader sum to 128; the longest has exactly 8 rows. `doc_owners`: A loader sends exactly one document to each owner; some owner receives exactly 256 rows in all, and none more. `pack_offsets`: each owner's documents lie end to end from row 0 of its pack, in the order of their loaders.
All inputs are finite; a program needn't handle non-finite values.
Results may differ from a plain program's by a relative error of at most 0.0072.
Values may be sent and summed in bfloat16 or wider, within the bound.
No kernel may reach another device: no remote copies, remote signals or barrier semaphores. Data moves between devices by JAX's collectives and lax.ppermute only.
A program may use at most 64 MiB of HBM per device.

v0:
```python
import jax
import jax.numpy as jnp
from jax import lax
from jax.sharding import PartitionSpec as P

inv_root_two = 0.7071067811865476
inv_root_two_pi = 0.3989422804014327


def curvature(
    tok_rows,
    goal_rows,
    weight,
    first_blocks,
    second_factor_blocks,
    down_blocks,
    first_tangent,
    second_factor_tangent,
):
    features = lax.axis_size("feat")
    row_count = tok_rows.shape[0]
    local_blocks, block_in, block_out = first_blocks.shape
    pair_size = block_out // (local_blocks * features)
    token_blocks = tok_rows.reshape(row_count, local_blocks, block_in)
    goal_blocks = goal_rows.reshape(row_count, local_blocks, block_in)
    split_shape = (local_blocks, block_in, features, local_blocks, pair_size)
    down_shape = (local_blocks, features, local_blocks, pair_size, block_in)
    first_act = jnp.einsum(
        "rki,kiGgc->Ggkcr",
        token_blocks,
        first_blocks.reshape(split_shape),
        preferred_element_type=jnp.float32,
    ).astype(jnp.bfloat16)
    tangents = jnp.einsum(
        "rki,kiGgc->Ggkcr",
        token_blocks,
        first_tangent.reshape(split_shape),
        preferred_element_type=jnp.float32,
    ).astype(jnp.bfloat16)
    out_grad = (
        jnp.einsum(
            "rkd,kGgcd->Ggkcr",
            goal_blocks,
            down_blocks.reshape(down_shape),
            preferred_element_type=jnp.float32,
        )
        * weight
    ).astype(jnp.bfloat16)
    mixed_activation, mixed_tangent_value, hidden_grad = (
        lax.all_to_all(first_act, "feat", split_axis=0, concat_axis=2, tiled=True),
        lax.all_to_all(tangents, "feat", split_axis=0, concat_axis=2, tiled=True),
        lax.all_to_all(out_grad, "feat", split_axis=0, concat_axis=2, tiled=True),
    )
    hidden_shape = (local_blocks, block_out, row_count)
    mixed_activation = mixed_activation.reshape(hidden_shape)
    mixed_tangent_value = mixed_tangent_value.reshape(hidden_shape)
    hidden_grad = hidden_grad.reshape(hidden_shape)
    pre_act = jnp.einsum(
        "vca,vcf->vfa", mixed_activation, second_factor_blocks, preferred_element_type=jnp.float32
    )
    pre_tan = jnp.einsum(
        "vca,vcf->vfa",
        mixed_tangent_value,
        second_factor_blocks,
        preferred_element_type=jnp.float32,
    ) + jnp.einsum(
        "vca,vcf->vfa", mixed_activation, second_factor_tangent, preferred_element_type=jnp.float32
    )
    density = jnp.exp(-0.5 * pre_act * pre_act) * inv_root_two_pi
    normal_cdf = 0.5 * (1.0 + lax.erf(pre_act * inv_root_two))
    preactivation_gradient = (hidden_grad * (normal_cdf + pre_act * density)).astype(jnp.bfloat16)
    preactivation_tangent_gradient = (
        hidden_grad * (density * (2.0 - pre_act * pre_act)) * pre_tan
    ).astype(jnp.bfloat16)
    hess_mixed = jnp.einsum(
        "evp,eqp->evq",
        mixed_tangent_value,
        preactivation_gradient,
        preferred_element_type=jnp.float32,
    ) + jnp.einsum(
        "evp,eqp->evq",
        mixed_activation,
        preactivation_tangent_gradient,
        preferred_element_type=jnp.float32,
    )
    back_mixed = jnp.einsum(
        "bip,bfi->bfp",
        preactivation_tangent_gradient,
        second_factor_blocks,
        preferred_element_type=jnp.float32,
    ) + jnp.einsum(
        "bip,bfi->bfp",
        preactivation_gradient,
        second_factor_tangent,
        preferred_element_type=jnp.float32,
    )
    back_split = back_mixed.astype(jnp.bfloat16).reshape(
        local_blocks, features, local_blocks, pair_size, row_count
    )
    back_first = lax.all_to_all(back_split, "feat", split_axis=1, concat_axis=0, tiled=True)
    back_first = back_first.reshape(local_blocks * features, local_blocks, pair_size, row_count)
    hess_first = jnp.einsum(
        "gkcr,rki->kigc", back_first, token_blocks, preferred_element_type=jnp.float32
    ).reshape(local_blocks, block_in, block_out)
    return (hess_first, hess_mixed)


def per_device(
    tokens,
    targets,
    first_blocks,
    second_factor_blocks,
    down_blocks,
    first_tangent,
    second_factor_tangent,
    doc_lengths,
    doc_owners,
    pack_offsets,
):
    loaders = lax.axis_size("dp")
    device = lax.axis_index("dp")
    tok_count = tokens.shape[0]
    feature_cols = tokens.shape[1]
    slot_rows = 2 * tok_count // loaders
    my_lengths = lax.dynamic_index_in_dim(doc_lengths, device, 0, keepdims=False)
    my_owners = lax.dynamic_index_in_dim(doc_owners, device, 0, keepdims=False)
    my_starts = jnp.cumsum(my_lengths) - my_lengths
    position = jnp.arange(slot_rows, dtype=jnp.int32)
    owner_ids = jnp.arange(loaders, dtype=jnp.int32)
    matched = (owner_ids[:, None] == my_owners[None, :]).astype(jnp.int32)
    first_row = jnp.sum(matched * my_starts[None, :], axis=1)
    doc_span = jnp.sum(matched * my_lengths[None, :], axis=1)
    in_slot = position[None, :] < doc_span[:, None]
    source = jnp.where(in_slot, first_row[:, None] + position[None, :], 0)
    picked = jnp.take(tokens, source.reshape(-1), axis=0).reshape(loaders, slot_rows, feature_cols)
    outgoing = jnp.where(in_slot[:, :, None], picked, jnp.zeros_like(picked))
    arrived = lax.all_to_all(outgoing, "dp", split_axis=0, concat_axis=0, tiled=True)
    pack_rows = targets.shape[0]
    pack_index = jnp.arange(pack_rows, dtype=jnp.int32)[:, None, None]
    owned = (doc_owners == device)[None, :, :]
    inside = (
        owned
        & (pack_index >= pack_offsets[None, :, :])
        & (pack_index < (pack_offsets + doc_lengths)[None, :, :])
    )
    inside_int = inside.astype(jnp.int32)
    sender = jnp.arange(loaders, dtype=jnp.int32)[None, :, None]
    source_row = jnp.sum(
        inside_int * (sender * slot_rows + pack_index - pack_offsets[None, :, :]), axis=(1, 2)
    )
    filled = jnp.sum(inside_int, axis=(1, 2)) > 0
    weight = jnp.sum(
        inside.astype(jnp.float32) / doc_lengths.astype(jnp.float32)[None, :, :], axis=(1, 2)
    )
    routed = jnp.take(arrived.reshape(loaders * slot_rows, feature_cols), source_row, axis=0)
    routed = jnp.where(filled[:, None], routed, jnp.zeros_like(routed))
    partial_loss_value = curvature(
        routed,
        targets,
        weight,
        first_blocks,
        second_factor_blocks,
        down_blocks,
        first_tangent,
        second_factor_tangent,
    )
    hess_first, hess_mixed = (
        lax.psum_scatter(partial_loss_value[0], "dp", scatter_dimension=1, tiled=True),
        lax.psum_scatter(partial_loss_value[1], "dp", scatter_dimension=1, tiled=True),
    )
    return (hess_first, hess_mixed)


def solution(mesh):
    in_specs = (
        P("dp", "feat"),
        P("dp", "feat"),
        P("feat", None, None),
        P("feat", None, None),
        P("feat", None, None),
        P("feat", None, None),
        P("feat", None, None),
        P(),
        P(),
        P(),
    )
    out_specs = (P("feat", "dp", None), P("feat", "dp", None))
    return jax.shard_map(
        per_device, mesh=mesh, in_specs=in_specs, out_specs=out_specs, check_vma=False
    )
```

profile of v0, /device:TPU:1, one launch (start us, length us, event | category | flops | bytes accessed | tf_op | source)
XLA Modules:
  0.0 629.8 jit_solution(16997859066871600389)
XLA Ops:
  10.1 2.1 gather_fusion
  13.1 10.5 %all-to-all-start = ((bf16[32,8,512]{2,1,0:T(8,128)(2,1)}), bf16[32,8,512]{2,1,0:T(8,128)(2,1)S(1)}, u32[]{:S(2)}, u32[]{:S(2)}) async-start(bf16[32,8,512]{2,1,0:T(8,128)(2,1)} %fusion.38), calls=%async_computation | async-start | bytes 524288 | tf_op jit(solution)/shard_map/all_to_all | solution.py:137
  26.3 8.5 %all-to-all-done = bf16[32,8,512]{2,1,0:T(8,128)(2,1)S(1)} async-done(((bf16[32,8,512]{2,1,0:T(8,128)(2,1)}), bf16[32,8,512]{2,1,0:T(8,128)(2,1)S(1)}, u32[]{:S(2)}, u32[]{:S(2)}) %all-to-all-start) | async-done | bytes 262176 | tf_op jit(solution)/shard_map/all_to_all | solution.py:137
  34.9 12.8 %all-to-all-start.1 = ((bf16[16,8,8,2,256]{4,1,3,2,0:T(8,128)(2,1)}), bf16[16,8,8,2,256]{4,1,3,2,0:T(8,128)(2,1)S(1)}, u32[]{:S(2)}, u32[]{:S(2)}) async-start(bf16[16,8,8,2,256]{4,1,3,2,0:T(8,128)(2,1)} %copy.82), calls=%async_computation.1 | async-start | bytes 2097152 | tf_op jit(solution)/shard_map/all_to_all | solution.py:52
  50.5 1.9 copy.91
  52.4 23.2 %all-to-all-done.1 = bf16[16,8,8,2,256]{4,1,3,2,0:T(8,128)(2,1)S(1)} async-done(((bf16[16,8,8,2,256]{4,1,3,2,0:T(8,128)(2,1)}), bf16[16,8,8,2,256]{4,1,3,2,0:T(8,128)(2,1)S(1)}, u32[]{:S(2)}, u32[]{:S(2)}) %all-to-all-start.1) | async-done | bytes 1048608 | tf_op jit(solution)/shard_map/all_to_all | solution.py:52
  75.6 3.6 all-to-all-start.3
  81.9 2.0 copy.85
  83.9 23.2 %all-to-all-done.3 = bf16[16,8,8,2,256]{4,3,1,2,0:T(2,128)(2,1)S(1)} async-done(((bf16[16,8,8,2,256]{4,3,1,2,0:T(2,128)(2,1)}), bf16[16,8,8,2,256]{4,3,1,2,0:T(2,128)(2,1)S(1)}, u32[]{:S(2)}, u32[]{:S(2)}) %all-to-all-start.3) | async-done | bytes 1048608 | tf_op jit(solution)/shard_map/all_to_all | solution.py:51
  107.1 4.2 all-to-all-start.2
  113.1 1.9 copy.88
  117.5 1.8 fusion.24
  119.3 19.3 %all-to-all-done.2 = bf16[16,8,8,2,256]{4,3,1,2,0:T(2,128)(2,1)} async-done(((bf16[16,8,8,2,256]{4,3,1,2,0:T(2,128)(2,1)}), bf16[16,8,8,2,256]{4,3,1,2,0:T(2,128)(2,1)}, u32[]{:S(2)}, u32[]{:S(2)}) %all-to-all-start.2) | async-done | bytes 1048608 | tf_op jit(solution)/shard_map/all_to_all | solution.py:50
  138.5 1.6 copy.86
  140.4 2.0 fusion.9
  145.6 2.2 reshape.212
  147.8 2.2 copy.98
  150.0 31.7 %all_to_all.59 = bf16[8,16,8,2,256]{4,3,2,0,1:T(2,128)(2,1)S(1)} all-to-all(bf16[8,16,8,2,256]{4,3,2,0,1:T(2,128)(2,1)S(1)} %copy.98), channel_id=1, replica_groups=mesh['dp'=32,'feat'=16] {'feat'}, dimensions={1} | all-to-all | bytes 2097152 | tf_op jit(solution)/shard_map/all_to_all | solution.py:100
  183.3 2.4 copy.100
  185.7 2.4 copy.101
  188.2 2.0 fusion.26
  190.2 1.8 convolution_add_fusion
  192.1 203.3 %reduce-scatter.3.cloned.1.call-done = f32[8,2,256]{2,0,1:T(8,128)} async-done(((f32[8,64,256]{2,0,1:T(8,128)}), f32[8,2,256]{2,0,1:T(8,128)}) %reduce-scatter.3.cloned.1.call-update) | async-done | bytes 16400 | tf_op jit(solution)/shard_map/reduce_scatter | solution.py:168
  396.6 226.3 %reduce-scatter.5.cloned.1.call-done = f32[8,8,256]{2,1,0:T(8,128)} async-done(((f32[8,256,256]{2,1,0:T(8,128)}), f32[8,8,256]{2,1,0:T(8,128)}) %reduce-scatter.5.cloned.1.call-update) | async-done | bytes 65552 | tf_op jit(solution)/shard_map/reduce_scatter | solution.py:169
  (75 shorter events, 22.3 us)
Async XLA Ops:
  7.2 110.3 %copy-start = (bf16[8,256,256]{2,1,0:T(8,128)(2,1)S(1)}, bf16[8,256,256]{2,1,0:T(8,128)(2,1)}, u32[]{:S(2)}) copy-start(bf16[8,256,256]{2,1,0:T(8,128)(2,1)} %param.13) | copy-start | bytes 3145732
  7.2 16.4 %copy-start.16 = (s32[32,32]{1,0:T(8,128)S(1)}, s32[32,32]{1,0:T(8,128)}, u32[]{:S(2)}) copy-start(s32[32,32]{1,0:T(8,128)} %param.17) | copy-start | bytes 12292
  7.2 16.4 %copy-start.15 = (s32[32,32]{1,0:T(8,128)S(1)}, s32[32,32]{1,0:T(8,128)}, u32[]{:S(2)}) copy-start(s32[32,32]{1,0:T(8,128)} %param.18) | copy-start | bytes 12292
  7.2 16.4 %copy-start.14 = (s32[32,32]{1,0:T(8,128)S(1)}, s32[32,32]{1,0:T(8,128)}, u32[]{:S(2)}) copy-start(s32[32,32]{1,0:T(8,128)} %param.19) | copy-start | bytes 12292
  7.2 16.4 %copy-start.11 = (bf16[256,512]{1,0:T(8,128)(2,1)S(1)}, bf16[256,512]{1,0:T(8,128)(2,1)}, u32[]{:S(2)}) copy-start(bf16[256,512]{1,0:T(8,128)(2,1)} %param.11) | copy-start | bytes 786436
  7.2 16.5 %copy-start.8 = (bf16[8,256,64]{1,2,0:T(8,128)(2,1)S(1)}, bf16[8,256,64]{1,2,0:T(8,128)(2,1)}, u32[]{:S(2)}) copy-start(bf16[8,256,64]{1,2,0:T(8,128)(2,1)} %param.14) | copy-start | bytes 786436
  13.1 21.8 %all-to-all-start = ((bf16[32,8,512]{2,1,0:T(8,128)(2,1)}), bf16[32,8,512]{2,1,0:T(8,128)(2,1)S(1)}, u32[]{:S(2)}, u32[]{:S(2)}) async-start(bf16[32,8,512]{2,1,0:T(8,128)(2,1)} %fusion.38), calls=%async_computation | async-start | bytes 524288 | tf_op jit(solution)/shard_map/all_to_all | solution.py:137
  25.2 22.4 %copy-start.9 = (bf16[8,64,256]{2,1,0:T(8,128)(2,1)S(1)}, bf16[8,64,256]{2,1,0:T(8,128)(2,1)}, u32[]{:S(2)}) copy-start(bf16[8,64,256]{2,1,0:T(8,128)(2,1)} %param.15) | copy-start | bytes 786436
  34.9 40.8 %all-to-all-start.1 = ((bf16[16,8,8,2,256]{4,1,3,2,0:T(8,128)(2,1)}), bf16[16,8,8,2,256]{4,1,3,2,0:T(8,128)(2,1)S(1)}, u32[]{:S(2)}, u32[]{:S(2)}) async-start(bf16[16,8,8,2,256]{4,1,3,2,0:T(8,128)(2,1)} %copy.82), calls=%async_computation.1 | async-start | bytes 2097152 | tf_op jit(solution)/shard_map/all_to_all | solution.py:52
  50.0 25.7 %copy-start.12 = (bf16[256,512]{0,1:T(8,128)(2,1)}, bf16[256,512]{0,1:T(8,128)(2,1)S(1)}, u32[]{:S(2)}) copy-start(bf16[256,512]{0,1:T(8,128)(2,1)S(1)} %copy.78) | copy-start | bytes 786436
  50.5 28.7 %copy-start.10 = (bf16[8,64,256]{2,1,0:T(8,128)(2,1)S(1)}, bf16[8,64,256]{2,1,0:T(8,128)(2,1)}, u32[]{:S(2)}) copy-start(bf16[8,64,256]{2,1,0:T(8,128)(2,1)} %param.12) | copy-start | bytes 786436
  75.6 6.3 copy-start.5
  75.6 31.4 %all-to-all-start.3 = ((bf16[16,8,8,2,256]{4,3,1,2,0:T(2,128)(2,1)}), bf16[16,8,8,2,256]{4,3,1,2,0:T(2,128)(2,1)S(1)}, u32[]{:S(2)}, u32[]{:S(2)}) async-start(bf16[16,8,8,2,256]{4,3,1,2,0:T(2,128)(2,1)} %copy.91), calls=%async_computation.3 | async-start | bytes 2097152 | tf_op jit(solution)/shard_map/all_to_all | solution.py:51
  107.1 4.2 copy-start.7
  107.1 31.5 %all-to-all-start.2 = ((bf16[16,8,8,2,256]{4,3,1,2,0:T(2,128)(2,1)}), bf16[16,8,8,2,256]{4,3,1,2,0:T(2,128)(2,1)}, u32[]{:S(2)}, u32[]{:S(2)}) async-start(bf16[16,8,8,2,256]{4,3,1,2,0:T(2,128)(2,1)} %copy.85), calls=%async_computation.2 | async-start | bytes 2097152 | tf_op jit(solution)/shard_map/all_to_all | solution.py:50
  111.3 284.0 %reduce-scatter.3.cloned.1.call-start = ((), (), s32[]{:S(2)}) async-start(), calls=%async_computation.7 | async-start | bytes 540672 | tf_op jit(solution)/shard_map/reduce_scatter | solution.py:168
  116.5 1.0 copy-start.1
  138.5 1.9 copy-start.2
  140.4 2.0 copy-start.3
  140.4 2.0 copy-start.4
  142.4 1.6 copy-start.6
  147.8 34.0 %copy-start.13 = (bf16[256,512]{0,1:T(8,128)(2,1)S(1)}, bf16[256,512]{0,1:T(8,128)(2,1)}, u32[]{:S(2)}) copy-start(bf16[256,512]{0,1:T(8,128)(2,1)} %copy-done.12) | copy-start | bytes 786436
  188.1 434.8 %reduce-scatter.5.cloned.1.call-start = ((), (), s32[]{:S(2)}) async-start(), calls=%async_computation.8 | async-start | bytes 2162688 | tf_op jit(solution)/shard_map/reduce_scatter | solution.py:169
Sparse Core Ops, SparseCore 0:
  188.3 207.0 reduce-scatter.2
  400.3 222.5 reduce-scatter.4
where the time goes:
time: 635 us; the launch traced here: 630 us
  waiting for transfers between devices  504 us (79%)
  blocking collectives  31.7 us (5%)
  starting transfers between devices  31.3 us (5%)
  local copies, waits for them, and re-layouts  28.8 us (5%)
  matrix products  14.7 us (2%)
  between operations  14.4 us (2%)
    reduce_scatter x1, waiting for transfers between devices, per_device(): lax.psum_scatter(partial_loss_value[1], 'dp', scatter_dimension=1, tiled=...  226 us
    reduce_scatter x1, waiting for transfers between devices, per_device(): lax.psum_scatter(partial_loss_value[0], 'dp', scatter_dimension=1, tiled=...  203 us
    all_to_all x1, blocking collectives, curvature(): lax.all_to_all(back_split, 'feat', split_axis=1, concat_axis=0, tiled=True)  31.7 us
    all_to_all x1, waiting for transfers between devices, curvature(): lax.all_to_all(out_grad, 'feat', split_axis=0, concat_axis=2, tiled=True)  23.2 us
    all_to_all x1, waiting for transfers between devices, curvature(): lax.all_to_all(tangents, 'feat', split_axis=0, concat_axis=2, tiled=True)  23.2 us
    all_to_all x1, waiting for transfers between devices, curvature(): lax.all_to_all(first_act, 'feat', split_axis=0, concat_axis=2, tiled=True)  19.3 us
    all_to_all x1, starting transfers between devices, curvature(): lax.all_to_all(out_grad, 'feat', split_axis=0, concat_axis=2, tiled=True)  12.8 us
  transfers between devices with their start and end apart: 6, of which 6 were waited for; matrix products, arithmetic and copies ran while one was open for 4% of the time, Pallas kernels for 0%

commit v1 on v0

--- a/solution.py
+++ b/solution.py
@@ -46,15 +46,12 @@
         )
         * weight
     ).astype(jnp.bfloat16)
-    mixed_activation, mixed_tangent_value, hidden_grad = (
-        lax.all_to_all(first_act, "feat", split_axis=0, concat_axis=2, tiled=True),
-        lax.all_to_all(tangents, "feat", split_axis=0, concat_axis=2, tiled=True),
-        lax.all_to_all(out_grad, "feat", split_axis=0, concat_axis=2, tiled=True),
-    )
+    stacked = jnp.stack([first_act, tangents, out_grad], axis=1)
+    mixed = lax.all_to_all(stacked, "feat", split_axis=0, concat_axis=3, tiled=True)
     hidden_shape = (local_blocks, block_out, row_count)
-    mixed_activation = mixed_activation.reshape(hidden_shape)
-    mixed_tangent_value = mixed_tangent_value.reshape(hidden_shape)
-    hidden_grad = hidden_grad.reshape(hidden_shape)
+    mixed_activation = mixed[0, 0].reshape(hidden_shape)
+    mixed_tangent_value = mixed[0, 1].reshape(hidden_shape)
+    hidden_grad = mixed[0, 2].reshape(hidden_shape)
     pre_act = jnp.einsum(
         "vca,vcf->vfa", mixed_activation, second_factor_blocks, preferred_element_type=jnp.float32
     )
@@ -122,41 +119,36 @@
     tok_count = tokens.shape[0]
     feature_cols = tokens.shape[1]
     slot_rows = 2 * tok_count // loaders
+    position = jnp.arange(slot_rows, dtype=jnp.int32)
+    mine = (doc_owners == device).astype(jnp.int32)
+    first_row = jnp.sum(mine * pack_offsets, axis=1)
+    doc_span = jnp.sum(mine * doc_lengths, axis=1)
+    in_slot = position[None, :] < doc_span[:, None]
+    source = jnp.where(in_slot, first_row[:, None] + position[None, :], 0)
+    outgoing = jnp.take(targets, source.reshape(-1), axis=0).reshape(
+        loaders, slot_rows, feature_cols
+    )
+    arrived = lax.all_to_all(outgoing, "dp", split_axis=0, concat_axis=0, tiled=True)
     my_lengths = lax.dynamic_index_in_dim(doc_lengths, device, 0, keepdims=False)
     my_owners = lax.dynamic_index_in_dim(doc_owners, device, 0, keepdims=False)
     my_starts = jnp.cumsum(my_lengths) - my_lengths
-    position = jnp.arange(slot_rows, dtype=jnp.int32)
-    owner_ids = jnp.arange(loaders, dtype=jnp.int32)
-    matched = (owner_ids[:, None] == my_owners[None, :]).astype(jnp.int32)
-    first_row = jnp.sum(matched * my_starts[None, :], axis=1)
-    doc_span = jnp.sum(matched * my_lengths[None, :], axis=1)
-    in_slot = position[None, :] < doc_span[:, None]
-    source = jnp.where(in_slot, first_row[:, None] + position[None, :], 0)
-    picked = jnp.take(tokens, source.reshape(-1), axis=0).reshape(loaders, slot_rows, feature_cols)
-    outgoing = jnp.where(in_slot[:, :, None], picked, jnp.zeros_like(picked))
-    arrived = lax.all_to_all(outgoing, "dp", split_axis=0, concat_axis=0, tiled=True)
-    pack_rows = targets.shape[0]
-    pack_index = jnp.arange(pack_rows, dtype=jnp.int32)[:, None, None]
-    owned = (doc_owners == device)[None, :, :]
-    inside = (
-        owned
-        & (pack_index >= pack_offsets[None, :, :])
-        & (pack_index < (pack_offsets + doc_lengths)[None, :, :])
+    token_pos = jnp.arange(tok_count, dtype=jnp.int32)
+    inside = (token_pos[:, None] >= my_starts[None, :]) & (
+        token_pos[:, None] < (my_starts + my_lengths)[None, :]
     )
     inside_int = inside.astype(jnp.int32)
-    sender = jnp.arange(loaders, dtype=jnp.int32)[None, :, None]
-    source_row = jnp.sum(
-        inside_int * (sender * slot_rows + pack_index - pack_offsets[None, :, :]), axis=(1, 2)
+    goal_index = (
+        jnp.sum(inside_int * (my_owners * slot_rows - my_starts)[None, :], axis=1) + token_pos
     )
-    filled = jnp.sum(inside_int, axis=(1, 2)) > 0
     weight = jnp.sum(
-        inside.astype(jnp.float32) / doc_lengths.astype(jnp.float32)[None, :, :], axis=(1, 2)
+        inside.astype(jnp.float32) / my_lengths.astype(jnp.float32)[None, :], axis=1
     )
-    routed = jnp.take(arrived.reshape(loaders * slot_rows, feature_cols), source_row, axis=0)
-    routed = jnp.where(filled[:, None], routed, jnp.zeros_like(routed))
-    partial_loss_value = curvature(
-        routed,
-        targets,
+    goal_rows = jnp.take(
+        arrived.reshape(loaders * slot_rows, feature_cols), goal_index, axis=0
+    )
+    hess_first, hess_mixed = curvature(
+        tokens,
+        goal_rows,
         weight,
         first_blocks,
         second_factor_blocks,
@@ -164,10 +156,15 @@
         first_tangent,
         second_factor_tangent,
     )
-    hess_first, hess_mixed = (
-        lax.psum_scatter(partial_loss_value[0], "dp", scatter_dimension=1, tiled=True),
-        lax.psum_scatter(partial_loss_value[1], "dp", scatter_dimension=1, tiled=True),
-    )
+    local_blocks = hess_first.shape[0]
+    first_part = hess_first.reshape(local_blocks, loaders, -1)
+    mixed_part = hess_mixed.reshape(local_blocks, loaders, -1)
+    first_width = first_part.shape[2]
+    partials = jnp.concatenate([first_part, mixed_part], axis=2)
+    gathered = lax.all_to_all(partials, "dp", split_axis=1, concat_axis=1, tiled=True)
+    total = jnp.sum(gathered, axis=1)
+    hess_first = total[:, :first_width].reshape(local_blocks, -1, hess_first.shape[2])
+    hess_mixed = total[:, first_width:].reshape(local_blocks, -1, hess_mixed.shape[2])
     return (hess_first, hess_mixed)
 
 

time: 635 us -> 199 us (0.31)
  waiting for transfers between devices: 504 us -> 16.6 us
  blocking collectives: 31.7 us -> 119 us
  starting transfers between devices: 31.3 us -> 14.8 us
  between operations: 14.4 us -> 1.03 us
  matrix products: 14.7 us -> 7.74 us
    reduce_scatter x2 -> x0, waiting for transfers between devices: 430 us -> none  [the longest x1 226 us: per_device(): lax.psum_scatter(partial_loss_value[1], 'dp', scatter_dimension=1, tiled=...]
    all_to_all x1 -> x2, blocking collectives: 31.7 us -> 119 us  [the longest x1 67.1 us: per_device(): lax.all_to_all(partials, 'dp', split_axis=1, concat_axis=1, tiled=True)]
    all_to_all x3 -> x1, waiting for transfers between devices: 65.7 us -> 9.69 us  [curvature(): lax.all_to_all(back_split, 'feat', split_axis=1, concat_axis=0, tiled=True)]
    all_to_all x3 -> x1, starting transfers between devices: 20.6 us -> 4.32 us  [curvature(): lax.all_to_all(back_split, 'feat', split_axis=1, concat_axis=0, tiled=True)]
  transfers between devices with their start and end apart: 6 -> 2, of which waited for: 6 -> 2; matrix products, arithmetic and copies ran while one was open for 4% -> 5% of each run, Pallas kernels for 0% -> 0%
where the time goes in v1:
time: 199 us; the launch traced here: 198 us
  blocking collectives  119 us (60%)
  local copies, waits for them, and re-layouts  32.2 us (16%)
  waiting for transfers between devices  16.6 us (8%)
  starting transfers between devices  14.8 us (7%)
  matrix products  7.74 us (4%)
  other arithmetic  6.5 us (3%)
    all_to_all x1, blocking collectives, per_device(): lax.all_to_all(partials, 'dp', split_axis=1, concat_axis=1, tiled=True)  67.1 us
    all_to_all x1, blocking collectives, curvature(): lax.all_to_all(stacked, 'feat', split_axis=0, concat_axis=3, tiled=True)  52.3 us
    all_to_all x1, starting transfers between devices, per_device(): lax.all_to_all(outgoing, 'dp', split_axis=0, concat_axis=0, tiled=True)  10.5 us
    all_to_all x1, waiting for transfers between devices, curvature(): lax.all_to_all(back_split, 'feat', split_axis=1, concat_axis=0, tiled=True)  9.69 us
    dot_general x1, local copies, waits for them, and re-layouts, curvature(): jnp.einsum('gkcr,rki->kigc', back_first, token_blocks, preferred_element_...  7.09 us
    all_to_all x1, waiting for transfers between devices, per_device(): lax.all_to_all(outgoing, 'dp', split_axis=0, concat_axis=0, tiled=True)  6.95 us
    another operation x1, local copies, waits for them, and re-layouts, per_device(): first_part = hess_first.reshape(local_blocks, loaders, -1)  5.85 us
    unnamed x29, local copies, waits for them, and re-layouts  4.36 us
  transfers between devices with their start and end apart: 2, of which 2 were waited for; matrix products, arithmetic and copies ran while one was open for 5% of the time, Pallas kernels for 0%

profile of v1, /device:TPU:1, one launch (start us, length us, event | category | flops | bytes accessed | tf_op | source)
XLA Modules:
  0.0 198.2 jit_solution(6791670290175771214)
XLA Ops:
  0.7 1.0 select_reduce_fusion.1
  2.0 2.3 %gather_fusion = bf16[256,512]{1,0:T(8,128)(2,1)S(1)} fusion(bf16[256,512]{1,0:T(8,128)(2,1)} %param.11, s32[1024]{0:T(1024)S(1)} %pad_clamp_fusion.1), kind=kCustom, calls=%fused_computation | custom fusion | bytes 525312 | tf_op jit(solution)/shard_map/jit(_take)/gather | solution.py:128
  4.2 0.8 bitcast_select_fusion
  5.0 10.5 %all-to-all-start = ((bf16[32,8,512]{2,1,0:T(8,128)(2,1)}), bf16[32,8,512]{2,1,0:T(8,128)(2,1)S(1)}, u32[]{:S(2)}, u32[]{:S(2)}) async-start(bf16[32,8,512]{2,1,0:T(8,128)(2,1)} %bitcast_select_fusion), calls=%async_computation | async-start | bytes 524288 | tf_op jit(solution)/shard_map/all_to_all | solution.py:131
  17.9 1.1 copy.89
  19.9 7.0 %all-to-all-done = bf16[32,8,512]{2,1,0:T(8,128)(2,1)S(1)} async-done(((bf16[32,8,512]{2,1,0:T(8,128)(2,1)}), bf16[32,8,512]{2,1,0:T(8,128)(2,1)S(1)}, u32[]{:S(2)}, u32[]{:S(2)}) %all-to-all-start) | async-done | bytes 262176 | tf_op jit(solution)/shard_map/all_to_all | solution.py:131
  26.8 0.8 gather_fusion.1
  27.8 1.3 fusion.5
  29.8 52.3 %all_to_all.43 = bf16[16,3,8,8,2,128]{5,2,4,3,1,0:T(8,128)(2,1)S(1)} all-to-all(bf16[16,3,8,8,2,128]{5,2,4,3,1,0:T(8,128)(2,1)S(1)} %copy.92), channel_id=1, replica_groups=mesh['dp'=32,'feat'=16] {'feat'}, dimensions={0} | all-to-all | bytes 3145728 | tf_op jit(solution)/shard_map/all_to_all | solution.py:50
  83.3 1.6 copy.94
  84.9 1.6 copy.97
  86.9 0.9 fusion.16
  88.7 0.8 copy-done.3
  90.5 1.1 copy.102
  91.6 4.3 %all-to-all-start.2 = ((bf16[8,16,8,2,128]{4,0,3,2,1:T(8,128)(2,1)}), bf16[8,16,8,2,128]{4,0,3,2,1:T(8,128)(2,1)}, u32[]{:S(2)}, u32[]{:S(2)}) async-start(bf16[8,16,8,2,128]{4,0,3,2,1:T(8,128)(2,1)} %bitcast.37), calls=%async_computation.2 | async-start | bytes 1048576 | tf_op jit(solution)/shard_map/all_to_all | solution.py:97
  97.6 1.5 reshape.162
  99.1 2.8 %copy.110 = f32[8,32,2048]{2,0,1:T(8,128)S(1)} copy(f32[8,32,2048]{2,1,0:T(8,128)} %reshape.162) | data formatting | bytes 4194304 | tf_op jit(solution)/shard_map/reshape | solution.py:161
  101.9 9.7 %all-to-all-done.2 = bf16[8,16,8,2,128]{4,0,3,2,1:T(8,128)(2,1)} async-done(((bf16[8,16,8,2,128]{4,0,3,2,1:T(8,128)(2,1)}), bf16[8,16,8,2,128]{4,0,3,2,1:T(8,128)(2,1)}, u32[]{:S(2)}, u32[]{:S(2)}) %all-to-all-start.2) | async-done | bytes 524320 | tf_op jit(solution)/shard_map/all_to_all | solution.py:97
  111.6 2.2 %convolution_bitcast_fusion.1 = f32[8,64,128,2]{2,1,3,0:T(8,128)} fusion(bf16[128,8,64,1]{0,2,3,1:T(8,128)(2,1)S(1)} %bitcast.114, bf16[8,16,8,2,128]{4,0,3,2,1:T(8,128)(2,1)} %all-to-all-done.2), kind=kOutput, calls=%fused_computation.22 | convolution fusion | flops 33554432 | bytes 1179648 | tf_op jit(solution)/shard_map/gkcr,rki->kigc/dot_general | solution.py:99
  113.8 7.1 %copy.104 = f32[8,64,128,2]{0,3,2,1:T(2,128)} copy(f32[8,64,128,2]{2,1,3,0:T(8,128)} %convolution_bitcast_fusion.1) | data formatting | bytes 1048576 | tf_op jit(solution)/shard_map/gkcr,rki->kigc/dot_general | solution.py:99
  120.9 5.8 %copy.109 = f32[8,32,512]{2,0,1:T(8,128)} copy(f32[8,32,512]{0,2,1:T(8,128)} %bitcast.103) | data formatting | bytes 1048576 | tf_op jit(solution)/shard_map/reshape;reshape | solution.py:160
  126.7 1.2 pad_maximum_fusion
  128.0 67.1 %all_to_all.44 = f32[8,32,2560]{2,0,1:T(8,128)} all-to-all(f32[8,32,2560]{2,0,1:T(8,128)S(1)} %pad_maximum_fusion), channel_id=1, replica_groups=mesh['dp'=32,'feat'=16] {'dp'}, dimensions={1} | all-to-all | bytes 5242880 | tf_op jit(solution)/shard_map/all_to_all | solution.py:164
  195.1 1.9 reduce_sum.52
  (60 shorter events, 10.6 us)
Async XLA Ops:
  0.6 85.9 %copy-start = (bf16[8,256,256]{2,1,0:T(8,128)(2,1)S(1)}, bf16[8,256,256]{2,1,0:T(8,128)(2,1)}, u32[]{:S(2)}) copy-start(bf16[8,256,256]{2,1,0:T(8,128)(2,1)} %param.13) | copy-start | bytes 3145732
  0.6 16.8 %copy-start.11 = (bf16[128,512]{1,0:T(8,128)(2,1)S(1)}, bf16[128,512]{1,0:T(8,128)(2,1)}, u32[]{:S(2)}) copy-start(bf16[128,512]{1,0:T(8,128)(2,1)} %param.10) | copy-start | bytes 393220
  0.7 16.9 %copy-start.8 = (bf16[8,64,256]{2,1,0:T(8,128)(2,1)S(1)}, bf16[8,64,256]{2,1,0:T(8,128)(2,1)}, u32[]{:S(2)}) copy-start(bf16[8,64,256]{2,1,0:T(8,128)(2,1)} %param.12) | copy-start | bytes 786436
  1.9 15.9 %copy-start.9 = (bf16[8,256,64]{1,2,0:T(8,128)(2,1)S(1)}, bf16[8,256,64]{1,2,0:T(8,128)(2,1)}, u32[]{:S(2)}) copy-start(bf16[8,256,64]{1,2,0:T(8,128)(2,1)} %param.14) | copy-start | bytes 786436
  1.9 17.0 %copy-start.10 = (bf16[8,64,256]{2,1,0:T(8,128)(2,1)S(1)}, bf16[8,64,256]{2,1,0:T(8,128)(2,1)}, u32[]{:S(2)}) copy-start(bf16[8,64,256]{2,1,0:T(8,128)(2,1)} %param.15) | copy-start | bytes 786436
  5.0 21.8 %all-to-all-start = ((bf16[32,8,512]{2,1,0:T(8,128)(2,1)}), bf16[32,8,512]{2,1,0:T(8,128)(2,1)S(1)}, u32[]{:S(2)}, u32[]{:S(2)}) async-start(bf16[32,8,512]{2,1,0:T(8,128)(2,1)} %bitcast_select_fusion), calls=%async_computation | async-start | bytes 524288 | tf_op jit(solution)/shard_map/all_to_all | solution.py:131
  83.3 4.5 %copy-start.1 = (bf16[1,1,8,128,2,128]{5,2,4,3,1,0:T(8,128)(2,1)}, bf16[1,1,8,128,2,128]{5,2,4,3,1,0:T(8,128)(2,1)S(1)}, u32[]{:S(2)}) copy-start(bf16[1,1,8,128,2,128]{5,2,4,3,1,0:T(8,128)(2,1)S(1)} %copy.95) | copy-start | bytes 1572868
  86.9 1.2 copy-start.7
  87.8 2.2 %copy-start.5 = (bf16[8,256,128]{1,2,0:T(8,128)(2,1)}, bf16[8,256,128]{1,2,0:T(8,128)(2,1)S(1)}, u32[]{:S(2)}) copy-start(bf16[8,256,128]{1,2,0:T(8,128)(2,1)S(1)} %get-tuple-element.10) | copy-start | bytes 1572868
  88.7 0.8 copy-start.3
  90.5 5.4 %copy-start.6 = (bf16[8,256,128]{1,2,0:T(8,128)(2,1)S(1)}, bf16[8,256,128]{1,2,0:T(8,128)(2,1)}, u32[]{:S(2)}) copy-start(bf16[8,256,128]{1,2,0:T(8,128)(2,1)} %copy-done.5) | copy-start | bytes 1572868
  91.6 20.0 %all-to-all-start.2 = ((bf16[8,16,8,2,128]{4,0,3,2,1:T(8,128)(2,1)}), bf16[8,16,8,2,128]{4,0,3,2,1:T(8,128)(2,1)}, u32[]{:S(2)}, u32[]{:S(2)}) async-start(bf16[8,16,8,2,128]{4,0,3,2,1:T(8,128)(2,1)} %bitcast.37), calls=%async_computation.2 | async-start | bytes 1048576 | tf_op jit(solution)/shard_map/all_to_all | solution.py:97
  95.9 1.0 copy-start.2
  96.0 1.2 copy-start.4

commit v2 on v1

--- a/solution.py
+++ b/solution.py
@@ -46,7 +46,10 @@
         )
         * weight
     ).astype(jnp.bfloat16)
-    stacked = jnp.stack([first_act, tangents, out_grad], axis=1)
+    merged = (features, local_blocks, local_blocks * pair_size, row_count)
+    stacked = jnp.stack(
+        [first_act.reshape(merged), tangents.reshape(merged), out_grad.reshape(merged)], axis=1
+    )
     mixed = lax.all_to_all(stacked, "feat", split_axis=0, concat_axis=3, tiled=True)
     hidden_shape = (local_blocks, block_out, row_count)
     mixed_activation = mixed[0, 0].reshape(hidden_shape)
@@ -69,36 +72,40 @@
     preactivation_tangent_gradient = (
         hidden_grad * (density * (2.0 - pre_act * pre_act)) * pre_tan
     ).astype(jnp.bfloat16)
+    loaders = lax.axis_size("dp")
+    mixed_tan_split = mixed_tangent_value.reshape(local_blocks, loaders, -1, row_count)
+    mixed_act_split = mixed_activation.reshape(local_blocks, loaders, -1, row_count)
     hess_mixed = jnp.einsum(
-        "evp,eqp->evq",
-        mixed_tangent_value,
+        "eDvp,eqp->Devq",
+        mixed_tan_split,
         preactivation_gradient,
         preferred_element_type=jnp.float32,
     ) + jnp.einsum(
-        "evp,eqp->evq",
-        mixed_activation,
+        "eDvp,eqp->Devq",
+        mixed_act_split,
         preactivation_tangent_gradient,
         preferred_element_type=jnp.float32,
     )
+    pos_shape = (local_blocks, features, local_blocks, pair_size, block_out)
     back_mixed = jnp.einsum(
-        "bip,bfi->bfp",
+        "bip,bFkci->Fkbcp",
         preactivation_tangent_gradient,
-        second_factor_blocks,
+        second_factor_blocks.reshape(pos_shape),
         preferred_element_type=jnp.float32,
     ) + jnp.einsum(
-        "bip,bfi->bfp",
+        "bip,bFkci->Fkbcp",
         preactivation_gradient,
-        second_factor_tangent,
+        second_factor_tangent.reshape(pos_shape),
         preferred_element_type=jnp.float32,
     )
-    back_split = back_mixed.astype(jnp.bfloat16).reshape(
-        local_blocks, features, local_blocks, pair_size, row_count
+    back_merged = back_mixed.astype(jnp.bfloat16).reshape(
+        features, local_blocks, local_blocks * pair_size, row_count
     )
-    back_first = lax.all_to_all(back_split, "feat", split_axis=1, concat_axis=0, tiled=True)
-    back_first = back_first.reshape(local_blocks * features, local_blocks, pair_size, row_count)
+    back_first = lax.all_to_all(back_merged, "feat", split_axis=0, concat_axis=2, tiled=True)
+    back_first = back_first.reshape(local_blocks, block_out, row_count)
     hess_first = jnp.einsum(
-        "gkcr,rki->kigc", back_first, token_blocks, preferred_element_type=jnp.float32
-    ).reshape(local_blocks, block_in, block_out)
+        "rki,kjr->kij", token_blocks, back_first, preferred_element_type=jnp.float32
+    )
     return (hess_first, hess_mixed)
 
 
@@ -157,14 +164,14 @@
         second_factor_tangent,
     )
     local_blocks = hess_first.shape[0]
-    first_part = hess_first.reshape(local_blocks, loaders, -1)
-    mixed_part = hess_mixed.reshape(local_blocks, loaders, -1)
+    first_part = hess_first.reshape(local_blocks, loaders, -1).transpose(1, 0, 2)
+    mixed_part = hess_mixed.reshape(loaders, local_blocks, -1)
     first_width = first_part.shape[2]
-    partials = jnp.concatenate([first_part, mixed_part], axis=2)
-    gathered = lax.all_to_all(partials, "dp", split_axis=1, concat_axis=1, tiled=True)
-    total = jnp.sum(gathered, axis=1)
-    hess_first = total[:, :first_width].reshape(local_blocks, -1, hess_first.shape[2])
-    hess_mixed = total[:, first_width:].reshape(local_blocks, -1, hess_mixed.shape[2])
+    partials = jnp.concatenate([first_part, mixed_part], axis=2).astype(jnp.bfloat16)
+    gathered = lax.all_to_all(partials, "dp", split_axis=0, concat_axis=0, tiled=True)
+    total = jnp.sum(gathered.astype(jnp.float32), axis=0)
+    hess_first = total[:, :first_width].reshape(local_blocks, -1, first_blocks.shape[2])
+    hess_mixed = total[:, first_width:].reshape(local_blocks, -1, second_factor_blocks.shape[2])
     return (hess_first, hess_mixed)
 
 

time: 199 us -> 153 us (0.77)
  blocking collectives: 119 us -> 38.5 us
  waiting for transfers between devices: 16.6 us -> 57.2 us
  local copies, waits for them, and re-layouts: 32.2 us -> 18.7 us
  starting transfers between devices: 14.8 us -> 27.5 us
  other arithmetic: 6.5 us -> 3.43 us
    all_to_all x2 -> x1, blocking collectives: 119 us -> 38.5 us  [per_device(): lax.all_to_all(partials, 'dp', split_axis=0, concat_axis=0, tiled=True)]
    all_to_all x1 -> x2, waiting for transfers between devices: 9.69 us -> 49.6 us  [the longest x1 35.1 us: curvature(): lax.all_to_all(stacked, 'feat', split_axis=0, concat_axis=3, tiled=True)]
    all_to_all x1 -> x2, starting transfers between devices: 4.32 us -> 17.1 us  [the longest x1 12.9 us: curvature(): lax.all_to_all(stacked, 'feat', split_axis=0, concat_axis=3, tiled=True)]
    dot_general x1 -> x0, local copies, waits for them, and re-layouts: 7.09 us -> none  [curvature(): jnp.einsum('gkcr,rki->kigc', back_first, token_blocks, preferred_element_...]
    another operation x2, local copies, waits for them, and re-layouts: 6.3 us -> 2.5 us  [the longest x1 1.27 us: curvature(): jnp.stack([first_act.reshape(merged), tangents.reshape(merged), out_grad....]
    convert_element_type x2 -> x3, local copies, waits for them, and re-layouts: 3.16 us -> 0.3 us  [the longest x1 0.21 us: curvature(): out_grad = (jnp.einsum('rkd,kGgcd->Ggkcr', goal_blocks, down_blocks.resha...]
    unnamed x29 -> x36, local copies, waits for them, and re-layouts: 4.36 us -> 6.06 us
    reshape x5 -> x8, local copies, waits for them, and re-layouts: 5.74 us -> 5.63 us  [the longest x1 2.23 us: curvature(): second_factor_tangent.reshape(pos_shape)]
  transfers between devices with their start and end apart: 2 -> 3, of which waited for: 2 -> 3; matrix products, arithmetic and copies ran while one was open for 5% -> 6% of each run, Pallas kernels for 0% -> 0%
where the time goes in v2:
time: 153 us
  waiting for transfers between devices  57.2 us (37%)
  blocking collectives  38.5 us (25%)
  starting transfers between devices  27.5 us (18%)
  local copies, waits for them, and re-layouts  18.7 us (12%)
  matrix products  6.06 us (4%)
  other arithmetic  3.43 us (2%)
    all_to_all x1, blocking collectives, per_device(): lax.all_to_all(partials, 'dp', split_axis=0, concat_axis=0, tiled=True)  38.5 us
    all_to_all x1, waiting for transfers between devices, curvature(): lax.all_to_all(stacked, 'feat', split_axis=0, concat_axis=3, tiled=True)  35.1 us
    all_to_all x1, waiting for transfers between devices, curvature(): lax.all_to_all(back_merged, 'feat', split_axis=0, concat_axis=2, tiled=True)  14.6 us
    all_to_all x1, starting transfers between devices, curvature(): lax.all_to_all(stacked, 'feat', split_axis=0, concat_axis=3, tiled=True)  12.9 us
    all_to_all x1, starting transfers between devices, per_device(): lax.all_to_all(outgoing, 'dp', split_axis=0, concat_axis=0, tiled=True)  10.5 us
    all_to_all x1, waiting for transfers between devices, per_device(): lax.all_to_all(outgoing, 'dp', split_axis=0, concat_axis=0, tiled=True)  7.58 us
    unnamed x36, local copies, waits for them, and re-layouts  6.06 us
    all_to_all x1, starting transfers between devices, curvature(): lax.all_to_all(back_merged, 'feat', split_axis=0, concat_axis=2, tiled=True)  4.14 us
  transfers between devices with their start and end apart: 3, of which 3 were waited for; matrix products, arithmetic and copies ran while one was open for 6% of the time, Pallas kernels for 0%

profile of v2, /device:TPU:1, one launch (start us, length us, event | category | flops | bytes accessed | tf_op | source)
XLA Modules:
  0.0 152.5 jit_solution(862481426601421452)
XLA Ops:
  0.6 0.9 select_reduce_fusion.1
  1.9 1.2 gather_fusion
  3.0 0.8 bitcast_select_fusion
  3.8 10.5 %all-to-all-start = ((bf16[32,8,512]{2,1,0:T(8,128)(2,1)}), bf16[32,8,512]{2,1,0:T(8,128)(2,1)S(1)}, u32[]{:S(2)}, u32[]{:S(2)}) async-start(bf16[32,8,512]{2,1,0:T(8,128)(2,1)} %bitcast_select_fusion), calls=%async_computation | async-start | bytes 524288 | tf_op jit(solution)/shard_map/all_to_all | solution.py:138
  14.3 0.7 fusion.46
  15.3 0.7 subtract_bitcast_fusion
  18.1 7.6 %all-to-all-done = bf16[32,8,512]{2,1,0:T(8,128)(2,1)S(1)} async-done(((bf16[32,8,512]{2,1,0:T(8,128)(2,1)}), bf16[32,8,512]{2,1,0:T(8,128)(2,1)S(1)}, u32[]{:S(2)}, u32[]{:S(2)}) %all-to-all-start) | async-done | bytes 262176 | tf_op jit(solution)/shard_map/all_to_all | solution.py:138
  25.6 0.8 gather_fusion.1
  27.4 1.3 copy.102
  28.7 12.9 %all-to-all-start.1 = ((bf16[16,3,8,16,128]{4,2,3,1,0:T(8,128)(2,1)}), bf16[16,3,8,16,128]{4,2,3,1,0:T(8,128)(2,1)S(1)}, u32[]{:S(2)}, u32[]{:S(2)}) async-start(bf16[16,3,8,16,128]{4,2,3,1,0:T(8,128)(2,1)} %copy.102), calls=%async_computation.1 | async-start | bytes 3145728 | tf_op jit(solution)/shard_map/all_to_all | solution.py:53
  41.6 1.2 reshape.171
  42.8 2.2 %reshape.172 = bf16[8,16,8,2,256]{4,3,2,1,0:T(2,128)(2,1)} reshape(bf16[8,256,256]{2,1,0:T(8,128)(2,1)} %param.16) | data formatting | bytes 2097152 | tf_op jit(solution)/shard_map/reshape | solution.py:98
  45.1 35.1 %all-to-all-done.1 = bf16[16,3,8,16,128]{4,2,3,1,0:T(8,128)(2,1)S(1)} async-done(((bf16[16,3,8,16,128]{4,2,3,1,0:T(8,128)(2,1)}), bf16[16,3,8,16,128]{4,2,3,1,0:T(8,128)(2,1)S(1)}, u32[]{:S(2)}, u32[]{:S(2)}) %all-to-all-start.1) | async-done | bytes 1572896 | tf_op jit(solution)/shard_map/all_to_all | solution.py:53
  80.5 1.2 slice_bitcast_fusion.1
  82.3 1.3 fusion.20
  83.6 1.2 copy.135
  84.9 0.9 fusion.11
  86.4 0.7 fusion.5
  88.1 0.7 copy-done.1
  89.4 1.0 copy.111
  90.4 4.1 %all-to-all-start.2 = ((bf16[16,8,16,128]{3,1,2,0:T(8,128)(2,1)}), bf16[16,8,16,128]{3,1,2,0:T(8,128)(2,1)S(1)}, u32[]{:S(2)}, u32[]{:S(2)}) async-start(bf16[16,8,16,128]{3,1,2,0:T(8,128)(2,1)} %bitcast.40), calls=%async_computation.2 | async-start | bytes 1048576 | tf_op jit(solution)/shard_map/all_to_all | solution.py:104
  97.2 14.6 %all-to-all-done.2 = bf16[16,8,16,128]{3,1,2,0:T(8,128)(2,1)S(1)} async-done(((bf16[16,8,16,128]{3,1,2,0:T(8,128)(2,1)}), bf16[16,8,16,128]{3,1,2,0:T(8,128)(2,1)S(1)}, u32[]{:S(2)}, u32[]{:S(2)}) %all-to-all-start.2) | async-done | bytes 524320 | tf_op jit(solution)/shard_map/all_to_all | solution.py:104
  112.5 38.5 %all_to_all.43 = bf16[32,8,2560]{2,1,0:T(8,128)(2,1)S(1)} all-to-all(bf16[32,8,2560]{2,1,0:T(8,128)(2,1)S(1)} %pad_maximum_fusion.1), channel_id=1, replica_groups=mesh['dp'=32,'feat'=16] {'dp'}, dimensions={0} | all-to-all | bytes 2621440 | tf_op jit(solution)/shard_map/all_to_all | solution.py:171
  151.2 0.7 copy.156
  (70 shorter events, 10.6 us)
Async XLA Ops:
  0.6 1.2 copy-start
  1.8 14.2 %copy-start.14 = (bf16[128,512]{1,0:T(8,128)(2,1)S(1)}, bf16[128,512]{1,0:T(8,128)(2,1)}, u32[]{:S(2)}) copy-start(bf16[128,512]{1,0:T(8,128)(2,1)} %param.10) | copy-start | bytes 393220
  1.9 14.3 %copy-start.11 = (bf16[8,64,256]{2,1,0:T(8,128)(2,1)S(1)}, bf16[8,64,256]{2,1,0:T(8,128)(2,1)}, u32[]{:S(2)}) copy-start(bf16[8,64,256]{2,1,0:T(8,128)(2,1)} %param.15) | copy-start | bytes 786436
  3.0 13.4 %copy-start.12 = (bf16[8,64,256]{2,1,0:T(8,128)(2,1)S(1)}, bf16[8,64,256]{2,1,0:T(8,128)(2,1)}, u32[]{:S(2)}) copy-start(bf16[8,64,256]{2,1,0:T(8,128)(2,1)} %param.12) | copy-start | bytes 786436
  3.8 21.8 %all-to-all-start = ((bf16[32,8,512]{2,1,0:T(8,128)(2,1)}), bf16[32,8,512]{2,1,0:T(8,128)(2,1)S(1)}, u32[]{:S(2)}, u32[]{:S(2)}) async-start(bf16[32,8,512]{2,1,0:T(8,128)(2,1)} %bitcast_select_fusion), calls=%async_computation | async-start | bytes 524288 | tf_op jit(solution)/shard_map/all_to_all | solution.py:138
  16.5 1.0 copy-start.13
  28.7 12.9 %copy-start.2 = (bf16[8,256,256]{2,1,0:T(8,128)(2,1)S(1)}, bf16[8,256,256]{2,1,0:T(8,128)(2,1)}, u32[]{:S(2)}) copy-start(bf16[8,256,256]{2,1,0:T(8,128)(2,1)} %param.13) | copy-start | bytes 3145732
  28.7 51.4 %all-to-all-start.1 = ((bf16[16,3,8,16,128]{4,2,3,1,0:T(8,128)(2,1)}), bf16[16,3,8,16,128]{4,2,3,1,0:T(8,128)(2,1)S(1)}, u32[]{:S(2)}, u32[]{:S(2)}) async-start(bf16[16,3,8,16,128]{4,2,3,1,0:T(8,128)(2,1)} %copy.102), calls=%async_computation.1 | async-start | bytes 3145728 | tf_op jit(solution)/shard_map/all_to_all | solution.py:53
  80.5 1.8 %copy-start.3 = (bf16[8,256,256]{2,1,0:T(8,128)(2,1)S(1)}, bf16[8,256,256]{2,1,0:T(8,128)(2,1)}, u32[]{:S(2)}) copy-start(bf16[8,256,256]{2,1,0:T(8,128)(2,1)} %param.13) | copy-start | bytes 3145732
  84.9 1.2 copy-start.5
  84.9 1.5 %copy-start.6 = (f32[8,128,256]{2,1,0:T(8,128)S(1)}, f32[8,128,256]{2,1,0:T(8,128)}, u32[]{:S(2)}) copy-start(f32[8,128,256]{2,1,0:T(8,128)} %fusion.20) | copy-start | bytes 3145732
  85.8 2.3 %copy-start.8 = (bf16[8,256,128]{1,2,0:T(8,128)(2,1)}, bf16[8,256,128]{1,2,0:T(8,128)(2,1)S(1)}, u32[]{:S(2)}) copy-start(bf16[8,256,128]{1,2,0:T(8,128)(2,1)S(1)} %get-tuple-element.10) | copy-start | bytes 1572868
  86.4 1.2 copy-start.4
  87.6 1.2 copy-start.1
  89.4 5.2 %copy-start.7 = (bf16[8,32,8,128]{3,2,1,0:T(8,128)(2,1)S(1)}, bf16[8,32,8,128]{3,2,1,0:T(8,128)(2,1)}, u32[]{:S(2)}) copy-start(bf16[8,32,8,128]{3,2,1,0:T(8,128)(2,1)} %get-tuple-element.5) | copy-start | bytes 1572868
  89.4 5.2 %copy-start.9 = (bf16[8,256,128]{1,2,0:T(8,128)(2,1)S(1)}, bf16[8,256,128]{1,2,0:T(8,128)(2,1)}, u32[]{:S(2)}) copy-start(bf16[8,256,128]{1,2,0:T(8,128)(2,1)} %copy-done.8) | copy-start | bytes 1572868
  90.4 21.3 %all-to-all-start.2 = ((bf16[16,8,16,128]{3,1,2,0:T(8,128)(2,1)}), bf16[16,8,16,128]{3,1,2,0:T(8,128)(2,1)S(1)}, u32[]{:S(2)}, u32[]{:S(2)}) async-start(bf16[16,8,16,128]{3,1,2,0:T(8,128)(2,1)} %bitcast.40), calls=%async_computation.2 | async-start | bytes 1048576 | tf_op jit(solution)/shard_map/all_to_all | solution.py:104
  94.6 1.0 copy-start.10

commit v3 on v2

--- a/solution.py
+++ b/solution.py
@@ -72,17 +72,14 @@
     preactivation_tangent_gradient = (
         hidden_grad * (density * (2.0 - pre_act * pre_act)) * pre_tan
     ).astype(jnp.bfloat16)
-    loaders = lax.axis_size("dp")
-    mixed_tan_split = mixed_tangent_value.reshape(local_blocks, loaders, -1, row_count)
-    mixed_act_split = mixed_activation.reshape(local_blocks, loaders, -1, row_count)
     hess_mixed = jnp.einsum(
-        "eDvp,eqp->Devq",
-        mixed_tan_split,
+        "evp,eqp->evq",
+        mixed_tangent_value,
         preactivation_gradient,
         preferred_element_type=jnp.float32,
     ) + jnp.einsum(
-        "eDvp,eqp->Devq",
-        mixed_act_split,
+        "evp,eqp->evq",
+        mixed_activation,
         preactivation_tangent_gradient,
         preferred_element_type=jnp.float32,
     )
@@ -165,7 +162,7 @@
     )
     local_blocks = hess_first.shape[0]
     first_part = hess_first.reshape(local_blocks, loaders, -1).transpose(1, 0, 2)
-    mixed_part = hess_mixed.reshape(loaders, local_blocks, -1)
+    mixed_part = hess_mixed.reshape(local_blocks, loaders, -1).transpose(1, 0, 2)
     first_width = first_part.shape[2]
     partials = jnp.concatenate([first_part, mixed_part], axis=2).astype(jnp.bfloat16)
     gathered = lax.all_to_all(partials, "dp", split_axis=0, concat_axis=0, tiled=True)

time: 153 us -> 153 us (level)
    unnamed x36 -> x34, local copies, waits for them, and re-layouts: 6.06 us -> 4.93 us
where the time goes in v3:
time: 153 us
  waiting for transfers between devices  58 us (38%)
  blocking collectives  38.5 us (25%)
  starting transfers between devices  27.5 us (18%)
  local copies, waits for them, and re-layouts  18.2 us (12%)
  matrix products  6.03 us (4%)
  other arithmetic  3.42 us (2%)
    all_to_all x1, blocking collectives, per_device(): lax.all_to_all(partials, 'dp', split_axis=0, concat_axis=0, tiled=True)  38.5 us
    all_to_all x1, waiting for transfers between devices, curvature(): lax.all_to_all(stacked, 'feat', split_axis=0, concat_axis=3, tiled=True)  35.1 us
    all_to_all x1, waiting for transfers between devices, curvature(): lax.all_to_all(back_merged, 'feat', split_axis=0, concat_axis=2, tiled=True)  15.3 us
    all_to_all x1, starting transfers between devices, curvature(): lax.all_to_all(stacked, 'feat', split_axis=0, concat_axis=3, tiled=True)  12.9 us
    all_to_all x1, starting transfers between devices, per_device(): lax.all_to_all(outgoing, 'dp', split_axis=0, concat_axis=0, tiled=True)  10.5 us
    all_to_all x1, waiting for transfers between devices, per_device(): lax.all_to_all(outgoing, 'dp', split_axis=0, concat_axis=0, tiled=True)  7.59 us
    unnamed x34, local copies, waits for them, and re-layouts  4.93 us
    all_to_all x1, starting transfers between devices, curvature(): lax.all_to_all(back_merged, 'feat', split_axis=0, concat_axis=2, tiled=True)  4.14 us
  transfers between devices with their start and end apart: 3, of which 3 were waited for; matrix products, arithmetic and copies ran while one was open for 6% of the time, Pallas kernels for 0%

profile of v3, /device:TPU:1, one launch (start us, length us, event | category | flops | bytes accessed | tf_op | source)
XLA Modules:
  0.0 152.7 jit_solution(6696845973760297946)
XLA Ops:
  0.6 0.9 select_reduce_fusion.1
  1.9 1.2 gather_fusion
  3.0 0.8 bitcast_select_fusion
  3.8 10.5 %all-to-all-start = ((bf16[32,8,512]{2,1,0:T(8,128)(2,1)}), bf16[32,8,512]{2,1,0:T(8,128)(2,1)S(1)}, u32[]{:S(2)}, u32[]{:S(2)}) async-start(bf16[32,8,512]{2,1,0:T(8,128)(2,1)} %bitcast_select_fusion), calls=%async_computation | async-start | bytes 524288 | tf_op jit(solution)/shard_map/all_to_all | solution.py:135
  14.3 0.7 fusion.35
  15.3 0.7 subtract_bitcast_fusion
  18.0 7.6 %all-to-all-done = bf16[32,8,512]{2,1,0:T(8,128)(2,1)S(1)} async-done(((bf16[32,8,512]{2,1,0:T(8,128)(2,1)}), bf16[32,8,512]{2,1,0:T(8,128)(2,1)S(1)}, u32[]{:S(2)}, u32[]{:S(2)}) %all-to-all-start) | async-done | bytes 262176 | tf_op jit(solution)/shard_map/all_to_all | solution.py:135
  25.6 0.8 gather_fusion.1
  27.4 1.3 copy.95
  28.7 12.9 %all-to-all-start.1 = ((bf16[16,3,8,16,128]{4,2,3,1,0:T(8,128)(2,1)}), bf16[16,3,8,16,128]{4,2,3,1,0:T(8,128)(2,1)S(1)}, u32[]{:S(2)}, u32[]{:S(2)}) async-start(bf16[16,3,8,16,128]{4,2,3,1,0:T(8,128)(2,1)} %copy.95), calls=%async_computation.1 | async-start | bytes 3145728 | tf_op jit(solution)/shard_map/all_to_all | solution.py:53
  41.6 1.2 reshape.171
  42.8 2.2 %reshape.172 = bf16[8,16,8,2,256]{4,3,2,1,0:T(2,128)(2,1)} reshape(bf16[8,256,256]{2,1,0:T(8,128)(2,1)} %param.16) | data formatting | bytes 2097152 | tf_op jit(solution)/shard_map/reshape | solution.py:95
  45.1 35.1 %all-to-all-done.1 = bf16[16,3,8,16,128]{4,2,3,1,0:T(8,128)(2,1)S(1)} async-done(((bf16[16,3,8,16,128]{4,2,3,1,0:T(8,128)(2,1)}), bf16[16,3,8,16,128]{4,2,3,1,0:T(8,128)(2,1)S(1)}, u32[]{:S(2)}, u32[]{:S(2)}) %all-to-all-start.1) | async-done | bytes 1572896 | tf_op jit(solution)/shard_map/all_to_all | solution.py:53
  80.5 0.8 slice.24
  81.4 1.3 fusion.25
  82.7 1.2 copy.124
  84.0 0.9 fusion.10
  85.5 0.7 fusion.4
  87.2 0.7 copy-done.1
  88.5 1.0 copy.104
  89.5 4.1 %all-to-all-start.2 = ((bf16[16,8,16,128]{3,1,2,0:T(8,128)(2,1)}), bf16[16,8,16,128]{3,1,2,0:T(8,128)(2,1)}, u32[]{:S(2)}, u32[]{:S(2)}) async-start(bf16[16,8,16,128]{3,1,2,0:T(8,128)(2,1)} %bitcast.40), calls=%async_computation.2 | async-start | bytes 1048576 | tf_op jit(solution)/shard_map/all_to_all | solution.py:101
  95.6 15.3 %all-to-all-done.2 = bf16[16,8,16,128]{3,1,2,0:T(8,128)(2,1)} async-done(((bf16[16,8,16,128]{3,1,2,0:T(8,128)(2,1)}), bf16[16,8,16,128]{3,1,2,0:T(8,128)(2,1)}, u32[]{:S(2)}, u32[]{:S(2)}) %all-to-all-start.2) | async-done | bytes 524320 | tf_op jit(solution)/shard_map/all_to_all | solution.py:101
  111.0 1.1 copy.105
  112.7 38.5 %all_to_all.43 = bf16[32,8,2560]{2,1,0:T(8,128)(2,1)S(1)} all-to-all(bf16[32,8,2560]{2,1,0:T(8,128)(2,1)S(1)} %pad_maximum_fusion.1), channel_id=1, replica_groups=mesh['dp'=32,'feat'=16] {'dp'}, dimensions={0} | all-to-all | bytes 2621440 | tf_op jit(solution)/shard_map/all_to_all | solution.py:168
  (68 shorter events, 10.0 us)
Async XLA Ops:
  0.6 1.2 copy-start
  1.8 14.2 %copy-start.13 = (bf16[128,512]{1,0:T(8,128)(2,1)S(1)}, bf16[128,512]{1,0:T(8,128)(2,1)}, u32[]{:S(2)}) copy-start(bf16[128,512]{1,0:T(8,128)(2,1)} %param.10) | copy-start | bytes 393220
  1.9 14.3 %copy-start.10 = (bf16[8,64,256]{2,1,0:T(8,128)(2,1)S(1)}, bf16[8,64,256]{2,1,0:T(8,128)(2,1)}, u32[]{:S(2)}) copy-start(bf16[8,64,256]{2,1,0:T(8,128)(2,1)} %param.15) | copy-start | bytes 786436
  3.0 13.4 %copy-start.11 = (bf16[8,64,256]{2,1,0:T(8,128)(2,1)S(1)}, bf16[8,64,256]{2,1,0:T(8,128)(2,1)}, u32[]{:S(2)}) copy-start(bf16[8,64,256]{2,1,0:T(8,128)(2,1)} %param.12) | copy-start | bytes 786436
  3.8 21.8 %all-to-all-start = ((bf16[32,8,512]{2,1,0:T(8,128)(2,1)}), bf16[32,8,512]{2,1,0:T(8,128)(2,1)S(1)}, u32[]{:S(2)}, u32[]{:S(2)}) async-start(bf16[32,8,512]{2,1,0:T(8,128)(2,1)} %bitcast_select_fusion), calls=%async_computation | async-start | bytes 524288 | tf_op jit(solution)/shard_map/all_to_all | solution.py:135
  16.5 1.0 copy-start.12
  28.7 12.9 %copy-start.2 = (bf16[8,256,256]{2,1,0:T(8,128)(2,1)S(1)}, bf16[8,256,256]{2,1,0:T(8,128)(2,1)}, u32[]{:S(2)}) copy-start(bf16[8,256,256]{2,1,0:T(8,128)(2,1)} %param.13) | copy-start | bytes 3145732
  28.7 51.4 %all-to-all-start.1 = ((bf16[16,3,8,16,128]{4,2,3,1,0:T(8,128)(2,1)}), bf16[16,3,8,16,128]{4,2,3,1,0:T(8,128)(2,1)S(1)}, u32[]{:S(2)}, u32[]{:S(2)}) async-start(bf16[16,3,8,16,128]{4,2,3,1,0:T(8,128)(2,1)} %copy.95), calls=%async_computation.1 | async-start | bytes 3145728 | tf_op jit(solution)/shard_map/all_to_all | solution.py:53
  80.2 1.2 copy-start.3
  81.4 2.6 %copy-start.4 = (bf16[8,256,256]{2,1,0:T(8,128)(2,1)S(1)}, bf16[8,256,256]{2,1,0:T(8,128)(2,1)}, u32[]{:S(2)}) copy-start(bf16[8,256,256]{2,1,0:T(8,128)(2,1)} %param.13) | copy-start | bytes 3145732
  84.0 1.2 copy-start.6
  84.0 1.5 %copy-start.7 = (f32[8,128,256]{2,1,0:T(8,128)S(1)}, f32[8,128,256]{2,1,0:T(8,128)}, u32[]{:S(2)}) copy-start(f32[8,128,256]{2,1,0:T(8,128)} %fusion.25) | copy-start | bytes 3145732
  84.9 2.3 %copy-start.8 = (bf16[8,256,128]{1,2,0:T(8,128)(2,1)}, bf16[8,256,128]{1,2,0:T(8,128)(2,1)S(1)}, u32[]{:S(2)}) copy-start(bf16[8,256,128]{1,2,0:T(8,128)(2,1)S(1)} %get-tuple-element.7) | copy-start | bytes 1572868
  85.5 1.2 copy-start.5
  86.7 1.2 copy-start.1
  88.5 5.2 %copy-start.9 = (bf16[8,256,128]{1,2,0:T(8,128)(2,1)S(1)}, bf16[8,256,128]{1,2,0:T(8,128)(2,1)}, u32[]{:S(2)}) copy-start(bf16[8,256,128]{1,2,0:T(8,128)(2,1)} %copy-done.8) | copy-start | bytes 1572868
  89.5 21.4 %all-to-all-start.2 = ((bf16[16,8,16,128]{3,1,2,0:T(8,128)(2,1)}), bf16[16,8,16,128]{3,1,2,0:T(8,128)(2,1)}, u32[]{:S(2)}, u32[]{:S(2)}) async-start(bf16[16,8,16,128]{3,1,2,0:T(8,128)(2,1)} %bitcast.40), calls=%async_computation.2 | async-start | bytes 1048576 | tf_op jit(solution)/shard_map/all_to_all | solution.py:101

commit v4 on v3

--- a/solution.py
+++ b/solution.py
@@ -1,10 +1,68 @@
 import jax
 import jax.numpy as jnp
 from jax import lax
+from jax.experimental import pallas as pl
 from jax.sharding import PartitionSpec as P
 
 inv_root_two = 0.7071067811865476
 inv_root_two_pi = 0.3989422804014327
+
+
+def second_factor_kernel(recv_ref, w_t_ref, wt_t_ref, w_ref, wt_ref, back_ref, hess_ref):
+    units = recv_ref.shape[0] * recv_ref.shape[3]
+    rows = recv_ref.shape[4]
+    mixed_activation = recv_ref[:, 0, 0].reshape(units, rows)
+    mixed_tangent_value = recv_ref[:, 1, 0].reshape(units, rows)
+    hidden_grad = recv_ref[:, 2, 0].reshape(units, rows).astype(jnp.float32)
+    w_t = w_t_ref[0]
+    pre_act = jnp.dot(w_t, mixed_activation, preferred_element_type=jnp.float32)
+    pre_tan = jnp.dot(w_t, mixed_tangent_value, preferred_element_type=jnp.float32) + jnp.dot(
+        wt_t_ref[0], mixed_activation, preferred_element_type=jnp.float32
+    )
+    density = jnp.exp(-0.5 * pre_act * pre_act) * inv_root_two_pi
+    normal_cdf = 0.5 * (1.0 + lax.erf(pre_act * inv_root_two))
+    preactivation_gradient = (hidden_grad * (normal_cdf + pre_act * density)).astype(jnp.bfloat16)
+    preactivation_tangent_gradient = (
+        hidden_grad * (density * (2.0 - pre_act * pre_act)) * pre_tan
+    ).astype(jnp.bfloat16)
+    back = jnp.dot(
+        w_ref[0], preactivation_tangent_gradient, preferred_element_type=jnp.float32
+    ) + jnp.dot(wt_ref[0], preactivation_gradient, preferred_element_type=jnp.float32)
+    back_ref[0] = back.astype(jnp.bfloat16)
+    row_contract = (((1,), (1,)), ((), ()))
+    hess = lax.dot_general(
+        mixed_tangent_value, preactivation_gradient, row_contract, preferred_element_type=jnp.float32
+    ) + lax.dot_general(
+        mixed_activation, preactivation_tangent_gradient, row_contract, preferred_element_type=jnp.float32
+    )
+    hess_ref[0] = hess.astype(jnp.bfloat16)
+
+
+def second_factor(received, second_factor_blocks, second_factor_tangent):
+    sources, kinds, local_blocks, pieces, rows = received.shape
+    units = second_factor_blocks.shape[1]
+    out_units = second_factor_blocks.shape[2]
+    recv_spec = pl.BlockSpec((sources, kinds, 1, pieces, rows), lambda g: (0, 0, g, 0, 0))
+    weight_spec = pl.BlockSpec((1, units, out_units), lambda g: (g, 0, 0))
+    return pl.pallas_call(
+        second_factor_kernel,
+        grid=(local_blocks,),
+        in_specs=[recv_spec, weight_spec, weight_spec, weight_spec, weight_spec],
+        out_specs=[
+            pl.BlockSpec((1, units, rows), lambda g: (g, 0, 0)),
+            pl.BlockSpec((1, units, out_units), lambda g: (g, 0, 0)),
+        ],
+        out_shape=[
+            jax.ShapeDtypeStruct((local_blocks, units, rows), jnp.bfloat16),
+            jax.ShapeDtypeStruct((local_blocks, units, out_units), jnp.bfloat16),
+        ],
+    )(
+        received,
+        second_factor_blocks.transpose(0, 2, 1),
+        second_factor_tangent.transpose(0, 2, 1),
+        second_factor_blocks,
+        second_factor_tangent,
+    )
 
 
 def curvature(
@@ -50,53 +108,12 @@
     stacked = jnp.stack(
         [first_act.reshape(merged), tangents.reshape(merged), out_grad.reshape(merged)], axis=1
     )
-    mixed = lax.all_to_all(stacked, "feat", split_axis=0, concat_axis=3, tiled=True)
-    hidden_shape = (local_blocks, block_out, row_count)
-    mixed_activation = mixed[0, 0].reshape(hidden_shape)
-    mixed_tangent_value = mixed[0, 1].reshape(hidden_shape)
-    hidden_grad = mixed[0, 2].reshape(hidden_shape)
-    pre_act = jnp.einsum(
-        "vca,vcf->vfa", mixed_activation, second_factor_blocks, preferred_element_type=jnp.float32
-    )
-    pre_tan = jnp.einsum(
-        "vca,vcf->vfa",
-        mixed_tangent_value,
-        second_factor_blocks,
-        preferred_element_type=jnp.float32,
-    ) + jnp.einsum(
-        "vca,vcf->vfa", mixed_activation, second_factor_tangent, preferred_element_type=jnp.float32
-    )
-    density = jnp.exp(-0.5 * pre_act * pre_act) * inv_root_two_pi
-    normal_cdf = 0.5 * (1.0 + lax.erf(pre_act * inv_root_two))
-    preactivation_gradient = (hidden_grad * (normal_cdf + pre_act * density)).astype(jnp.bfloat16)
-    preactivation_tangent_gradient = (
-        hidden_grad * (density * (2.0 - pre_act * pre_act)) * pre_tan
-    ).astype(jnp.bfloat16)
-    hess_mixed = jnp.einsum(
-        "evp,eqp->evq",
-        mixed_tangent_value,
-        preactivation_gradient,
-        preferred_element_type=jnp.float32,
-    ) + jnp.einsum(
-        "evp,eqp->evq",
-        mixed_activation,
-        preactivation_tangent_gradient,
-        preferred_element_type=jnp.float32,
-    )
-    pos_shape = (local_blocks, features, local_blocks, pair_size, block_out)
-    back_mixed = jnp.einsum(
-        "bip,bFkci->Fkbcp",
-        preactivation_tangent_gradient,
-        second_factor_blocks.reshape(pos_shape),
-        preferred_element_type=jnp.float32,
-    ) + jnp.einsum(
-        "bip,bFkci->Fkbcp",
-        preactivation_gradient,
-        second_factor_tangent.reshape(pos_shape),
-        preferred_element_type=jnp.float32,
-    )
-    back_merged = back_mixed.astype(jnp.bfloat16).reshape(
-        features, local_blocks, local_blocks * pair_size, row_count
+    mixed = lax.all_to_all(stacked, "feat", split_axis=0, concat_axis=0, tiled=True)
+    back_mixed, hess_mixed = second_factor(mixed, second_factor_blocks, second_factor_tangent)
+    back_merged = (
+        back_mixed.reshape(local_blocks, features, local_blocks, pair_size, row_count)
+        .transpose(1, 2, 0, 3, 4)
+        .reshape(features, local_blocks, local_blocks * pair_size, row_count)
     )
     back_first = lax.all_to_all(back_merged, "feat", split_axis=0, concat_axis=2, tiled=True)
     back_first = back_first.reshape(local_blocks, block_out, row_count)

time: 153 us -> 155 us (1.013)
  Pallas kernels: 0 us -> 8.56 us
  matrix products: 6.03 us -> 1.29 us
  local copies, waits for them, and re-layouts: 18.2 us -> 15.1 us
    pallas_call x0 -> x1, Pallas kernels: none -> 8.56 us  [second_factor(): pl.pallas_call(second_factor_kernel, grid=(local_blocks,), in_specs=[recv...]
    dot_general x7 -> x0, matrix products: 4.74 us -> none  [the longest x1 1.33 us: curvature(): jnp.einsum('vca,vcf->vfa', mixed_tangent_value, second_factor_blocks, pre...]
    reshape x6 -> x3, local copies, waits for them, and re-layouts: 5.35 us -> 2.82 us  [the longest x1 2.04 us: curvature(): back_mixed.reshape(local_blocks, features, local_blocks, pair_size, row_c...]
    unnamed x34 -> x23, local copies, waits for them, and re-layouts: 4.93 us -> 6.47 us
where the time goes in v4:
time: 155 us; the launch traced here: 154 us
  waiting for transfers between devices  57.7 us (37%)
  blocking collectives  38.5 us (25%)
  starting transfers between devices  27.5 us (18%)
  local copies, waits for them, and re-layouts  15.1 us (10%)
  Pallas kernels  8.56 us (6%)
  other arithmetic  4.57 us (3%)
    all_to_all x1, blocking collectives, per_device(): lax.all_to_all(partials, 'dp', split_axis=0, concat_axis=0, tiled=True)  38.5 us
    all_to_all x1, waiting for transfers between devices, curvature(): lax.all_to_all(stacked, 'feat', split_axis=0, concat_axis=0, tiled=True)  35 us
    all_to_all x1, waiting for transfers between devices, curvature(): lax.all_to_all(back_merged, 'feat', split_axis=0, concat_axis=2, tiled=True)  16.1 us
    all_to_all x1, starting transfers between devices, curvature(): lax.all_to_all(stacked, 'feat', split_axis=0, concat_axis=0, tiled=True)  12.9 us
    all_to_all x1, starting transfers between devices, per_device(): lax.all_to_all(outgoing, 'dp', split_axis=0, concat_axis=0, tiled=True)  10.5 us
    pallas_call x1, Pallas kernels, second_factor(): pl.pallas_call(second_factor_kernel, grid=(local_blocks,), in_specs=[recv...  8.56 us
    all_to_all x1, waiting for transfers between devices, per_device(): lax.all_to_all(outgoing, 'dp', split_axis=0, concat_axis=0, tiled=True)  6.64 us
    unnamed x23, local copies, waits for them, and re-layouts  6.47 us
  transfers between devices with their start and end apart: 3, of which 3 were waited for; matrix products, arithmetic and copies ran while one was open for 6% of the time, Pallas kernels for 0%

profile of v4, /device:TPU:1, one launch (start us, length us, event | category | flops | bytes accessed | tf_op | source)
XLA Modules:
  0.0 154.1 jit_solution(18141826851105184989)
XLA Ops:
  0.6 0.9 select_reduce_fusion.1
  1.9 1.2 gather_fusion
  3.0 0.8 bitcast_select_fusion
  3.8 10.5 %all-to-all-start = ((bf16[32,8,512]{2,1,0:T(8,128)(2,1)}), bf16[32,8,512]{2,1,0:T(8,128)(2,1)S(1)}, u32[]{:S(2)}, u32[]{:S(2)}) async-start(bf16[32,8,512]{2,1,0:T(8,128)(2,1)} %bitcast_select_fusion), calls=%async_computation | async-start | bytes 524288 | tf_op jit(solution)/shard_map/all_to_all | solution.py:152
  14.3 0.7 fusion.17
  15.3 0.7 subtract_bitcast_fusion
  17.5 0.5 copy.62
  19.0 6.6 %all-to-all-done = bf16[32,8,512]{2,1,0:T(8,128)(2,1)S(1)} async-done(((bf16[32,8,512]{2,1,0:T(8,128)(2,1)}), bf16[32,8,512]{2,1,0:T(8,128)(2,1)S(1)}, u32[]{:S(2)}, u32[]{:S(2)}) %all-to-all-start) | async-done | bytes 262176 | tf_op jit(solution)/shard_map/all_to_all | solution.py:152
  25.6 0.8 gather_fusion.1
  27.6 1.3 pad_maximum_fusion
  28.9 12.9 %all-to-all-start.1 = ((bf16[16,3,8,16,128]{4,3,2,1,0:T(8,128)(2,1)}), bf16[16,3,8,16,128]{4,3,2,1,0:T(8,128)(2,1)S(1)}, u32[]{:S(2)}, u32[]{:S(2)}) async-start(bf16[16,3,8,16,128]{4,3,2,1,0:T(8,128)(2,1)} %pad_maximum_fusion), calls=%async_computation.1 | async-start | bytes 3145728 | tf_op jit(solution)/shard_map/all_to_all | solution.py:111
  41.8 1.3 copy.71
  43.1 2.3 %copy.72 = bf16[8,256,256]{1,2,0:T(8,128)(2,1)} copy(bf16[8,256,256]{2,1,0:T(8,128)(2,1)} %wt_ref.1) | data formatting | bytes 2097152 | tf_op args[6]
  45.4 35.0 %all-to-all-done.1.recv_ref = bf16[16,3,8,16,128]{4,3,2,1,0:T(8,128)(2,1)S(1)} async-done(((bf16[16,3,8,16,128]{4,3,2,1,0:T(8,128)(2,1)}), bf16[16,3,8,16,128]{4,3,2,1,0:T(8,128)(2,1)S(1)}, u32[]{:S(2)}, u32[]{:S(2)}) %all-to-all-start.1) | async-done | bytes 1572896 | tf_op jit(solution)/shard_map/all_to_all | solution.py:111
  80.3 1.2 copy-done.1
  81.5 8.6 %shard_map.113 = (bf16[8,256,128]{2,1,0:T(8,128)(2,1)}, bf16[8,256,256]{2,1,0:T(8,128)(2,1)}) custom-call(bf16[16,3,8,16,128]{4,3,2,1,0:T(8,128)(2,1)} %copy-done.1, bf16[8,256,256]{2,1,0:T(8,128)(2,1)} %bitcast.75, bf16[8,256,256]{2,1,0:T(8,128)(2,1)} %bitcast.76, bf16[8,256,256]{2,1,0:T(8,128)(2,1)} %w_ref.1, bf16[8,256,256]{2,1,0:T(8,128)(2,1)} %wt_ref.1), custom_call_target="tpu_custom_call" | custom-call | tf_op jit(solution)/shard_map/pallas_call | solution.py:47
  90.0 2.0 %copy.73 = bf16[8,16,8,2,128]{4,2,3,0,1:T(8,128)(2,1)} copy(bf16[8,16,8,2,128]{4,3,2,1,0:T(2,128)(2,1)} %bitcast.89) | data formatting | bytes 1048576 | tf_op jit(solution)/shard_map/reshape | solution.py:114
  92.1 4.1 %all-to-all-start.2 = ((bf16[16,8,16,128]{3,1,2,0:T(8,128)(2,1)}), bf16[16,8,16,128]{3,1,2,0:T(8,128)(2,1)S(1)}, u32[]{:S(2)}, u32[]{:S(2)}) async-start(bf16[16,8,16,128]{3,1,2,0:T(8,128)(2,1)} %bitcast.30), calls=%async_computation.2 | async-start | bytes 1048576 | tf_op jit(solution)/shard_map/all_to_all | solution.py:118
  96.2 0.5 convert_element_type.46
  96.7 0.6 copy.89
  97.3 16.1 %all-to-all-done.2 = bf16[16,8,16,128]{3,1,2,0:T(8,128)(2,1)S(1)} async-done(((bf16[16,8,16,128]{3,1,2,0:T(8,128)(2,1)}), bf16[16,8,16,128]{3,1,2,0:T(8,128)(2,1)S(1)}, u32[]{:S(2)}, u32[]{:S(2)}) %all-to-all-start.2) | async-done | bytes 524320 | tf_op jit(solution)/shard_map/all_to_all | solution.py:118
  114.1 38.5 %all_to_all.30 = bf16[32,8,2560]{2,1,0:T(8,128)(2,1)S(1)} all-to-all(bf16[32,8,2560]{2,1,0:T(8,128)(2,1)S(1)} %pad_maximum_fusion.1), channel_id=1, replica_groups=mesh['dp'=32,'feat'=16] {'dp'}, dimensions={0} | all-to-all | bytes 2621440 | tf_op jit(solution)/shard_map/all_to_all | solution.py:185
  152.9 0.7 copy.91
  153.5 0.6 reshape.169
  (46 shorter events, 4.9 us)
Async XLA Ops:
  0.6 1.2 copy-start
  1.9 14.2 %copy-start.7 = (bf16[128,512]{1,0:T(8,128)(2,1)S(1)}, bf16[128,512]{1,0:T(8,128)(2,1)}, u32[]{:S(2)}) copy-start(bf16[128,512]{1,0:T(8,128)(2,1)} %param.10) | copy-start | bytes 393220
  1.9 14.3 %copy-start.4 = (bf16[8,64,256]{2,1,0:T(8,128)(2,1)S(1)}, bf16[8,64,256]{2,1,0:T(8,128)(2,1)}, u32[]{:S(2)}) copy-start(bf16[8,64,256]{2,1,0:T(8,128)(2,1)} %param.12) | copy-start | bytes 786436
  3.0 13.4 %copy-start.5 = (bf16[8,64,256]{2,1,0:T(8,128)(2,1)S(1)}, bf16[8,64,256]{2,1,0:T(8,128)(2,1)}, u32[]{:S(2)}) copy-start(bf16[8,64,256]{2,1,0:T(8,128)(2,1)} %param.15) | copy-start | bytes 786436
  3.8 21.8 %all-to-all-start = ((bf16[32,8,512]{2,1,0:T(8,128)(2,1)}), bf16[32,8,512]{2,1,0:T(8,128)(2,1)S(1)}, u32[]{:S(2)}, u32[]{:S(2)}) async-start(bf16[32,8,512]{2,1,0:T(8,128)(2,1)} %bitcast_select_fusion), calls=%async_computation | async-start | bytes 524288 | tf_op jit(solution)/shard_map/all_to_all | solution.py:152
  16.8 1.2 copy-start.6
  28.9 12.9 %copy-start.2 = (bf16[8,256,256]{2,1,0:T(8,128)(2,1)S(1)}, bf16[8,256,256]{2,1,0:T(8,128)(2,1)}, u32[]{:S(2)}) copy-start(bf16[8,256,256]{2,1,0:T(8,128)(2,1)} %w_ref.1) | copy-start | bytes 3145732
  28.9 51.4 %all-to-all-start.1 = ((bf16[16,3,8,16,128]{4,3,2,1,0:T(8,128)(2,1)}), bf16[16,3,8,16,128]{4,3,2,1,0:T(8,128)(2,1)S(1)}, u32[]{:S(2)}, u32[]{:S(2)}) async-start(bf16[16,3,8,16,128]{4,3,2,1,0:T(8,128)(2,1)} %pad_maximum_fusion), calls=%async_computation.1 | async-start | bytes 3145728 | tf_op jit(solution)/shard_map/all_to_all | solution.py:111
  80.3 1.2 copy-start.1
  90.0 6.2 %copy-start.3 = (bf16[8,256,256]{2,1,0:T(8,128)(2,1)S(1)}, bf16[8,256,256]{2,1,0:T(8,128)(2,1)}, u32[]{:S(2)}) copy-start(bf16[8,256,256]{2,1,0:T(8,128)(2,1)} %get-tuple-element.5) | copy-start | bytes 3145732
  92.1 21.3 %all-to-all-start.2 = ((bf16[16,8,16,128]{3,1,2,0:T(8,128)(2,1)}), bf16[16,8,16,128]{3,1,2,0:T(8,128)(2,1)S(1)}, u32[]{:S(2)}, u32[]{:S(2)}) async-start(bf16[16,8,16,128]{3,1,2,0:T(8,128)(2,1)} %bitcast.30), calls=%async_computation.2 | async-start | bytes 1048576 | tf_op jit(solution)/shard_map/all_to_all | solution.py:118

commit v5 on v3

--- a/solution.py
+++ b/solution.py
@@ -129,7 +129,7 @@
     doc_span = jnp.sum(mine * doc_lengths, axis=1)
     in_slot = position[None, :] < doc_span[:, None]
     source = jnp.where(in_slot, first_row[:, None] + position[None, :], 0)
-    outgoing = jnp.take(targets, source.reshape(-1), axis=0).reshape(
+    outgoing = targets.at[source.reshape(-1)].get(mode="promise_in_bounds").reshape(
         loaders, slot_rows, feature_cols
     )
     arrived = lax.all_to_all(outgoing, "dp", split_axis=0, concat_axis=0, tiled=True)
@@ -147,8 +147,10 @@
     weight = jnp.sum(
         inside.astype(jnp.float32) / my_lengths.astype(jnp.float32)[None, :], axis=1
     )
-    goal_rows = jnp.take(
-        arrived.reshape(loaders * slot_rows, feature_cols), goal_index, axis=0
+    goal_rows = (
+        arrived.reshape(loaders * slot_rows, feature_cols)
+        .at[goal_index]
+        .get(mode="promise_in_bounds")
     )
     hess_first, hess_mixed = curvature(
         tokens,

time: 153 us -> 153 us (level)
  no operation moved by 1% of the time
where the time goes in v5:
time: 153 us
  waiting for transfers between devices  58 us (38%)
  blocking collectives  38.5 us (25%)
  starting transfers between devices  27.5 us (18%)
  local copies, waits for them, and re-layouts  18.9 us (12%)
  matrix products  6.01 us (4%)
  other arithmetic  2.53 us (2%)
    all_to_all x1, blocking collectives, per_device(): lax.all_to_all(partials, 'dp', split_axis=0, concat_axis=0, tiled=True)  38.5 us
    all_to_all x1, waiting for transfers between devices, curvature(): lax.all_to_all(stacked, 'feat', split_axis=0, concat_axis=3, tiled=True)  35.1 us
    all_to_all x1, waiting for transfers between devices, curvature(): lax.all_to_all(back_merged, 'feat', split_axis=0, concat_axis=2, tiled=True)  15.3 us
    all_to_all x1, starting transfers between devices, curvature(): lax.all_to_all(stacked, 'feat', split_axis=0, concat_axis=3, tiled=True)  12.9 us
    all_to_all x1, starting transfers between devices, per_device(): lax.all_to_all(outgoing, 'dp', split_axis=0, concat_axis=0, tiled=True)  10.5 us
    all_to_all x1, waiting for transfers between devices, per_device(): lax.all_to_all(outgoing, 'dp', split_axis=0, concat_axis=0, tiled=True)  7.6 us
    unnamed x34, local copies, waits for them, and re-layouts  4.94 us
    all_to_all x1, starting transfers between devices, curvature(): lax.all_to_all(back_merged, 'feat', split_axis=0, concat_axis=2, tiled=True)  4.14 us
  transfers between devices with their start and end apart: 3, of which 3 were waited for; matrix products, arithmetic and copies ran while one was open for 6% of the time, Pallas kernels for 0%

profile of v5, /device:TPU:1, one launch (start us, length us, event | category | flops | bytes accessed | tf_op | source)
XLA Modules:
  0.0 152.5 jit_solution(13853685546849559228)
XLA Ops:
  0.7 0.9 select_reduce_fusion.2
  1.8 1.8 %gather_fusion = bf16[256,512]{1,0:T(8,128)(2,1)} fusion(bf16[256,512]{1,0:T(8,128)(2,1)S(1)} %copy-done, s32[1024]{0:T(1024)S(1)} %pad_clamp_fusion.1), kind=kCustom, calls=%fused_computation | custom fusion | bytes 525312 | tf_op jit(solution)/shard_map/gather | solution.py:132
  3.6 10.5 %all-to-all-start = ((bf16[32,8,512]{2,1,0:T(8,128)(2,1)}), bf16[32,8,512]{2,1,0:T(8,128)(2,1)S(1)}, u32[]{:S(2)}, u32[]{:S(2)}) async-start(bf16[32,8,512]{2,1,0:T(8,128)(2,1)} %bitcast.12), calls=%async_computation | async-start | bytes 524288 | tf_op jit(solution)/shard_map/all_to_all | solution.py:135
  14.1 0.7 fusion.30
  15.1 0.7 fusion.29
  17.8 7.6 %all-to-all-done = bf16[32,8,512]{2,1,0:T(8,128)(2,1)S(1)} async-done(((bf16[32,8,512]{2,1,0:T(8,128)(2,1)}), bf16[32,8,512]{2,1,0:T(8,128)(2,1)S(1)}, u32[]{:S(2)}, u32[]{:S(2)}) %all-to-all-start) | async-done | bytes 262176 | tf_op jit(solution)/shard_map/all_to_all | solution.py:135
  25.4 0.8 gather_fusion.1
  27.2 1.3 copy.95
  28.5 12.9 %all-to-all-start.1 = ((bf16[16,3,8,16,128]{4,2,3,1,0:T(8,128)(2,1)}), bf16[16,3,8,16,128]{4,2,3,1,0:T(8,128)(2,1)S(1)}, u32[]{:S(2)}, u32[]{:S(2)}) async-start(bf16[16,3,8,16,128]{4,2,3,1,0:T(8,128)(2,1)} %copy.95), calls=%async_computation.1 | async-start | bytes 3145728 | tf_op jit(solution)/shard_map/all_to_all | solution.py:53
  41.4 1.2 reshape.149
  42.7 2.2 %reshape.150 = bf16[8,16,8,2,256]{4,3,2,1,0:T(2,128)(2,1)} reshape(bf16[8,256,256]{2,1,0:T(8,128)(2,1)} %param.16) | data formatting | bytes 2097152 | tf_op jit(solution)/shard_map/reshape | solution.py:95
  44.9 35.1 %all-to-all-done.1 = bf16[16,3,8,16,128]{4,2,3,1,0:T(8,128)(2,1)S(1)} async-done(((bf16[16,3,8,16,128]{4,2,3,1,0:T(8,128)(2,1)}), bf16[16,3,8,16,128]{4,2,3,1,0:T(8,128)(2,1)S(1)}, u32[]{:S(2)}, u32[]{:S(2)}) %all-to-all-start.1) | async-done | bytes 1572896 | tf_op jit(solution)/shard_map/all_to_all | solution.py:53
  80.3 0.8 slice.24
  81.2 1.3 fusion.25
  82.5 1.2 copy.124
  83.8 0.9 fusion.10
  85.3 0.7 fusion.4
  87.0 0.7 copy-done.1
  88.3 1.0 copy.104
  89.3 4.1 %all-to-all-start.2 = ((bf16[16,8,16,128]{3,1,2,0:T(8,128)(2,1)}), bf16[16,8,16,128]{3,1,2,0:T(8,128)(2,1)}, u32[]{:S(2)}, u32[]{:S(2)}) async-start(bf16[16,8,16,128]{3,1,2,0:T(8,128)(2,1)} %bitcast.40), calls=%async_computation.2 | async-start | bytes 1048576 | tf_op jit(solution)/shard_map/all_to_all | solution.py:101
  95.5 15.3 %all-to-all-done.2 = bf16[16,8,16,128]{3,1,2,0:T(8,128)(2,1)} async-done(((bf16[16,8,16,128]{3,1,2,0:T(8,128)(2,1)}), bf16[16,8,16,128]{3,1,2,0:T(8,128)(2,1)}, u32[]{:S(2)}, u32[]{:S(2)}) %all-to-all-start.2) | async-done | bytes 524320 | tf_op jit(solution)/shard_map/all_to_all | solution.py:101
  110.8 1.1 copy.105
  112.5 38.5 %all_to_all.43 = bf16[32,8,2560]{2,1,0:T(8,128)(2,1)S(1)} all-to-all(bf16[32,8,2560]{2,1,0:T(8,128)(2,1)S(1)} %pad_maximum_fusion.1), channel_id=1, replica_groups=mesh['dp'=32,'feat'=16] {'dp'}, dimensions={0} | all-to-all | bytes 2621440 | tf_op jit(solution)/shard_map/all_to_all | solution.py:170
  151.3 0.7 copy.143
  (65 shorter events, 9.3 us)
Async XLA Ops:
  0.6 1.1 copy-start
  0.6 15.2 %copy-start.13 = (bf16[128,512]{1,0:T(8,128)(2,1)S(1)}, bf16[128,512]{1,0:T(8,128)(2,1)}, u32[]{:S(2)}) copy-start(bf16[128,512]{1,0:T(8,128)(2,1)} %param.10) | copy-start | bytes 393220
  1.8 14.2 %copy-start.10 = (bf16[8,64,256]{2,1,0:T(8,128)(2,1)S(1)}, bf16[8,64,256]{2,1,0:T(8,128)(2,1)}, u32[]{:S(2)}) copy-start(bf16[8,64,256]{2,1,0:T(8,128)(2,1)} %param.15) | copy-start | bytes 786436
  1.8 14.5 %copy-start.11 = (bf16[8,64,256]{2,1,0:T(8,128)(2,1)S(1)}, bf16[8,64,256]{2,1,0:T(8,128)(2,1)}, u32[]{:S(2)}) copy-start(bf16[8,64,256]{2,1,0:T(8,128)(2,1)} %param.12) | copy-start | bytes 786436
  3.6 21.8 %all-to-all-start = ((bf16[32,8,512]{2,1,0:T(8,128)(2,1)}), bf16[32,8,512]{2,1,0:T(8,128)(2,1)S(1)}, u32[]{:S(2)}, u32[]{:S(2)}) async-start(bf16[32,8,512]{2,1,0:T(8,128)(2,1)} %bitcast.12), calls=%async_computation | async-start | bytes 524288 | tf_op jit(solution)/shard_map/all_to_all | solution.py:135
  16.3 1.0 copy-start.12
  28.5 12.9 %copy-start.2 = (bf16[8,256,256]{2,1,0:T(8,128)(2,1)S(1)}, bf16[8,256,256]{2,1,0:T(8,128)(2,1)}, u32[]{:S(2)}) copy-start(bf16[8,256,256]{2,1,0:T(8,128)(2,1)} %param.13) | copy-start | bytes 3145732
  28.5 51.4 %all-to-all-start.1 = ((bf16[16,3,8,16,128]{4,2,3,1,0:T(8,128)(2,1)}), bf16[16,3,8,16,128]{4,2,3,1,0:T(8,128)(2,1)S(1)}, u32[]{:S(2)}, u32[]{:S(2)}) async-start(bf16[16,3,8,16,128]{4,2,3,1,0:T(8,128)(2,1)} %copy.95), calls=%async_computation.1 | async-start | bytes 3145728 | tf_op jit(solution)/shard_map/all_to_all | solution.py:53
  80.0 1.2 copy-start.3
  81.2 2.6 %copy-start.4 = (bf16[8,256,256]{2,1,0:T(8,128)(2,1)S(1)}, bf16[8,256,256]{2,1,0:T(8,128)(2,1)}, u32[]{:S(2)}) copy-start(bf16[8,256,256]{2,1,0:T(8,128)(2,1)} %param.13) | copy-start | bytes 3145732
  83.8 1.2 copy-start.6
  83.8 1.5 %copy-start.7 = (f32[8,128,256]{2,1,0:T(8,128)S(1)}, f32[8,128,256]{2,1,0:T(8,128)}, u32[]{:S(2)}) copy-start(f32[8,128,256]{2,1,0:T(8,128)} %fusion.25) | copy-start | bytes 3145732
  84.7 2.3 %copy-start.8 = (bf16[8,256,128]{1,2,0:T(8,128)(2,1)}, bf16[8,256,128]{1,2,0:T(8,128)(2,1)S(1)}, u32[]{:S(2)}) copy-start(bf16[8,256,128]{1,2,0:T(8,128)(2,1)S(1)} %get-tuple-element.7) | copy-start | bytes 1572868
  85.3 1.2 copy-start.5
  86.5 1.2 copy-start.1
  88.3 5.2 %copy-start.9 = (bf16[8,256,128]{1,2,0:T(8,128)(2,1)S(1)}, bf16[8,256,128]{1,2,0:T(8,128)(2,1)}, u32[]{:S(2)}) copy-start(bf16[8,256,128]{1,2,0:T(8,128)(2,1)} %copy-done.8) | copy-start | bytes 1572868
  89.3 21.4 %all-to-all-start.2 = ((bf16[16,8,16,128]{3,1,2,0:T(8,128)(2,1)}), bf16[16,8,16,128]{3,1,2,0:T(8,128)(2,1)}, u32[]{:S(2)}, u32[]{:S(2)}) async-start(bf16[16,8,16,128]{3,1,2,0:T(8,128)(2,1)} %bitcast.40), calls=%async_computation.2 | async-start | bytes 1048576 | tf_op jit(solution)/shard_map/all_to_all | solution.py:101

commit v6 on v3

--- a/solution.py
+++ b/solution.py
@@ -1,7 +1,10 @@
 import jax
 import jax.numpy as jnp
 from jax import lax
-from jax.sharding import PartitionSpec as P
+from jax.sharding import Mesh, PartitionSpec as P
+
+DP = ("y", "x")
+FE = ("z", "core")
 
 inv_root_two = 0.7071067811865476
 inv_root_two_pi = 0.3989422804014327
@@ -17,7 +20,7 @@
     first_tangent,
     second_factor_tangent,
 ):
-    features = lax.axis_size("feat")
+    features = lax.axis_size(FE)
     row_count = tok_rows.shape[0]
     local_blocks, block_in, block_out = first_blocks.shape
     pair_size = block_out // (local_blocks * features)
@@ -50,7 +53,7 @@
     stacked = jnp.stack(
         [first_act.reshape(merged), tangents.reshape(merged), out_grad.reshape(merged)], axis=1
     )
-    mixed = lax.all_to_all(stacked, "feat", split_axis=0, concat_axis=3, tiled=True)
+    mixed = lax.all_to_all(stacked, FE, split_axis=0, concat_axis=3, tiled=True)
     hidden_shape = (local_blocks, block_out, row_count)
     mixed_activation = mixed[0, 0].reshape(hidden_shape)
     mixed_tangent_value = mixed[0, 1].reshape(hidden_shape)
@@ -98,7 +101,7 @@
     back_merged = back_mixed.astype(jnp.bfloat16).reshape(
         features, local_blocks, local_blocks * pair_size, row_count
     )
-    back_first = lax.all_to_all(back_merged, "feat", split_axis=0, concat_axis=2, tiled=True)
+    back_first = lax.all_to_all(back_merged, FE, split_axis=0, concat_axis=2, tiled=True)
     back_first = back_first.reshape(local_blocks, block_out, row_count)
     hess_first = jnp.einsum(
         "rki,kjr->kij", token_blocks, back_first, preferred_element_type=jnp.float32
@@ -118,8 +121,8 @@
     doc_owners,
     pack_offsets,
 ):
-    loaders = lax.axis_size("dp")
-    device = lax.axis_index("dp")
+    loaders = lax.axis_size(DP)
+    device = lax.axis_index(DP)
     tok_count = tokens.shape[0]
     feature_cols = tokens.shape[1]
     slot_rows = 2 * tok_count // loaders
@@ -132,7 +135,7 @@
     outgoing = jnp.take(targets, source.reshape(-1), axis=0).reshape(
         loaders, slot_rows, feature_cols
     )
-    arrived = lax.all_to_all(outgoing, "dp", split_axis=0, concat_axis=0, tiled=True)
+    arrived = lax.all_to_all(outgoing, DP, split_axis=0, concat_axis=0, tiled=True)
     my_lengths = lax.dynamic_index_in_dim(doc_lengths, device, 0, keepdims=False)
     my_owners = lax.dynamic_index_in_dim(doc_owners, device, 0, keepdims=False)
     my_starts = jnp.cumsum(my_lengths) - my_lengths
@@ -165,27 +168,37 @@
     mixed_part = hess_mixed.reshape(local_blocks, loaders, -1).transpose(1, 0, 2)
     first_width = first_part.shape[2]
     partials = jnp.concatenate([first_part, mixed_part], axis=2).astype(jnp.bfloat16)
-    gathered = lax.all_to_all(partials, "dp", split_axis=0, concat_axis=0, tiled=True)
-    total = jnp.sum(gathered.astype(jnp.float32), axis=0)
+    x_size = lax.axis_size("x")
+    partials = partials.reshape(loaders // x_size, x_size, *partials.shape[1:])
+    across_x = lax.all_to_all(partials, "x", split_axis=1, concat_axis=1, tiled=True)
+    row_sums = jnp.sum(across_x.astype(jnp.float32), axis=1).astype(jnp.bfloat16)
+    across_y = lax.all_to_all(row_sums, "y", split_axis=0, concat_axis=0, tiled=True)
+    total = jnp.sum(across_y.astype(jnp.float32), axis=0)
     hess_first = total[:, :first_width].reshape(local_blocks, -1, first_blocks.shape[2])
     hess_mixed = total[:, first_width:].reshape(local_blocks, -1, second_factor_blocks.shape[2])
     return (hess_first, hess_mixed)
 
 
 def solution(mesh):
+    dp_size, feat_size = mesh.shape["dp"], mesh.shape["feat"]
+    x_size = 4
+    view = Mesh(
+        mesh.devices.reshape(dp_size // x_size, x_size, feat_size // 2, 2),
+        ("y", "x", "z", "core"),
+    )
     in_specs = (
-        P("dp", "feat"),
-        P("dp", "feat"),
-        P("feat", None, None),
-        P("feat", None, None),
-        P("feat", None, None),
-        P("feat", None, None),
-        P("feat", None, None),
+        P(DP, FE),
+        P(DP, FE),
+        P(FE, None, None),
+        P(FE, None, None),
+        P(FE, None, None),
+        P(FE, None, None),
+        P(FE, None, None),
         P(),
         P(),
         P(),
     )
-    out_specs = (P("feat", "dp", None), P("feat", "dp", None))
+    out_specs = (P(FE, DP, None), P(FE, DP, None))
     return jax.shard_map(
-        per_device, mesh=mesh, in_specs=in_specs, out_specs=out_specs, check_vma=False
-    )
+        per_device, mesh=view, in_specs=in_specs, out_specs=out_specs, check_vma=False
+    )

time: 153 us -> 152 us (level)
  blocking collectives: 38.5 us -> 36.4 us
    all_to_all x1 -> x2, blocking collectives: 38.5 us -> 36.4 us  [the longest x1 20.2 us: per_device(): lax.all_to_all(partials, 'x', split_axis=1, concat_axis=1, tiled=True)]
where the time goes in v6:
time: 152 us
  waiting for transfers between devices  58 us (38%)
  blocking collectives  36.4 us (24%)
  starting transfers between devices  27.5 us (18%)
  local copies, waits for them, and re-layouts  19 us (12%)
  matrix products  6.05 us (4%)
  other arithmetic  3.52 us (2%)
    all_to_all x1, waiting for transfers between devices, curvature(): mixed = lax.all_to_all(stacked, FE, split_axis=0, concat_axis=3, tiled=True)  35.1 us
    all_to_all x1, blocking collectives, per_device(): lax.all_to_all(partials, 'x', split_axis=1, concat_axis=1, tiled=True)  20.2 us
    all_to_all x1, blocking collectives, per_device(): lax.all_to_all(row_sums, 'y', split_axis=0, concat_axis=0, tiled=True)  16.1 us
    all_to_all x1, waiting for transfers between devices, curvature(): lax.all_to_all(back_merged, FE, split_axis=0, concat_axis=2, tiled=True)  15.3 us
    all_to_all x1, starting transfers between devices, curvature(): mixed = lax.all_to_all(stacked, FE, split_axis=0, concat_axis=3, tiled=True)  12.9 us
    all_to_all x1, starting transfers between devices, per_device(): lax.all_to_all(outgoing, DP, split_axis=0, concat_axis=0, tiled=True)  10.5 us
    all_to_all x1, waiting for transfers between devices, per_device(): lax.all_to_all(outgoing, DP, split_axis=0, concat_axis=0, tiled=True)  7.59 us
    unnamed x34, local copies, waits for them, and re-layouts  4.92 us
  transfers between devices with their start and end apart: 3, of which 3 were waited for; matrix products, arithmetic and copies ran while one was open for 6% of the time, Pallas kernels for 0%

profile of v6, /device:TPU:1, one launch (start us, length us, event | category | flops | bytes accessed | tf_op | source)
XLA Modules:
  0.0 151.5 jit_solution(3483442435683392946)
XLA Ops:
  0.7 0.9 select_reduce_fusion.1
  1.9 1.2 gather_fusion
  3.0 0.8 bitcast_select_fusion
  3.8 10.5 %all-to-all-start = ((bf16[32,8,512]{2,1,0:T(8,128)(2,1)}), bf16[32,8,512]{2,1,0:T(8,128)(2,1)S(1)}, u32[]{:S(2)}, u32[]{:S(2)}) async-start(bf16[32,8,512]{2,1,0:T(8,128)(2,1)} %bitcast_select_fusion), calls=%async_computation | async-start | bytes 524288 | tf_op jit(solution)/shard_map/all_to_all | solution.py:138
  15.3 0.7 subtract_bitcast_fusion
  18.1 7.6 %all-to-all-done = bf16[32,8,512]{2,1,0:T(8,128)(2,1)S(1)} async-done(((bf16[32,8,512]{2,1,0:T(8,128)(2,1)}), bf16[32,8,512]{2,1,0:T(8,128)(2,1)S(1)}, u32[]{:S(2)}, u32[]{:S(2)}) %all-to-all-start) | async-done | bytes 262176 | tf_op jit(solution)/shard_map/all_to_all | solution.py:138
  25.6 0.8 gather_fusion.1
  27.4 1.3 copy.157
  28.7 12.9 %all-to-all-start.1 = ((bf16[16,3,8,16,128]{4,2,3,1,0:T(8,128)(2,1)}), bf16[16,3,8,16,128]{4,2,3,1,0:T(8,128)(2,1)S(1)}, u32[]{:S(2)}, u32[]{:S(2)}) async-start(bf16[16,3,8,16,128]{4,2,3,1,0:T(8,128)(2,1)} %copy.157), calls=%async_computation.1 | async-start | bytes 3145728 | tf_op jit(solution)/shard_map/all_to_all | solution.py:56
  41.6 1.2 reshape.176
  42.8 2.2 %reshape.177 = bf16[8,16,8,2,256]{4,3,2,1,0:T(2,128)(2,1)} reshape(bf16[8,256,256]{2,1,0:T(8,128)(2,1)} %param.16) | data formatting | bytes 2097152 | tf_op jit(solution)/shard_map/reshape | solution.py:98
  45.1 35.1 %all-to-all-done.1 = bf16[16,3,8,16,128]{4,2,3,1,0:T(8,128)(2,1)S(1)} async-done(((bf16[16,3,8,16,128]{4,2,3,1,0:T(8,128)(2,1)}), bf16[16,3,8,16,128]{4,2,3,1,0:T(8,128)(2,1)S(1)}, u32[]{:S(2)}, u32[]{:S(2)}) %all-to-all-start.1) | async-done | bytes 1572896 | tf_op jit(solution)/shard_map/all_to_all | solution.py:56
  80.5 0.9 slice.24
  81.4 1.3 fusion.25
  82.7 1.2 copy.190
  84.0 0.9 fusion.10
  87.3 0.7 copy-done.1
  88.5 1.0 copy.166
  89.5 4.1 %all-to-all-start.2 = ((bf16[16,8,16,128]{3,1,2,0:T(8,128)(2,1)}), bf16[16,8,16,128]{3,1,2,0:T(8,128)(2,1)}, u32[]{:S(2)}, u32[]{:S(2)}) async-start(bf16[16,8,16,128]{3,1,2,0:T(8,128)(2,1)} %bitcast.40), calls=%async_computation.2 | async-start | bytes 1048576 | tf_op jit(solution)/shard_map/all_to_all | solution.py:104
  95.7 15.3 %all-to-all-done.2 = bf16[16,8,16,128]{3,1,2,0:T(8,128)(2,1)} async-done(((bf16[16,8,16,128]{3,1,2,0:T(8,128)(2,1)}), bf16[16,8,16,128]{3,1,2,0:T(8,128)(2,1)}, u32[]{:S(2)}, u32[]{:S(2)}) %all-to-all-start.2) | async-done | bytes 524320 | tf_op jit(solution)/shard_map/all_to_all | solution.py:104
  111.0 1.1 copy.167
  112.8 0.7 copy.174
  113.5 20.2 %all_to_all.48 = bf16[8,4,8,2560]{3,0,2,1:T(8,128)(2,1)S(1)} all-to-all(bf16[8,4,8,2560]{3,0,2,1:T(8,128)(2,1)S(1)} %copy.174), channel_id=1, replica_groups=mesh['y'=8,'x'=4,'z'=8,'core'=2] {'x'}, dimensions={1} | all-to-all | bytes 2621440 | tf_op jit(solution)/shard_map/all_to_all | solution.py:173
  134.1 16.1 %all_to_all.49 = bf16[8,8,2560]{2,1,0:T(8,128)(2,1)S(1)} all-to-all(bf16[8,8,2560]{2,1,0:T(8,128)(2,1)S(1)} %copy.176), channel_id=1, replica_groups=mesh['y'=8,'x'=4,'z'=8,'core'=2] {'y'}, dimensions={0} | all-to-all | bytes 655360 | tf_op jit(solution)/shard_map/all_to_all | solution.py:175
  (72 shorter events, 11.6 us)
Async XLA Ops:
  0.6 1.2 copy-start
  1.9 14.2 %copy-start.13 = (bf16[128,512]{1,0:T(8,128)(2,1)S(1)}, bf16[128,512]{1,0:T(8,128)(2,1)}, u32[]{:S(2)}) copy-start(bf16[128,512]{1,0:T(8,128)(2,1)} %param.10) | copy-start | bytes 393220
  1.9 14.3 %copy-start.10 = (bf16[8,64,256]{2,1,0:T(8,128)(2,1)S(1)}, bf16[8,64,256]{2,1,0:T(8,128)(2,1)}, u32[]{:S(2)}) copy-start(bf16[8,64,256]{2,1,0:T(8,128)(2,1)} %param.15) | copy-start | bytes 786436
  3.0 13.4 %copy-start.11 = (bf16[8,64,256]{2,1,0:T(8,128)(2,1)S(1)}, bf16[8,64,256]{2,1,0:T(8,128)(2,1)}, u32[]{:S(2)}) copy-start(bf16[8,64,256]{2,1,0:T(8,128)(2,1)} %param.12) | copy-start | bytes 786436
  3.8 21.8 %all-to-all-start = ((bf16[32,8,512]{2,1,0:T(8,128)(2,1)}), bf16[32,8,512]{2,1,0:T(8,128)(2,1)S(1)}, u32[]{:S(2)}, u32[]{:S(2)}) async-start(bf16[32,8,512]{2,1,0:T(8,128)(2,1)} %bitcast_select_fusion), calls=%async_computation | async-start | bytes 524288 | tf_op jit(solution)/shard_map/all_to_all | solution.py:138
  16.5 1.0 copy-start.12
  28.7 12.9 %copy-start.2 = (bf16[8,256,256]{2,1,0:T(8,128)(2,1)S(1)}, bf16[8,256,256]{2,1,0:T(8,128)(2,1)}, u32[]{:S(2)}) copy-start(bf16[8,256,256]{2,1,0:T(8,128)(2,1)} %param.13) | copy-start | bytes 3145732
  28.7 51.4 %all-to-all-start.1 = ((bf16[16,3,8,16,128]{4,2,3,1,0:T(8,128)(2,1)}), bf16[16,3,8,16,128]{4,2,3,1,0:T(8,128)(2,1)S(1)}, u32[]{:S(2)}, u32[]{:S(2)}) async-start(bf16[16,3,8,16,128]{4,2,3,1,0:T(8,128)(2,1)} %copy.157), calls=%async_computation.1 | async-start | bytes 3145728 | tf_op jit(solution)/shard_map/all_to_all | solution.py:56
  80.1 1.2 copy-start.3
  81.4 2.6 %copy-start.4 = (bf16[8,256,256]{2,1,0:T(8,128)(2,1)S(1)}, bf16[8,256,256]{2,1,0:T(8,128)(2,1)}, u32[]{:S(2)}) copy-start(bf16[8,256,256]{2,1,0:T(8,128)(2,1)} %param.13) | copy-start | bytes 3145732
  84.0 1.2 copy-start.6
  84.0 1.5 %copy-start.7 = (f32[8,128,256]{2,1,0:T(8,128)S(1)}, f32[8,128,256]{2,1,0:T(8,128)}, u32[]{:S(2)}) copy-start(f32[8,128,256]{2,1,0:T(8,128)} %fusion.25) | copy-start | bytes 3145732
  84.9 2.3 %copy-start.8 = (bf16[8,256,128]{1,2,0:T(8,128)(2,1)}, bf16[8,256,128]{1,2,0:T(8,128)(2,1)S(1)}, u32[]{:S(2)}) copy-start(bf16[8,256,128]{1,2,0:T(8,128)(2,1)S(1)} %get-tuple-element.7) | copy-start | bytes 1572868
  85.5 1.2 copy-start.5
  86.7 1.2 copy-start.1
  88.5 5.2 %copy-start.9 = (bf16[8,256,128]{1,2,0:T(8,128)(2,1)S(1)}, bf16[8,256,128]{1,2,0:T(8,128)(2,1)}, u32[]{:S(2)}) copy-start(bf16[8,256,128]{1,2,0:T(8,128)(2,1)} %copy-done.8) | copy-start | bytes 1572868
  89.5 21.4 %all-to-all-start.2 = ((bf16[16,8,16,128]{3,1,2,0:T(8,128)(2,1)}), bf16[16,8,16,128]{3,1,2,0:T(8,128)(2,1)}, u32[]{:S(2)}, u32[]{:S(2)}) async-start(bf16[16,8,16,128]{3,1,2,0:T(8,128)(2,1)} %bitcast.40), calls=%async_computation.2 | async-start | bytes 1048576 | tf_op jit(solution)/shard_map/all_to_all | solution.py:104

commit v7 on v6

--- a/solution.py
+++ b/solution.py
@@ -25,7 +25,7 @@
     local_blocks, block_in, block_out = first_blocks.shape
     pair_size = block_out // (local_blocks * features)
     token_blocks = tok_rows.reshape(row_count, local_blocks, block_in)
-    goal_blocks = goal_rows.reshape(row_count, local_blocks, block_in)
+    goal_blocks = goal_rows.reshape(local_blocks, block_in, row_count)
     split_shape = (local_blocks, block_in, features, local_blocks, pair_size)
     down_shape = (local_blocks, features, local_blocks, pair_size, block_in)
     first_act = jnp.einsum(
@@ -42,7 +42,7 @@
     ).astype(jnp.bfloat16)
     out_grad = (
         jnp.einsum(
-            "rkd,kGgcd->Ggkcr",
+            "kdr,kGgcd->Ggkcr",
             goal_blocks,
             down_blocks.reshape(down_shape),
             preferred_element_type=jnp.float32,
@@ -150,12 +150,18 @@
     weight = jnp.sum(
         inside.astype(jnp.float32) / my_lengths.astype(jnp.float32)[None, :], axis=1
     )
-    goal_rows = jnp.take(
-        arrived.reshape(loaders * slot_rows, feature_cols), goal_index, axis=0
-    )
+    picks = (
+        jnp.arange(loaders * slot_rows, dtype=jnp.int32)[:, None] == goal_index[None, :]
+    ).astype(jnp.bfloat16)
+    goal_cols = lax.dot_general(
+        arrived.reshape(loaders * slot_rows, feature_cols),
+        picks,
+        (((0,), (0,)), ((), ())),
+        preferred_element_type=jnp.float32,
+    ).astype(jnp.bfloat16)
     hess_first, hess_mixed = curvature(
         tokens,
-        goal_rows,
+        goal_cols,
         weight,
         first_blocks,
         second_factor_blocks,

time: 152 us -> 152 us (level)
  no operation moved by 1% of the time
where the time goes in v7:
time: 152 us; the launch traced here: 151 us
  waiting for transfers between devices  58 us (38%)
  blocking collectives  36.4 us (24%)
  starting transfers between devices  27.5 us (18%)
  local copies, waits for them, and re-layouts  18.1 us (12%)
  matrix products  6.3 us (4%)
  other arithmetic  3.5 us (2%)
    all_to_all x1, waiting for transfers between devices, curvature(): mixed = lax.all_to_all(stacked, FE, split_axis=0, concat_axis=3, tiled=True)  35.1 us
    all_to_all x1, blocking collectives, per_device(): lax.all_to_all(partials, 'x', split_axis=1, concat_axis=1, tiled=True)  20.2 us
    all_to_all x1, blocking collectives, per_device(): lax.all_to_all(row_sums, 'y', split_axis=0, concat_axis=0, tiled=True)  16.1 us
    all_to_all x1, waiting for transfers between devices, curvature(): lax.all_to_all(back_merged, FE, split_axis=0, concat_axis=2, tiled=True)  15.3 us
    all_to_all x1, starting transfers between devices, curvature(): mixed = lax.all_to_all(stacked, FE, split_axis=0, concat_axis=3, tiled=True)  12.9 us
    all_to_all x1, starting transfers between devices, per_device(): lax.all_to_all(outgoing, DP, split_axis=0, concat_axis=0, tiled=True)  10.5 us
    all_to_all x1, waiting for transfers between devices, per_device(): lax.all_to_all(outgoing, DP, split_axis=0, concat_axis=0, tiled=True)  7.6 us
    unnamed x34, local copies, waits for them, and re-layouts  4.92 us
  transfers between devices with their start and end apart: 3, of which 3 were waited for; matrix products, arithmetic and copies ran while one was open for 6% of the time, Pallas kernels for 0%

profile of v7, /device:TPU:1, one launch (start us, length us, event | category | flops | bytes accessed | tf_op | source)
XLA Modules:
  0.0 150.8 jit_solution(16992500566892806563)
XLA Ops:
  0.7 0.9 select_reduce_fusion.2
  1.9 1.2 gather_fusion
  3.0 0.8 bitcast_select_fusion
  3.8 10.5 %all-to-all-start = ((bf16[32,8,512]{2,1,0:T(8,128)(2,1)}), bf16[32,8,512]{2,1,0:T(8,128)(2,1)S(1)}, u32[]{:S(2)}, u32[]{:S(2)}) async-start(bf16[32,8,512]{2,1,0:T(8,128)(2,1)} %bitcast_select_fusion), calls=%async_computation | async-start | bytes 524288 | tf_op jit(solution)/shard_map/all_to_all | solution.py:138
  14.3 0.7 fusion.31
  16.7 0.7 fusion.30
  18.0 7.6 %all-to-all-done = bf16[32,8,512]{2,1,0:T(8,128)(2,1)S(1)} async-done(((bf16[32,8,512]{2,1,0:T(8,128)(2,1)}), bf16[32,8,512]{2,1,0:T(8,128)(2,1)S(1)}, u32[]{:S(2)}, u32[]{:S(2)}) %all-to-all-start) | async-done | bytes 262176 | tf_op jit(solution)/shard_map/all_to_all | solution.py:138
  26.7 1.3 copy.151
  28.0 12.9 %all-to-all-start.1 = ((bf16[16,3,8,16,128]{4,2,3,1,0:T(8,128)(2,1)}), bf16[16,3,8,16,128]{4,2,3,1,0:T(8,128)(2,1)S(1)}, u32[]{:S(2)}, u32[]{:S(2)}) async-start(bf16[16,3,8,16,128]{4,2,3,1,0:T(8,128)(2,1)} %copy.151), calls=%async_computation.1 | async-start | bytes 3145728 | tf_op jit(solution)/shard_map/all_to_all | solution.py:56
  40.9 1.2 reshape.154
  42.1 2.2 %reshape.155 = bf16[8,16,8,2,256]{4,3,2,1,0:T(2,128)(2,1)} reshape(bf16[8,256,256]{2,1,0:T(8,128)(2,1)} %param.16) | data formatting | bytes 2097152 | tf_op jit(solution)/shard_map/reshape | solution.py:98
  44.4 35.1 %all-to-all-done.1 = bf16[16,3,8,16,128]{4,2,3,1,0:T(8,128)(2,1)S(1)} async-done(((bf16[16,3,8,16,128]{4,2,3,1,0:T(8,128)(2,1)}), bf16[16,3,8,16,128]{4,2,3,1,0:T(8,128)(2,1)S(1)}, u32[]{:S(2)}, u32[]{:S(2)}) %all-to-all-start.1) | async-done | bytes 1572896 | tf_op jit(solution)/shard_map/all_to_all | solution.py:56
  79.8 0.9 slice.22
  80.7 1.3 fusion.25
  82.0 1.2 copy.184
  83.3 0.9 fusion.10
  86.5 0.7 copy-done.1
  87.8 1.0 copy.160
  88.8 4.1 %all-to-all-start.2 = ((bf16[16,8,16,128]{3,1,2,0:T(8,128)(2,1)}), bf16[16,8,16,128]{3,1,2,0:T(8,128)(2,1)}, u32[]{:S(2)}, u32[]{:S(2)}) async-start(bf16[16,8,16,128]{3,1,2,0:T(8,128)(2,1)} %bitcast.38), calls=%async_computation.2 | async-start | bytes 1048576 | tf_op jit(solution)/shard_map/all_to_all | solution.py:104
  94.9 15.3 %all-to-all-done.2 = bf16[16,8,16,128]{3,1,2,0:T(8,128)(2,1)} async-done(((bf16[16,8,16,128]{3,1,2,0:T(8,128)(2,1)}), bf16[16,8,16,128]{3,1,2,0:T(8,128)(2,1)}, u32[]{:S(2)}, u32[]{:S(2)}) %all-to-all-start.2) | async-done | bytes 524320 | tf_op jit(solution)/shard_map/all_to_all | solution.py:104
  110.3 1.1 copy.161
  112.0 0.7 copy.168
  112.8 20.2 %all_to_all.48 = bf16[8,4,8,2560]{3,0,2,1:T(8,128)(2,1)S(1)} all-to-all(bf16[8,4,8,2560]{3,0,2,1:T(8,128)(2,1)S(1)} %copy.168), channel_id=1, replica_groups=mesh['y'=8,'x'=4,'z'=8,'core'=2] {'x'}, dimensions={1} | all-to-all | bytes 2621440 | tf_op jit(solution)/shard_map/all_to_all | solution.py:179
  133.3 16.1 %all_to_all.49 = bf16[8,8,2560]{2,1,0:T(8,128)(2,1)S(1)} all-to-all(bf16[8,8,2560]{2,1,0:T(8,128)(2,1)S(1)} %copy.170), channel_id=1, replica_groups=mesh['y'=8,'x'=4,'z'=8,'core'=2] {'y'}, dimensions={0} | all-to-all | bytes 655360 | tf_op jit(solution)/shard_map/all_to_all | solution.py:181
  (69 shorter events, 11.0 us)
Async XLA Ops:
  0.6 1.2 copy-start
  1.9 13.4 %copy-start.13 = (bf16[128,512]{1,0:T(8,128)(2,1)S(1)}, bf16[128,512]{1,0:T(8,128)(2,1)}, u32[]{:S(2)}) copy-start(bf16[128,512]{1,0:T(8,128)(2,1)} %param.10) | copy-start | bytes 393220
  1.9 13.6 %copy-start.10 = (bf16[8,64,256]{2,1,0:T(8,128)(2,1)S(1)}, bf16[8,64,256]{2,1,0:T(8,128)(2,1)}, u32[]{:S(2)}) copy-start(bf16[8,64,256]{2,1,0:T(8,128)(2,1)} %param.15) | copy-start | bytes 786436
  3.0 12.7 %copy-start.11 = (bf16[8,64,256]{2,1,0:T(8,128)(2,1)S(1)}, bf16[8,64,256]{2,1,0:T(8,128)(2,1)}, u32[]{:S(2)}) copy-start(bf16[8,64,256]{2,1,0:T(8,128)(2,1)} %param.12) | copy-start | bytes 786436
  3.8 21.8 %all-to-all-start = ((bf16[32,8,512]{2,1,0:T(8,128)(2,1)}), bf16[32,8,512]{2,1,0:T(8,128)(2,1)S(1)}, u32[]{:S(2)}, u32[]{:S(2)}) async-start(bf16[32,8,512]{2,1,0:T(8,128)(2,1)} %bitcast_select_fusion), calls=%async_computation | async-start | bytes 524288 | tf_op jit(solution)/shard_map/all_to_all | solution.py:138
  15.8 1.6 %copy-start.12 = (bf16[8,256,64]{1,2,0:T(8,128)(2,1)S(1)}, bf16[8,256,64]{1,2,0:T(8,128)(2,1)}, u32[]{:S(2)}) copy-start(bf16[8,256,64]{1,2,0:T(8,128)(2,1)} %param.14) | copy-start | bytes 786436
  28.0 12.9 %copy-start.2 = (bf16[8,256,256]{2,1,0:T(8,128)(2,1)S(1)}, bf16[8,256,256]{2,1,0:T(8,128)(2,1)}, u32[]{:S(2)}) copy-start(bf16[8,256,256]{2,1,0:T(8,128)(2,1)} %param.13) | copy-start | bytes 3145732
  28.0 51.4 %all-to-all-start.1 = ((bf16[16,3,8,16,128]{4,2,3,1,0:T(8,128)(2,1)}), bf16[16,3,8,16,128]{4,2,3,1,0:T(8,128)(2,1)S(1)}, u32[]{:S(2)}, u32[]{:S(2)}) async-start(bf16[16,3,8,16,128]{4,2,3,1,0:T(8,128)(2,1)} %copy.151), calls=%async_computation.1 | async-start | bytes 3145728 | tf_op jit(solution)/shard_map/all_to_all | solution.py:56
  79.4 1.2 copy-start.3
  80.7 2.6 %copy-start.4 = (bf16[8,256,256]{2,1,0:T(8,128)(2,1)S(1)}, bf16[8,256,256]{2,1,0:T(8,128)(2,1)}, u32[]{:S(2)}) copy-start(bf16[8,256,256]{2,1,0:T(8,128)(2,1)} %param.13) | copy-start | bytes 3145732
  83.3 1.2 copy-start.6
  83.3 1.5 %copy-start.7 = (f32[8,128,256]{2,1,0:T(8,128)S(1)}, f32[8,128,256]{2,1,0:T(8,128)}, u32[]{:S(2)}) copy-start(f32[8,128,256]{2,1,0:T(8,128)} %fusion.25) | copy-start | bytes 3145732
  84.2 2.3 %copy-start.8 = (bf16[8,256,128]{1,2,0:T(8,128)(2,1)}, bf16[8,256,128]{1,2,0:T(8,128)(2,1)S(1)}, u32[]{:S(2)}) copy-start(bf16[8,256,128]{1,2,0:T(8,128)(2,1)S(1)} %get-tuple-element.7) | copy-start | bytes 1572868
  84.8 1.2 copy-start.5
  86.0 1.2 copy-start.1
  87.8 5.2 %copy-start.9 = (bf16[8,256,128]{1,2,0:T(8,128)(2,1)S(1)}, bf16[8,256,128]{1,2,0:T(8,128)(2,1)}, u32[]{:S(2)}) copy-start(bf16[8,256,128]{1,2,0:T(8,128)(2,1)} %copy-done.8) | copy-start | bytes 1572868
  88.8 21.4 %all-to-all-start.2 = ((bf16[16,8,16,128]{3,1,2,0:T(8,128)(2,1)}), bf16[16,8,16,128]{3,1,2,0:T(8,128)(2,1)}, u32[]{:S(2)}, u32[]{:S(2)}) async-start(bf16[16,8,16,128]{3,1,2,0:T(8,128)(2,1)} %bitcast.38), calls=%async_computation.2 | async-start | bytes 1048576 | tf_op jit(solution)/shard_map/all_to_all | solution.py:104

commit v8 on v7

--- a/solution.py
+++ b/solution.py
@@ -101,12 +101,28 @@
     back_merged = back_mixed.astype(jnp.bfloat16).reshape(
         features, local_blocks, local_blocks * pair_size, row_count
     )
+    loaders = lax.axis_size(DP)
+    x_size = lax.axis_size("x")
+    me_x = lax.axis_index("x")
+    mixed_part = (
+        hess_mixed.reshape(local_blocks, loaders, -1)
+        .transpose(1, 0, 2)
+        .astype(jnp.bfloat16)
+        .reshape(loaders // x_size, x_size, local_blocks, -1)
+    )
+    mixed_rows = lax.dynamic_index_in_dim(mixed_part, me_x, 1, keepdims=False).astype(
+        jnp.float32
+    )
+    for shift in range(1, x_size):
+        piece = lax.dynamic_index_in_dim(mixed_part, (me_x + shift) % x_size, 1, keepdims=False)
+        moved = lax.ppermute(piece, "x", [(i, (i + shift) % x_size) for i in range(x_size)])
+        mixed_rows = mixed_rows + moved.astype(jnp.float32)
     back_first = lax.all_to_all(back_merged, FE, split_axis=0, concat_axis=2, tiled=True)
     back_first = back_first.reshape(local_blocks, block_out, row_count)
     hess_first = jnp.einsum(
         "rki,kjr->kij", token_blocks, back_first, preferred_element_type=jnp.float32
     )
-    return (hess_first, hess_mixed)
+    return (hess_first, mixed_rows)
 
 
 def per_device(
@@ -159,7 +175,7 @@
         (((0,), (0,)), ((), ())),
         preferred_element_type=jnp.float32,
     ).astype(jnp.bfloat16)
-    hess_first, hess_mixed = curvature(
+    hess_first, mixed_rows = curvature(
         tokens,
         goal_cols,
         weight,
@@ -170,14 +186,17 @@
         second_factor_tangent,
     )
     local_blocks = hess_first.shape[0]
-    first_part = hess_first.reshape(local_blocks, loaders, -1).transpose(1, 0, 2)
-    mixed_part = hess_mixed.reshape(local_blocks, loaders, -1).transpose(1, 0, 2)
-    first_width = first_part.shape[2]
-    partials = jnp.concatenate([first_part, mixed_part], axis=2).astype(jnp.bfloat16)
     x_size = lax.axis_size("x")
-    partials = partials.reshape(loaders // x_size, x_size, *partials.shape[1:])
-    across_x = lax.all_to_all(partials, "x", split_axis=1, concat_axis=1, tiled=True)
-    row_sums = jnp.sum(across_x.astype(jnp.float32), axis=1).astype(jnp.bfloat16)
+    first_part = (
+        hess_first.reshape(local_blocks, loaders, -1)
+        .transpose(1, 0, 2)
+        .astype(jnp.bfloat16)
+        .reshape(loaders // x_size, x_size, local_blocks, -1)
+    )
+    first_width = first_part.shape[3]
+    across_x = lax.all_to_all(first_part, "x", split_axis=1, concat_axis=1, tiled=True)
+    first_rows = jnp.sum(across_x.astype(jnp.float32), axis=1)
+    row_sums = jnp.concatenate([first_rows, mixed_rows], axis=2).astype(jnp.bfloat16)
     across_y = lax.all_to_all(row_sums, "y", split_axis=0, concat_axis=0, tiled=True)
     total = jnp.sum(across_y.astype(jnp.float32), axis=0)
     hess_first = total[:, :first_width].reshape(local_blocks, -1, first_blocks.shape[2])

time: 152 us -> 141 us (0.928)
  blocking collectives: 36.4 us -> 16.2 us
  starting transfers between devices: 27.5 us -> 40.2 us
  waiting for transfers between devices: 58 us -> 53.7 us
    all_to_all x1 -> x0, blocking collectives: 20.2 us -> none  [per_device(): lax.all_to_all(partials, 'x', split_axis=1, concat_axis=1, tiled=True)]
    all_to_all x1, waiting for transfers between devices: 15.3 us -> 5.96 us  [curvature(): lax.all_to_all(back_merged, FE, split_axis=0, concat_axis=2, tiled=True)]
    ppermute x0 -> x3, starting transfers between devices: none -> 9.21 us  [curvature(): lax.ppermute(piece, 'x', [(i, (i + shift) % x_size) for i in range(x_size)])]
    all_to_all x0 -> x1, waiting for transfers between devices: none -> 5.07 us  [per_device(): lax.all_to_all(first_part, 'x', split_axis=1, concat_axis=1, tiled=True)]
    all_to_all x0 -> x1, starting transfers between devices: none -> 3.4 us  [per_device(): lax.all_to_all(first_part, 'x', split_axis=1, concat_axis=1, tiled=True)]
  transfers between devices with their start and end apart: 3 -> 7, of which waited for: 3 -> 4; matrix products, arithmetic and copies ran while one was open for 6% -> 9% of each run, Pallas kernels for 0% -> 0%
where the time goes in v8:
time: 141 us; the launch traced here: 140 us
  waiting for transfers between devices  53.7 us (38%)
  starting transfers between devices  40.2 us (29%)
  local copies, waits for them, and re-layouts  18.2 us (13%)
  blocking collectives  16.2 us (11%)
  matrix products  6.29 us (4%)
  other arithmetic  4.34 us (3%)
    all_to_all x1, waiting for transfers between devices, curvature(): mixed = lax.all_to_all(stacked, FE, split_axis=0, concat_axis=3, tiled=True)  35.1 us
    all_to_all x1, blocking collectives, per_device(): lax.all_to_all(row_sums, 'y', split_axis=0, concat_axis=0, tiled=True)  16.2 us
    all_to_all x1, starting transfers between devices, curvature(): mixed = lax.all_to_all(stacked, FE, split_axis=0, concat_axis=3, tiled=True)  12.9 us
    all_to_all x1, starting transfers between devices, per_device(): lax.all_to_all(outgoing, DP, split_axis=0, concat_axis=0, tiled=True)  10.5 us
    ppermute x3, starting transfers between devices, curvature(): lax.ppermute(piece, 'x', [(i, (i + shift) % x_size) for i in range(x_size)])  9.21 us
    all_to_all x1, waiting for transfers between devices, per_device(): lax.all_to_all(outgoing, DP, split_axis=0, concat_axis=0, tiled=True)  7.6 us
    all_to_all x1, waiting for transfers between devices, curvature(): lax.all_to_all(back_merged, FE, split_axis=0, concat_axis=2, tiled=True)  5.96 us
    all_to_all x1, waiting for transfers between devices, per_device(): lax.all_to_all(first_part, 'x', split_axis=1, concat_axis=1, tiled=True)  5.07 us
  transfers between devices with their start and end apart: 7, of which 4 were waited for; matrix products, arithmetic and copies ran while one was open for 9% of the time, Pallas kernels for 0%

profile of v8, /device:TPU:1, one launch (start us, length us, event | category | flops | bytes accessed | tf_op | source)
XLA Modules:
  0.0 140.0 jit_solution(7907586287894505545)
XLA Ops:
  0.7 0.9 select_reduce_fusion.2
  1.9 1.2 gather_fusion
  3.8 10.5 %all-to-all-start = ((bf16[32,8,512]{2,1,0:T(8,128)(2,1)}), bf16[32,8,512]{2,1,0:T(8,128)(2,1)S(1)}, u32[]{:S(2)}, u32[]{:S(2)}) async-start(bf16[32,8,512]{2,1,0:T(8,128)(2,1)} %bitcast_select_fusion), calls=%async_computation | async-start | bytes 524288 | tf_op jit(solution)/shard_map/all_to_all | solution.py:154
  18.0 7.6 %all-to-all-done = bf16[32,8,512]{2,1,0:T(8,128)(2,1)S(1)} async-done(((bf16[32,8,512]{2,1,0:T(8,128)(2,1)}), bf16[32,8,512]{2,1,0:T(8,128)(2,1)S(1)}, u32[]{:S(2)}, u32[]{:S(2)}) %all-to-all-start) | async-done | bytes 262176 | tf_op jit(solution)/shard_map/all_to_all | solution.py:154
  26.7 1.3 copy.149
  28.0 12.9 %all-to-all-start.1 = ((bf16[16,3,8,16,128]{4,2,3,1,0:T(8,128)(2,1)}), bf16[16,3,8,16,128]{4,2,3,1,0:T(8,128)(2,1)S(1)}, u32[]{:S(2)}, u32[]{:S(2)}) async-start(bf16[16,3,8,16,128]{4,2,3,1,0:T(8,128)(2,1)} %copy.149), calls=%async_computation.1 | async-start | bytes 3145728 | tf_op jit(solution)/shard_map/all_to_all | solution.py:56
  40.9 1.2 reshape.153
  42.1 2.2 %reshape.154 = bf16[8,16,8,2,256]{4,3,2,1,0:T(2,128)(2,1)} reshape(bf16[8,256,256]{2,1,0:T(8,128)(2,1)} %param.16) | data formatting | bytes 2097152 | tf_op jit(solution)/shard_map/reshape | solution.py:98
  44.4 35.1 %all-to-all-done.1 = bf16[16,3,8,16,128]{4,2,3,1,0:T(8,128)(2,1)S(1)} async-done(((bf16[16,3,8,16,128]{4,2,3,1,0:T(8,128)(2,1)}), bf16[16,3,8,16,128]{4,2,3,1,0:T(8,128)(2,1)S(1)}, u32[]{:S(2)}, u32[]{:S(2)}) %all-to-all-start.1) | async-done | bytes 1572896 | tf_op jit(solution)/shard_map/all_to_all | solution.py:56
  80.7 1.3 fusion.28
  82.0 1.2 copy.182
  83.3 0.9 fusion.10
  87.8 1.0 copy.158
  88.8 4.1 %all-to-all-start.2 = ((bf16[16,8,16,128]{3,1,2,0:T(8,128)(2,1)}), bf16[16,8,16,128]{3,1,2,0:T(8,128)(2,1)}, u32[]{:S(2)}, u32[]{:S(2)}) async-start(bf16[16,8,16,128]{3,1,2,0:T(8,128)(2,1)} %bitcast.38), calls=%async_computation.2 | async-start | bytes 1048576 | tf_op jit(solution)/shard_map/all_to_all | solution.py:120
  95.0 1.9 %collective-permute-start = (bf16[8,8,2048]{2,1,0:T(8,128)(2,1)S(1)}, bf16[8,8,2048]{2,1,0:T(8,128)(2,1)S(1)}, u32[]{:S(2)}, u32[]{:S(2)}) collective-permute-start(bf16[8,8,2048]{2,1,0:T(8,128)(2,1)S(1)} %get-tuple-element.4), channel_id=1, source_target_pairs={{0,16},{16,32},{32,48},{48,0},{1,17},{17,33},{33,49},{49,1},{2,18}... | collective-permute-start | bytes 786440 | tf_op jit(solution)/shard_map/ppermute | solution.py:118
  97.0 4.2 %collective-permute-start.1 = (bf16[8,8,2048]{2,1,0:T(8,128)(2,1)S(1)}, bf16[8,8,2048]{2,1,0:T(8,128)(2,1)S(1)}, u32[]{:S(2)}, u32[]{:S(2)}) collective-permute-start(bf16[8,8,2048]{2,1,0:T(8,128)(2,1)S(1)} %get-tuple-element.6), channel_id=1, source_target_pairs={{0,32},{16,48},{32,0},{48,16},{1,33},{17,49},{33,1},{49,17},{2,34}... | collective-permute-start | bytes 786440 | tf_op jit(solution)/shard_map/ppermute | solution.py:118
  101.2 3.1 %collective-permute-start.2 = (bf16[8,8,2048]{2,1,0:T(8,128)(2,1)S(1)}, bf16[8,8,2048]{2,1,0:T(8,128)(2,1)}, u32[]{:S(2)}, u32[]{:S(2)}) collective-permute-start(bf16[8,8,2048]{2,1,0:T(8,128)(2,1)S(1)} %get-tuple-element.5), channel_id=1, source_target_pairs={{0,48},{16,0},{32,16},{48,32},{1,49},{17,1},{33,17},{49,33},{2,50}... | collective-permute-start | bytes 786440 | tf_op jit(solution)/shard_map/ppermute | solution.py:118
  104.3 6.0 %all-to-all-done.2 = bf16[16,8,16,128]{3,1,2,0:T(8,128)(2,1)} async-done(((bf16[16,8,16,128]{3,1,2,0:T(8,128)(2,1)}), bf16[16,8,16,128]{3,1,2,0:T(8,128)(2,1)}, u32[]{:S(2)}, u32[]{:S(2)}) %all-to-all-start.2) | async-done | bytes 524320 | tf_op jit(solution)/shard_map/all_to_all | solution.py:120
  110.2 1.1 copy.159
  111.9 0.8 copy.161
  112.8 3.4 %all-to-all-start.3 = ((bf16[8,4,8,512]{3,0,2,1:T(8,128)(2,1)}), bf16[8,4,8,512]{3,0,2,1:T(8,128)(2,1)S(1)}, u32[]{:S(2)}, u32[]{:S(2)}) async-start(bf16[8,4,8,512]{3,0,2,1:T(8,128)(2,1)} %copy.161), calls=%async_computation.3 | async-start | bytes 524288 | tf_op jit(solution)/shard_map/all_to_all | solution.py:197
  116.2 1.1 fusion.23
  117.3 5.1 %all-to-all-done.3 = bf16[8,4,8,512]{3,0,2,1:T(8,128)(2,1)S(1)} async-done(((bf16[8,4,8,512]{3,0,2,1:T(8,128)(2,1)}), bf16[8,4,8,512]{3,0,2,1:T(8,128)(2,1)S(1)}, u32[]{:S(2)}, u32[]{:S(2)}) %all-to-all-start.3) | async-done | bytes 262176 | tf_op jit(solution)/shard_map/all_to_all | solution.py:197
  122.5 16.2 %all_to_all.48 = bf16[8,8,2560]{2,1,0:T(8,128)(2,1)S(1)} all-to-all(bf16[8,8,2560]{2,1,0:T(8,128)(2,1)S(1)} %pad_maximum_fusion.1), channel_id=1, replica_groups=mesh['y'=8,'x'=4,'z'=8,'core'=2] {'y'}, dimensions={0} | all-to-all | bytes 655360 | tf_op jit(solution)/shard_map/all_to_all | solution.py:200
  (78 shorter events, 14.5 us)
Async XLA Ops:
  0.6 1.2 copy-start
  1.9 13.5 %copy-start.13 = (bf16[128,512]{1,0:T(8,128)(2,1)S(1)}, bf16[128,512]{1,0:T(8,128)(2,1)}, u32[]{:S(2)}) copy-start(bf16[128,512]{1,0:T(8,128)(2,1)} %param.10) | copy-start | bytes 393220
  1.9 13.6 %copy-start.10 = (bf16[8,64,256]{2,1,0:T(8,128)(2,1)S(1)}, bf16[8,64,256]{2,1,0:T(8,128)(2,1)}, u32[]{:S(2)}) copy-start(bf16[8,64,256]{2,1,0:T(8,128)(2,1)} %param.15) | copy-start | bytes 786436
  3.0 12.7 %copy-start.11 = (bf16[8,64,256]{2,1,0:T(8,128)(2,1)S(1)}, bf16[8,64,256]{2,1,0:T(8,128)(2,1)}, u32[]{:S(2)}) copy-start(bf16[8,64,256]{2,1,0:T(8,128)(2,1)} %param.12) | copy-start | bytes 786436
  3.8 21.8 %all-to-all-start = ((bf16[32,8,512]{2,1,0:T(8,128)(2,1)}), bf16[32,8,512]{2,1,0:T(8,128)(2,1)S(1)}, u32[]{:S(2)}, u32[]{:S(2)}) async-start(bf16[32,8,512]{2,1,0:T(8,128)(2,1)} %bitcast_select_fusion), calls=%async_computation | async-start | bytes 524288 | tf_op jit(solution)/shard_map/all_to_all | solution.py:154
  15.8 1.6 %copy-start.12 = (bf16[8,256,64]{1,2,0:T(8,128)(2,1)S(1)}, bf16[8,256,64]{1,2,0:T(8,128)(2,1)}, u32[]{:S(2)}) copy-start(bf16[8,256,64]{1,2,0:T(8,128)(2,1)} %param.14) | copy-start | bytes 786436
  28.0 12.9 %copy-start.2 = (bf16[8,256,256]{2,1,0:T(8,128)(2,1)S(1)}, bf16[8,256,256]{2,1,0:T(8,128)(2,1)}, u32[]{:S(2)}) copy-start(bf16[8,256,256]{2,1,0:T(8,128)(2,1)} %param.13) | copy-start | bytes 3145732
  28.0 51.4 %all-to-all-start.1 = ((bf16[16,3,8,16,128]{4,2,3,1,0:T(8,128)(2,1)}), bf16[16,3,8,16,128]{4,2,3,1,0:T(8,128)(2,1)S(1)}, u32[]{:S(2)}, u32[]{:S(2)}) async-start(bf16[16,3,8,16,128]{4,2,3,1,0:T(8,128)(2,1)} %copy.149), calls=%async_computation.1 | async-start | bytes 3145728 | tf_op jit(solution)/shard_map/all_to_all | solution.py:56
  79.4 1.2 copy-start.3
  80.7 2.6 %copy-start.4 = (bf16[8,256,256]{2,1,0:T(8,128)(2,1)S(1)}, bf16[8,256,256]{2,1,0:T(8,128)(2,1)}, u32[]{:S(2)}) copy-start(bf16[8,256,256]{2,1,0:T(8,128)(2,1)} %param.13) | copy-start | bytes 3145732
  83.3 1.2 copy-start.6
  83.3 1.5 %copy-start.7 = (f32[8,128,256]{2,1,0:T(8,128)S(1)}, f32[8,128,256]{2,1,0:T(8,128)}, u32[]{:S(2)}) copy-start(f32[8,128,256]{2,1,0:T(8,128)} %fusion.28) | copy-start | bytes 3145732
  84.2 2.3 %copy-start.8 = (bf16[8,256,128]{1,2,0:T(8,128)(2,1)}, bf16[8,256,128]{1,2,0:T(8,128)(2,1)S(1)}, u32[]{:S(2)}) copy-start(bf16[8,256,128]{1,2,0:T(8,128)(2,1)S(1)} %get-tuple-element.10) | copy-start | bytes 1572868
  84.8 1.2 copy-start.5
  86.0 1.2 copy-start.1
  87.8 5.2 %copy-start.9 = (bf16[8,256,128]{1,2,0:T(8,128)(2,1)S(1)}, bf16[8,256,128]{1,2,0:T(8,128)(2,1)}, u32[]{:S(2)}) copy-start(bf16[8,256,128]{1,2,0:T(8,128)(2,1)} %copy-done.8) | copy-start | bytes 1572868
  88.8 21.4 %all-to-all-start.2 = ((bf16[16,8,16,128]{3,1,2,0:T(8,128)(2,1)}), bf16[16,8,16,128]{3,1,2,0:T(8,128)(2,1)}, u32[]{:S(2)}, u32[]{:S(2)}) async-start(bf16[16,8,16,128]{3,1,2,0:T(8,128)(2,1)} %bitcast.38), calls=%async_computation.2 | async-start | bytes 1048576 | tf_op jit(solution)/shard_map/all_to_all | solution.py:120
  95.0 21.1 %collective-permute-start = (bf16[8,8,2048]{2,1,0:T(8,128)(2,1)S(1)}, bf16[8,8,2048]{2,1,0:T(8,128)(2,1)S(1)}, u32[]{:S(2)}, u32[]{:S(2)}) collective-permute-start(bf16[8,8,2048]{2,1,0:T(8,128)(2,1)S(1)} %get-tuple-element.4), channel_id=1, source_target_pairs={{0,16},{16,32},{32,48},{48,0},{1,17},{17,33},{33,49},{49,1},{2,18}... | collective-permute-start | bytes 786440 | tf_op jit(solution)/shard_map/ppermute | solution.py:118
  97.0 19.2 %collective-permute-start.1 = (bf16[8,8,2048]{2,1,0:T(8,128)(2,1)S(1)}, bf16[8,8,2048]{2,1,0:T(8,128)(2,1)S(1)}, u32[]{:S(2)}, u32[]{:S(2)}) collective-permute-start(bf16[8,8,2048]{2,1,0:T(8,128)(2,1)S(1)} %get-tuple-element.6), channel_id=1, source_target_pairs={{0,32},{16,48},{32,0},{48,16},{1,33},{17,49},{33,1},{49,17},{2,34}... | collective-permute-start | bytes 786440 | tf_op jit(solution)/shard_map/ppermute | solution.py:118
  101.2 15.0 %collective-permute-start.2 = (bf16[8,8,2048]{2,1,0:T(8,128)(2,1)S(1)}, bf16[8,8,2048]{2,1,0:T(8,128)(2,1)}, u32[]{:S(2)}, u32[]{:S(2)}) collective-permute-start(bf16[8,8,2048]{2,1,0:T(8,128)(2,1)S(1)} %get-tuple-element.5), channel_id=1, source_target_pairs={{0,48},{16,0},{32,16},{48,32},{1,49},{17,1},{33,17},{49,33},{2,50}... | collective-permute-start | bytes 786440 | tf_op jit(solution)/shard_map/ppermute | solution.py:118
  112.8 9.6 %all-to-all-start.3 = ((bf16[8,4,8,512]{3,0,2,1:T(8,128)(2,1)}), bf16[8,4,8,512]{3,0,2,1:T(8,128)(2,1)S(1)}, u32[]{:S(2)}, u32[]{:S(2)}) async-start(bf16[8,4,8,512]{3,0,2,1:T(8,128)(2,1)} %copy.161), calls=%async_computation.3 | async-start | bytes 524288 | tf_op jit(solution)/shard_map/all_to_all | solution.py:197

commit v9 on v8

--- a/solution.py
+++ b/solution.py
@@ -187,20 +187,32 @@
     )
     local_blocks = hess_first.shape[0]
     x_size = lax.axis_size("x")
+    me_x = lax.axis_index("x")
+    mixed_in = lax.all_to_all(
+        mixed_rows.astype(jnp.bfloat16), "y", split_axis=0, concat_axis=0, tiled=True
+    )
     first_part = (
         hess_first.reshape(local_blocks, loaders, -1)
         .transpose(1, 0, 2)
         .astype(jnp.bfloat16)
         .reshape(loaders // x_size, x_size, local_blocks, -1)
     )
-    first_width = first_part.shape[3]
-    across_x = lax.all_to_all(first_part, "x", split_axis=1, concat_axis=1, tiled=True)
-    first_rows = jnp.sum(across_x.astype(jnp.float32), axis=1)
-    row_sums = jnp.concatenate([first_rows, mixed_rows], axis=2).astype(jnp.bfloat16)
-    across_y = lax.all_to_all(row_sums, "y", split_axis=0, concat_axis=0, tiled=True)
-    total = jnp.sum(across_y.astype(jnp.float32), axis=0)
-    hess_first = total[:, :first_width].reshape(local_blocks, -1, first_blocks.shape[2])
-    hess_mixed = total[:, first_width:].reshape(local_blocks, -1, second_factor_blocks.shape[2])
+    first_rows = lax.dynamic_index_in_dim(first_part, me_x, 1, keepdims=False).astype(
+        jnp.float32
+    )
+    for shift in range(1, x_size):
+        piece = lax.dynamic_index_in_dim(first_part, (me_x + shift) % x_size, 1, keepdims=False)
+        moved = lax.ppermute(piece, "x", [(i, (i + shift) % x_size) for i in range(x_size)])
+        first_rows = first_rows + moved.astype(jnp.float32)
+    first_in = lax.all_to_all(
+        first_rows.astype(jnp.bfloat16), "y", split_axis=0, concat_axis=0, tiled=True
+    )
+    hess_first = jnp.sum(first_in.astype(jnp.float32), axis=0).reshape(
+        local_blocks, -1, first_blocks.shape[2]
+    )
+    hess_mixed = jnp.sum(mixed_in.astype(jnp.float32), axis=0).reshape(
+        local_blocks, -1, second_factor_blocks.shape[2]
+    )
     return (hess_first, hess_mixed)
 
 

time: 141 us -> 156 us (1.11)
  blocking collectives: 16.2 us -> 0 us
  starting transfers between devices: 40.2 us -> 52.7 us
  waiting for transfers between devices: 53.7 us -> 65.5 us
  matrix products: 6.29 us -> 10.2 us
    all_to_all x1 -> x0, blocking collectives: 16.2 us -> none  [per_device(): lax.all_to_all(row_sums, 'y', split_axis=0, concat_axis=0, tiled=True)]
    ppermute x3, waiting for transfers between devices: 0.01 us -> 12.3 us  [curvature(): lax.ppermute(piece, 'x', [(i, (i + shift) % x_size) for i in range(x_size)])]
    ppermute x0 -> x3, starting transfers between devices: none -> 7.2 us  [per_device(): lax.ppermute(piece, 'x', [(i, (i + shift) % x_size) for i in range(x_size)])]
    all_to_all x1 -> x2, starting transfers between devices: 3.4 us -> 9.97 us  [the longest x1 6.56 us: per_device(): lax.all_to_all(first_rows.astype(jnp.bfloat16), 'y', split_axis=0, concat...]
    all_to_all x1, waiting for transfers between devices: 5.96 us -> 0.01 us  [curvature(): lax.all_to_all(back_merged, FE, split_axis=0, concat_axis=2, tiled=True)]
    ppermute x0 -> x3, waiting for transfers between devices: none -> 4.01 us  [per_device(): lax.ppermute(piece, 'x', [(i, (i + shift) % x_size) for i in range(x_size)])]
    dot_general x1, matrix products: 0.42 us -> 3 us  [curvature(): jnp.einsum('evp,eqp->evq', mixed_activation, preactivation_tangent_gradie...]
    all_to_all x1 -> x2, waiting for transfers between devices: 5.07 us -> 6.54 us  [the longest x1 6.54 us: per_device(): lax.all_to_all(first_rows.astype(jnp.bfloat16), 'y', split_axis=0, concat...]
  transfers between devices with their start and end apart: 7 -> 11, of which waited for: 4 -> 8; matrix products, arithmetic and copies ran while one was open for 9% -> 11% of each run, Pallas kernels for 0% -> 0%
where the time goes in v9:
time: 156 us; the launch traced here: 153 us
  waiting for transfers between devices  65.5 us (42%)
  starting transfers between devices  52.7 us (34%)
  local copies, waits for them, and re-layouts  19.3 us (12%)
  matrix products  10.2 us (7%)
  other arithmetic  4.69 us (3%)
    all_to_all x1, waiting for transfers between devices, curvature(): mixed = lax.all_to_all(stacked, FE, split_axis=0, concat_axis=3, tiled=True)  35 us
    all_to_all x1, starting transfers between devices, curvature(): mixed = lax.all_to_all(stacked, FE, split_axis=0, concat_axis=3, tiled=True)  12.9 us
    ppermute x3, waiting for transfers between devices, curvature(): lax.ppermute(piece, 'x', [(i, (i + shift) % x_size) for i in range(x_size)])  12.3 us
    all_to_all x1, starting transfers between devices, per_device(): lax.all_to_all(outgoing, DP, split_axis=0, concat_axis=0, tiled=True)  10.5 us
    ppermute x3, starting transfers between devices, curvature(): lax.ppermute(piece, 'x', [(i, (i + shift) % x_size) for i in range(x_size)])  8 us
    all_to_all x1, waiting for transfers between devices, per_device(): lax.all_to_all(outgoing, DP, split_axis=0, concat_axis=0, tiled=True)  7.6 us
    ppermute x3, starting transfers between devices, per_device(): lax.ppermute(piece, 'x', [(i, (i + shift) % x_size) for i in range(x_size)])  7.2 us
    all_to_all x1, starting transfers between devices, per_device(): lax.all_to_all(first_rows.astype(jnp.bfloat16), 'y', split_axis=0, concat...  6.56 us
  transfers between devices with their start and end apart: 11, of which 8 were waited for; matrix products, arithmetic and copies ran while one was open for 11% of the time, Pallas kernels for 0%

profile of v9, /device:TPU:1, one launch (start us, length us, event | category | flops | bytes accessed | tf_op | source)
XLA Modules:
  0.0 153.5 jit_solution(729511559981818708)
XLA Ops:
  3.9 10.5 %all-to-all-start = ((bf16[32,8,512]{2,1,0:T(8,128)(2,1)}), bf16[32,8,512]{2,1,0:T(8,128)(2,1)S(1)}, u32[]{:S(2)}, u32[]{:S(2)}) async-start(bf16[32,8,512]{2,1,0:T(8,128)(2,1)} %bitcast_select_fusion), calls=%async_computation | async-start | bytes 524288 | tf_op jit(solution)/shard_map/all_to_all | solution.py:154
  18.1 7.6 %all-to-all-done = bf16[32,8,512]{2,1,0:T(8,128)(2,1)S(1)} async-done(((bf16[32,8,512]{2,1,0:T(8,128)(2,1)}), bf16[32,8,512]{2,1,0:T(8,128)(2,1)S(1)}, u32[]{:S(2)}, u32[]{:S(2)}) %all-to-all-start) | async-done | bytes 262176 | tf_op jit(solution)/shard_map/all_to_all | solution.py:154
  26.7 1.3 copy.118
  28.0 12.9 %all-to-all-start.1 = ((bf16[16,3,8,16,128]{4,2,3,1,0:T(8,128)(2,1)}), bf16[16,3,8,16,128]{4,2,3,1,0:T(8,128)(2,1)S(1)}, u32[]{:S(2)}, u32[]{:S(2)}) async-start(bf16[16,3,8,16,128]{4,2,3,1,0:T(8,128)(2,1)} %copy.118), calls=%async_computation.1 | async-start | bytes 3145728 | tf_op jit(solution)/shard_map/all_to_all | solution.py:56
  42.2 2.2 %reshape.156 = bf16[8,16,8,2,256]{4,3,2,1,0:T(2,128)(2,1)} reshape(bf16[8,256,256]{2,1,0:T(8,128)(2,1)} %param.16) | data formatting | bytes 2097152 | tf_op jit(solution)/shard_map/reshape | solution.py:98
  44.4 35.0 %all-to-all-done.1 = bf16[16,3,8,16,128]{4,2,3,1,0:T(8,128)(2,1)S(1)} async-done(((bf16[16,3,8,16,128]{4,2,3,1,0:T(8,128)(2,1)}), bf16[16,3,8,16,128]{4,2,3,1,0:T(8,128)(2,1)S(1)}, u32[]{:S(2)}, u32[]{:S(2)}) %all-to-all-start.1) | async-done | bytes 1572896 | tf_op jit(solution)/shard_map/all_to_all | solution.py:56
  80.7 1.3 fusion.28
  85.1 1.8 %fusion.27 = f32[8,256,256]{2,1,0:T(8,128)} fusion(bf16[8,256,128]{1,2,0:T(8,128)(2,1)S(1)} %get-tuple-element.13, bf16[1,3,8,256,128]{4,3,2,1,0:T(8,128)(2,1)S(1)} %bitcast.135), kind=kOutput, calls=%fused_computation.45 | convolution fusion | flops 134217728 | bytes 3145728 | tf_op jit(solution)/shard_map/evp,eqp->evq/dot_general | solution.py:78
  91.5 4.1 %all-to-all-start.2 = ((bf16[16,8,16,128]{3,1,2,0:T(8,128)(2,1)}), bf16[16,8,16,128]{3,1,2,0:T(8,128)(2,1)}, u32[]{:S(2)}, u32[]{:S(2)}) async-start(bf16[16,8,16,128]{3,1,2,0:T(8,128)(2,1)} %bitcast.38), calls=%async_computation.2 | async-start | bytes 1048576 | tf_op jit(solution)/shard_map/all_to_all | solution.py:120
  95.6 3.0 %add_convert_fusion = bf16[8,256,256]{2,1,0:T(8,128)(2,1)} fusion(f32[8,256,256]{2,1,0:T(8,128)} %fusion.27, bf16[8,256,128]{1,2,0:T(8,128)(2,1)S(1)} %fusion.4, bf16[1,3,8,256,128]{4,3,2,1,0:T(8,128)(2,1)S(1)} %bitcast.137), kind=kOutput, calls=%fused_computation.1 | convolution fusion | flops 135266304 | bytes 4194304 | tf_op jit(solution)/shard_map/evp,eqp->evq/dot_general | solution.py:83
  98.6 1.6 %convert_element_type.140 = bf16[8,32,2048]{2,1,0:T(8,128)(2,1)S(1)} reshape(bf16[8,256,256]{2,1,0:T(8,128)(2,1)} %add_convert_fusion) | data formatting | bytes 2097152 | tf_op jit(solution)/shard_map/convert_element_type | solution.py:110
  100.8 3.0 %collective-permute-start.5 = (bf16[8,8,2048]{2,1,0:T(8,128)(2,1)S(1)}, bf16[8,8,2048]{2,1,0:T(8,128)(2,1)S(1)}, u32[]{:S(2)}, u32[]{:S(2)}) collective-permute-start(bf16[8,8,2048]{2,1,0:T(8,128)(2,1)S(1)} %get-tuple-element.5), channel_id=1, source_target_pairs={{0,48},{16,0},{32,16},{48,32},{1,49},{17,1},{33,17},{49,33},{2,50}... | collective-permute-start | bytes 786440 | tf_op jit(solution)/shard_map/ppermute | solution.py:118
  103.9 2.5 %collective-permute-start.4 = (bf16[8,8,2048]{2,1,0:T(8,128)(2,1)S(1)}, bf16[8,8,2048]{2,1,0:T(8,128)(2,1)S(1)}, u32[]{:S(2)}, u32[]{:S(2)}) collective-permute-start(bf16[8,8,2048]{2,1,0:T(8,128)(2,1)S(1)} %get-tuple-element.6), channel_id=1, source_target_pairs={{0,32},{16,48},{32,0},{48,16},{1,33},{17,49},{33,1},{49,17},{2,34}... | collective-permute-start | bytes 786440 | tf_op jit(solution)/shard_map/ppermute | solution.py:118
  106.4 2.5 %collective-permute-start.3 = (bf16[8,8,2048]{2,1,0:T(8,128)(2,1)S(1)}, bf16[8,8,2048]{2,1,0:T(8,128)(2,1)S(1)}, u32[]{:S(2)}, u32[]{:S(2)}) collective-permute-start(bf16[8,8,2048]{2,1,0:T(8,128)(2,1)S(1)} %get-tuple-element.4), channel_id=1, source_target_pairs={{0,16},{16,32},{32,48},{48,0},{1,17},{17,33},{33,49},{49,1},{2,18}... | collective-permute-start | bytes 786440 | tf_op jit(solution)/shard_map/ppermute | solution.py:118
  108.9 1.7 %collective-permute-done.5 = bf16[8,8,2048]{2,1,0:T(8,128)(2,1)S(1)} collective-permute-done((bf16[8,8,2048]{2,1,0:T(8,128)(2,1)S(1)}, bf16[8,8,2048]{2,1,0:T(8,128)(2,1)S(1)}, u32[]{:S(2)}, u32[]{:S(2)}) %collective-permute-start.5) | collective-permute-done | bytes 262176 | tf_op jit(solution)/shard_map/ppermute | solution.py:118
  110.6 4.2 %collective-permute-done.4 = bf16[8,8,2048]{2,1,0:T(8,128)(2,1)S(1)} collective-permute-done((bf16[8,8,2048]{2,1,0:T(8,128)(2,1)S(1)}, bf16[8,8,2048]{2,1,0:T(8,128)(2,1)S(1)}, u32[]{:S(2)}, u32[]{:S(2)}) %collective-permute-start.4) | collective-permute-done | bytes 262176 | tf_op jit(solution)/shard_map/ppermute | solution.py:118
  114.8 6.4 %collective-permute-done.3 = bf16[8,8,2048]{2,1,0:T(8,128)(2,1)S(1)} collective-permute-done((bf16[8,8,2048]{2,1,0:T(8,128)(2,1)S(1)}, bf16[8,8,2048]{2,1,0:T(8,128)(2,1)S(1)}, u32[]{:S(2)}, u32[]{:S(2)}) %collective-permute-start.3) | collective-permute-done | bytes 262176 | tf_op jit(solution)/shard_map/ppermute | solution.py:118
  122.0 3.4 %all-to-all-start.4 = ((bf16[8,8,2048]{2,1,0:T(8,128)(2,1)}), bf16[8,8,2048]{2,1,0:T(8,128)(2,1)S(1)}, u32[]{:S(2)}, u32[]{:S(2)}) async-start(bf16[8,8,2048]{2,1,0:T(8,128)(2,1)} %fusion.23), calls=%async_computation.4 | async-start | bytes 524288 | tf_op jit(solution)/shard_map/all_to_all | solution.py:191
  127.1 1.9 %collective-permute-start.2 = (bf16[8,8,512]{2,1,0:T(8,128)(2,1)S(1)}, bf16[8,8,512]{2,1,0:T(8,128)(2,1)S(1)}, u32[]{:S(2)}, u32[]{:S(2)}) collective-permute-start(bf16[8,8,512]{2,1,0:T(8,128)(2,1)S(1)} %get-tuple-element.8), channel_id=1, source_target_pairs={{0,48},{16,0},{32,16},{48,32},{1,49},{17,1},{33,17},{49,33},{2,50}... | collective-permute-start | bytes 196616 | tf_op jit(solution)/shard_map/ppermute | solution.py:205
  129.0 2.5 %collective-permute-start.1 = (bf16[8,8,512]{2,1,0:T(8,128)(2,1)S(1)}, bf16[8,8,512]{2,1,0:T(8,128)(2,1)S(1)}, u32[]{:S(2)}, u32[]{:S(2)}) collective-permute-start(bf16[8,8,512]{2,1,0:T(8,128)(2,1)S(1)} %get-tuple-element.9), channel_id=1, source_target_pairs={{0,32},{16,48},{32,0},{48,16},{1,33},{17,49},{33,1},{49,17},{2,34}... | collective-permute-start | bytes 196616 | tf_op jit(solution)/shard_map/ppermute | solution.py:205
  131.5 2.8 %collective-permute-start = (bf16[8,8,512]{2,1,0:T(8,128)(2,1)S(1)}, bf16[8,8,512]{2,1,0:T(8,128)(2,1)S(1)}, u32[]{:S(2)}, u32[]{:S(2)}) collective-permute-start(bf16[8,8,512]{2,1,0:T(8,128)(2,1)S(1)} %get-tuple-element.7), channel_id=1, source_target_pairs={{0,16},{16,32},{32,48},{48,0},{1,17},{17,33},{33,49},{49,1},{2,18}... | collective-permute-start | bytes 196616 | tf_op jit(solution)/shard_map/ppermute | solution.py:205
  135.6 2.8 %collective-permute-done = bf16[8,8,512]{2,1,0:T(8,128)(2,1)S(1)} collective-permute-done((bf16[8,8,512]{2,1,0:T(8,128)(2,1)S(1)}, bf16[8,8,512]{2,1,0:T(8,128)(2,1)S(1)}, u32[]{:S(2)}, u32[]{:S(2)}) %collective-permute-start) | collective-permute-done | bytes 65568 | tf_op jit(solution)/shard_map/ppermute | solution.py:205
  139.0 6.6 %all-to-all-start.3 = ((bf16[8,8,512]{2,1,0:T(8,128)(2,1)}), bf16[8,8,512]{2,1,0:T(8,128)(2,1)S(1)}, u32[]{:S(2)}, u32[]{:S(2)}) async-start(bf16[8,8,512]{2,1,0:T(8,128)(2,1)} %fusion.32), calls=%async_computation.3 | async-start | bytes 131072 | tf_op jit(solution)/shard_map/all_to_all | solution.py:207
  146.3 6.5 %all-to-all-done.3 = bf16[8,8,512]{2,1,0:T(8,128)(2,1)S(1)} async-done(((bf16[8,8,512]{2,1,0:T(8,128)(2,1)}), bf16[8,8,512]{2,1,0:T(8,128)(2,1)S(1)}, u32[]{:S(2)}, u32[]{:S(2)}) %all-to-all-start.3) | async-done | bytes 65568 | tf_op jit(solution)/shard_map/all_to_all | solution.py:207
  (82 shorter events, 24.3 us)
Async XLA Ops:
  0.6 1.2 copy-start
  1.9 13.5 %copy-start.13 = (bf16[128,512]{1,0:T(8,128)(2,1)S(1)}, bf16[128,512]{1,0:T(8,128)(2,1)}, u32[]{:S(2)}) copy-start(bf16[128,512]{1,0:T(8,128)(2,1)} %param.10) | copy-start | bytes 393220
  1.9 13.6 %copy-start.10 = (bf16[8,64,256]{2,1,0:T(8,128)(2,1)S(1)}, bf16[8,64,256]{2,1,0:T(8,128)(2,1)}, u32[]{:S(2)}) copy-start(bf16[8,64,256]{2,1,0:T(8,128)(2,1)} %param.15) | copy-start | bytes 786436
  3.0 12.7 %copy-start.11 = (bf16[8,64,256]{2,1,0:T(8,128)(2,1)S(1)}, bf16[8,64,256]{2,1,0:T(8,128)(2,1)}, u32[]{:S(2)}) copy-start(bf16[8,64,256]{2,1,0:T(8,128)(2,1)} %param.12) | copy-start | bytes 786436
  3.9 21.8 %all-to-all-start = ((bf16[32,8,512]{2,1,0:T(8,128)(2,1)}), bf16[32,8,512]{2,1,0:T(8,128)(2,1)S(1)}, u32[]{:S(2)}, u32[]{:S(2)}) async-start(bf16[32,8,512]{2,1,0:T(8,128)(2,1)} %bitcast_select_fusion), calls=%async_computation | async-start | bytes 524288 | tf_op jit(solution)/shard_map/all_to_all | solution.py:154
  15.8 1.6 %copy-start.12 = (bf16[8,256,64]{1,2,0:T(8,128)(2,1)S(1)}, bf16[8,256,64]{1,2,0:T(8,128)(2,1)}, u32[]{:S(2)}) copy-start(bf16[8,256,64]{1,2,0:T(8,128)(2,1)} %param.14) | copy-start | bytes 786436
  28.0 12.9 %copy-start.2 = (bf16[8,256,256]{2,1,0:T(8,128)(2,1)S(1)}, bf16[8,256,256]{2,1,0:T(8,128)(2,1)}, u32[]{:S(2)}) copy-start(bf16[8,256,256]{2,1,0:T(8,128)(2,1)} %param.13) | copy-start | bytes 3145732
  28.0 51.4 %all-to-all-start.1 = ((bf16[16,3,8,16,128]{4,2,3,1,0:T(8,128)(2,1)}), bf16[16,3,8,16,128]{4,2,3,1,0:T(8,128)(2,1)S(1)}, u32[]{:S(2)}, u32[]{:S(2)}) async-start(bf16[16,3,8,16,128]{4,2,3,1,0:T(8,128)(2,1)} %copy.118), calls=%async_computation.1 | async-start | bytes 3145728 | tf_op jit(solution)/shard_map/all_to_all | solution.py:56
  79.4 1.2 copy-start.3
  82.0 2.1 %copy-start.4 = (bf16[8,256,256]{2,1,0:T(8,128)(2,1)S(1)}, bf16[8,256,256]{2,1,0:T(8,128)(2,1)}, u32[]{:S(2)}) copy-start(bf16[8,256,256]{2,1,0:T(8,128)(2,1)} %param.13) | copy-start | bytes 3145732
  85.0 1.8 %copy-start.6 = (bf16[8,256,256]{2,1,0:T(8,128)(2,1)S(1)}, bf16[8,256,256]{2,1,0:T(8,128)(2,1)}, u32[]{:S(2)}) copy-start(bf16[8,256,256]{2,1,0:T(8,128)(2,1)} %param.16) | copy-start | bytes 3145732
  85.0 1.9 %copy-start.7 = (f32[8,128,256]{2,1,0:T(8,128)S(1)}, f32[8,128,256]{2,1,0:T(8,128)}, u32[]{:S(2)}) copy-start(f32[8,128,256]{2,1,0:T(8,128)} %fusion.28) | copy-start | bytes 3145732
  85.0 2.4 %copy-start.9 = (bf16[1,1,8,256,128]{3,4,2,1,0:T(8,128)(2,1)S(1)}, bf16[1,1,8,256,128]{3,4,2,1,0:T(8,128)(2,1)}, u32[]{:S(2)}) copy-start(bf16[1,1,8,256,128]{3,4,2,1,0:T(8,128)(2,1)} %copy-done.8) | copy-start | bytes 1572868
  87.5 1.2 copy-start.5
  88.7 1.2 copy-start.1
  91.5 30.5 %all-to-all-start.2 = ((bf16[16,8,16,128]{3,1,2,0:T(8,128)(2,1)}), bf16[16,8,16,128]{3,1,2,0:T(8,128)(2,1)}, u32[]{:S(2)}, u32[]{:S(2)}) async-start(bf16[16,8,16,128]{3,1,2,0:T(8,128)(2,1)} %bitcast.38), calls=%async_computation.2 | async-start | bytes 1048576 | tf_op jit(solution)/shard_map/all_to_all | solution.py:120
  100.8 9.7 %collective-permute-start.5 = (bf16[8,8,2048]{2,1,0:T(8,128)(2,1)S(1)}, bf16[8,8,2048]{2,1,0:T(8,128)(2,1)S(1)}, u32[]{:S(2)}, u32[]{:S(2)}) collective-permute-start(bf16[8,8,2048]{2,1,0:T(8,128)(2,1)S(1)} %get-tuple-element.5), channel_id=1, source_target_pairs={{0,48},{16,0},{32,16},{48,32},{1,49},{17,1},{33,17},{49,33},{2,50}... | collective-permute-start | bytes 786440 | tf_op jit(solution)/shard_map/ppermute | solution.py:118
  103.9 10.9 %collective-permute-start.4 = (bf16[8,8,2048]{2,1,0:T(8,128)(2,1)S(1)}, bf16[8,8,2048]{2,1,0:T(8,128)(2,1)S(1)}, u32[]{:S(2)}, u32[]{:S(2)}) collective-permute-start(bf16[8,8,2048]{2,1,0:T(8,128)(2,1)S(1)} %get-tuple-element.6), channel_id=1, source_target_pairs={{0,32},{16,48},{32,0},{48,16},{1,33},{17,49},{33,1},{49,17},{2,34}... | collective-permute-start | bytes 786440 | tf_op jit(solution)/shard_map/ppermute | solution.py:118
  106.4 14.8 %collective-permute-start.3 = (bf16[8,8,2048]{2,1,0:T(8,128)(2,1)S(1)}, bf16[8,8,2048]{2,1,0:T(8,128)(2,1)S(1)}, u32[]{:S(2)}, u32[]{:S(2)}) collective-permute-start(bf16[8,8,2048]{2,1,0:T(8,128)(2,1)S(1)} %get-tuple-element.4), channel_id=1, source_target_pairs={{0,16},{16,32},{32,48},{48,0},{1,17},{17,33},{33,49},{49,1},{2,18}... | collective-permute-start | bytes 786440 | tf_op jit(solution)/shard_map/ppermute | solution.py:118
  122.0 17.0 %all-to-all-start.4 = ((bf16[8,8,2048]{2,1,0:T(8,128)(2,1)}), bf16[8,8,2048]{2,1,0:T(8,128)(2,1)S(1)}, u32[]{:S(2)}, u32[]{:S(2)}) async-start(bf16[8,8,2048]{2,1,0:T(8,128)(2,1)} %fusion.23), calls=%async_computation.4 | async-start | bytes 524288 | tf_op jit(solution)/shard_map/all_to_all | solution.py:191
  127.1 7.2 %collective-permute-start.2 = (bf16[8,8,512]{2,1,0:T(8,128)(2,1)S(1)}, bf16[8,8,512]{2,1,0:T(8,128)(2,1)S(1)}, u32[]{:S(2)}, u32[]{:S(2)}) collective-permute-start(bf16[8,8,512]{2,1,0:T(8,128)(2,1)S(1)} %get-tuple-element.8), channel_id=1, source_target_pairs={{0,48},{16,0},{32,16},{48,32},{1,49},{17,1},{33,17},{49,33},{2,50}... | collective-permute-start | bytes 196616 | tf_op jit(solution)/shard_map/ppermute | solution.py:205
  129.0 6.5 %collective-permute-start.1 = (bf16[8,8,512]{2,1,0:T(8,128)(2,1)S(1)}, bf16[8,8,512]{2,1,0:T(8,128)(2,1)S(1)}, u32[]{:S(2)}, u32[]{:S(2)}) collective-permute-start(bf16[8,8,512]{2,1,0:T(8,128)(2,1)S(1)} %get-tuple-element.9), channel_id=1, source_target_pairs={{0,32},{16,48},{32,0},{48,16},{1,33},{17,49},{33,1},{49,17},{2,34}... | collective-permute-start | bytes 196616 | tf_op jit(solution)/shard_map/ppermute | solution.py:205
  131.5 6.8 %collective-permute-start = (bf16[8,8,512]{2,1,0:T(8,128)(2,1)S(1)}, bf16[8,8,512]{2,1,0:T(8,128)(2,1)S(1)}, u32[]{:S(2)}, u32[]{:S(2)}) collective-permute-start(bf16[8,8,512]{2,1,0:T(8,128)(2,1)S(1)} %get-tuple-element.7), channel_id=1, source_target_pairs={{0,16},{16,32},{32,48},{48,0},{1,17},{17,33},{33,49},{49,1},{2,18}... | collective-permute-start | bytes 196616 | tf_op jit(solution)/shard_map/ppermute | solution.py:205
  139.0 13.8 %all-to-all-start.3 = ((bf16[8,8,512]{2,1,0:T(8,128)(2,1)}), bf16[8,8,512]{2,1,0:T(8,128)(2,1)S(1)}, u32[]{:S(2)}, u32[]{:S(2)}) async-start(bf16[8,8,512]{2,1,0:T(8,128)(2,1)} %fusion.32), calls=%async_computation.3 | async-start | bytes 131072 | tf_op jit(solution)/shard_map/all_to_all | solution.py:207
  (1 other events, 0.9 us)

commit v10 on v8

--- a/solution.py
+++ b/solution.py
@@ -2,6 +2,7 @@
 import jax.numpy as jnp
 from jax import lax
 from jax.sharding import Mesh, PartitionSpec as P
+
 
 DP = ("y", "x")
 FE = ("z", "core")
@@ -50,14 +51,13 @@
         * weight
     ).astype(jnp.bfloat16)
     merged = (features, local_blocks, local_blocks * pair_size, row_count)
-    stacked = jnp.stack(
-        [first_act.reshape(merged), tangents.reshape(merged), out_grad.reshape(merged)], axis=1
-    )
+    stacked = jnp.stack([first_act.reshape(merged), tangents.reshape(merged)], axis=1)
     mixed = lax.all_to_all(stacked, FE, split_axis=0, concat_axis=3, tiled=True)
+    hidden = lax.all_to_all(out_grad.reshape(merged), FE, split_axis=0, concat_axis=2, tiled=True)
     hidden_shape = (local_blocks, block_out, row_count)
     mixed_activation = mixed[0, 0].reshape(hidden_shape)
     mixed_tangent_value = mixed[0, 1].reshape(hidden_shape)
-    hidden_grad = mixed[0, 2].reshape(hidden_shape)
+    hidden_grad = hidden[0].reshape(hidden_shape)
     pre_act = jnp.einsum(
         "vca,vcf->vfa", mixed_activation, second_factor_blocks, preferred_element_type=jnp.float32
     )
@@ -151,7 +151,22 @@
     outgoing = jnp.take(targets, source.reshape(-1), axis=0).reshape(
         loaders, slot_rows, feature_cols
     )
-    arrived = lax.all_to_all(outgoing, DP, split_axis=0, concat_axis=0, tiled=True)
+    x_size = lax.axis_size("x")
+    y_size = loaders // x_size
+    me_x = lax.axis_index("x")
+    me_y = lax.axis_index("y")
+    by_column = outgoing.reshape(y_size, x_size, slot_rows, feature_cols).transpose(1, 0, 2, 3)
+    got = [lax.dynamic_index_in_dim(by_column, me_x, 0, keepdims=False)]
+    for shift in range(1, x_size):
+        piece = lax.dynamic_index_in_dim(by_column, (me_x + shift) % x_size, 0, keepdims=False)
+        got.append(lax.ppermute(piece, "x", [(i, (i + shift) % x_size) for i in range(x_size)]))
+    from_x = jnp.take(jnp.stack(got), (me_x - jnp.arange(x_size)) % x_size, axis=0)
+    by_row = from_x.transpose(1, 0, 2, 3)
+    got = [lax.dynamic_index_in_dim(by_row, me_y, 0, keepdims=False)]
+    for shift in range(1, y_size):
+        piece = lax.dynamic_index_in_dim(by_row, (me_y + shift) % y_size, 0, keepdims=False)
+        got.append(lax.ppermute(piece, "y", [(i, (i + shift) % y_size) for i in range(y_size)]))
+    arrived = jnp.take(jnp.stack(got), (me_y - jnp.arange(y_size)) % y_size, axis=0)
     my_lengths = lax.dynamic_index_in_dim(doc_lengths, device, 0, keepdims=False)
     my_owners = lax.dynamic_index_in_dim(doc_owners, device, 0, keepdims=False)
     my_starts = jnp.cumsum(my_lengths) - my_lengths
@@ -224,6 +239,5 @@
         P(),
     )
     out_specs = (P(FE, DP, None), P(FE, DP, None))
-    return jax.shard_map(
-        per_device, mesh=view, in_specs=in_specs, out_specs=out_specs, check_vma=False
-    )
+
+    return jax.shard_map(per_device, mesh=view, in_specs=in_specs, out_specs=out_specs, check_vma=False)

time: 141 us -> 173 us (1.23)
  starting transfers between devices: 40.2 us -> 75.9 us
  waiting for transfers between devices: 53.7 us -> 51 us
    ppermute x0 -> x10, starting transfers between devices: none -> 39.8 us  [the longest x7 28.4 us: per_device(): lax.ppermute(piece, 'y', [(i, (i + shift) % y_size) for i in range(y_size)])]
    all_to_all x1, waiting for transfers between devices: 35.1 us -> 23.8 us  [curvature(): mixed = lax.all_to_all(stacked, FE, split_axis=0, concat_axis=3, tiled=True)]
    all_to_all x1, starting transfers between devices: 12.9 us -> 4.23 us  [curvature(): mixed = lax.all_to_all(stacked, FE, split_axis=0, concat_axis=3, tiled=True)]
    all_to_all x1, waiting for transfers between devices: 7.6 us -> 14.5 us  [curvature(): lax.all_to_all(out_grad.reshape(merged), FE, split_axis=0, concat_axis=2,...]
    all_to_all x1, starting transfers between devices: 10.5 us -> 14.8 us  [curvature(): lax.all_to_all(out_grad.reshape(merged), FE, split_axis=0, concat_axis=2,...]
    unnamed x34 -> x36, local copies, waits for them, and re-layouts: 4.93 us -> 3.43 us
  transfers between devices with their start and end apart: 7 -> 17, of which waited for: 4 -> 5; matrix products, arithmetic and copies ran while one was open for 9% -> 8% of each run, Pallas kernels for 0% -> 0%
where the time goes in v10:
time: 173 us; the launch traced here: 172 us
  starting transfers between devices  75.9 us (44%)
  waiting for transfers between devices  51 us (29%)
  local copies, waits for them, and re-layouts  18.5 us (11%)
  blocking collectives  16.1 us (9%)
  matrix products  5.25 us (3%)
  other arithmetic  3.97 us (2%)
    ppermute x7, starting transfers between devices, per_device(): lax.ppermute(piece, 'y', [(i, (i + shift) % y_size) for i in range(y_size)])  28.4 us
    all_to_all x1, waiting for transfers between devices, curvature(): mixed = lax.all_to_all(stacked, FE, split_axis=0, concat_axis=3, tiled=True)  23.8 us
    all_to_all x1, blocking collectives, per_device(): lax.all_to_all(row_sums, 'y', split_axis=0, concat_axis=0, tiled=True)  16.1 us
    all_to_all x1, starting transfers between devices, curvature(): lax.all_to_all(out_grad.reshape(merged), FE, split_axis=0, concat_axis=2,...  14.8 us
    all_to_all x1, waiting for transfers between devices, curvature(): lax.all_to_all(out_grad.reshape(merged), FE, split_axis=0, concat_axis=2,...  14.5 us
    ppermute x3, starting transfers between devices, per_device(): lax.ppermute(piece, 'x', [(i, (i + shift) % x_size) for i in range(x_size)])  11.4 us
    ppermute x3, starting transfers between devices, curvature(): lax.ppermute(piece, 'x', [(i, (i + shift) % x_size) for i in range(x_size)])  9.29 us
    all_to_all x1, waiting for transfers between devices, per_device(): lax.all_to_all(first_part, 'x', split_axis=1, concat_axis=1, tiled=True)  5.63 us
  transfers between devices with their start and end apart: 17, of which 5 were waited for; matrix products, arithmetic and copies ran while one was open for 8% of the time, Pallas kernels for 0%

profile of v10, /device:TPU:1, one launch (start us, length us, event | category | flops | bytes accessed | tf_op | source)
XLA Modules:
  0.0 172.3 jit_solution(16387663178301209027)
XLA Ops:
  3.4 3.9 %collective-permute-start = (bf16[8,8,512]{2,1,0:T(8,128)(2,1)S(1)}, bf16[8,8,512]{2,1,0:T(8,128)(2,1)S(1)}, u32[]{:S(2)}, u32[]{:S(2)}) collective-permute-start(bf16[8,8,512]{2,1,0:T(8,128)(2,1)S(1)} %get-tuple-element.17), channel_id=1, source_target_pairs={{0,16},{16,32},{32,48},{48,0},{1,17},{17,33},{33,49},{49,1},{2,18}... | collective-permute-start | bytes 196616 | tf_op jit(solution)/shard_map/ppermute | solution.py:162
  7.3 4.4 %collective-permute-start.1 = (bf16[8,8,512]{2,1,0:T(8,128)(2,1)S(1)}, bf16[8,8,512]{2,1,0:T(8,128)(2,1)S(1)}, u32[]{:S(2)}, u32[]{:S(2)}) collective-permute-start(bf16[8,8,512]{2,1,0:T(8,128)(2,1)S(1)} %get-tuple-element.16), channel_id=1, source_target_pairs={{0,32},{16,48},{32,0},{48,16},{1,33},{17,49},{33,1},{49,17},{2,34}... | collective-permute-start | bytes 196616 | tf_op jit(solution)/shard_map/ppermute | solution.py:162
  11.7 3.1 %collective-permute-start.2 = (bf16[8,8,512]{2,1,0:T(8,128)(2,1)S(1)}, bf16[8,8,512]{2,1,0:T(8,128)(2,1)S(1)}, u32[]{:S(2)}, u32[]{:S(2)}) collective-permute-start(bf16[8,8,512]{2,1,0:T(8,128)(2,1)S(1)} %get-tuple-element.15), channel_id=1, source_target_pairs={{0,48},{16,0},{32,16},{48,32},{1,49},{17,1},{33,17},{49,33},{2,50}... | collective-permute-start | bytes 196616 | tf_op jit(solution)/shard_map/ppermute | solution.py:162
  18.2 3.2 %collective-permute-start.3 = (bf16[4,8,512]{2,1,0:T(8,128)(2,1)S(1)}, bf16[4,8,512]{2,1,0:T(8,128)(2,1)S(1)}, u32[]{:S(2)}, u32[]{:S(2)}) collective-permute-start(bf16[4,8,512]{2,1,0:T(8,128)(2,1)S(1)} %get-tuple-element.13), channel_id=1, source_target_pairs={{0,64},{64,128},{128,192},{192,256},{256,320},{320,384},{384,448},... | collective-permute-start | bytes 98312 | tf_op jit(solution)/shard_map/ppermute | solution.py:168
  21.4 4.2 %collective-permute-start.4 = (bf16[4,8,512]{2,1,0:T(8,128)(2,1)S(1)}, bf16[4,8,512]{2,1,0:T(8,128)(2,1)S(1)}, u32[]{:S(2)}, u32[]{:S(2)}) collective-permute-start(bf16[4,8,512]{2,1,0:T(8,128)(2,1)S(1)} %get-tuple-element.12), channel_id=1, source_target_pairs={{0,128},{64,192},{128,256},{192,320},{256,384},{320,448},{384,0},{... | collective-permute-start | bytes 98312 | tf_op jit(solution)/shard_map/ppermute | solution.py:168
  25.6 4.6 %collective-permute-start.5 = (bf16[4,8,512]{2,1,0:T(8,128)(2,1)S(1)}, bf16[4,8,512]{2,1,0:T(8,128)(2,1)S(1)}, u32[]{:S(2)}, u32[]{:S(2)}) collective-permute-start(bf16[4,8,512]{2,1,0:T(8,128)(2,1)S(1)} %get-tuple-element.11), channel_id=1, source_target_pairs={{0,192},{64,256},{128,320},{192,384},{256,448},{320,0},{384,64},{4... | collective-permute-start | bytes 98312 | tf_op jit(solution)/shard_map/ppermute | solution.py:168
  30.3 3.5 %collective-permute-start.6 = (bf16[4,8,512]{2,1,0:T(8,128)(2,1)S(1)}, bf16[4,8,512]{2,1,0:T(8,128)(2,1)S(1)}, u32[]{:S(2)}, u32[]{:S(2)}) collective-permute-start(bf16[4,8,512]{2,1,0:T(8,128)(2,1)S(1)} %get-tuple-element.10), channel_id=1, source_target_pairs={{0,256},{64,320},{128,384},{192,448},{256,0},{320,64},{384,128},{4... | collective-permute-start | bytes 98312 | tf_op jit(solution)/shard_map/ppermute | solution.py:168
  33.8 4.9 %collective-permute-start.7 = (bf16[4,8,512]{2,1,0:T(8,128)(2,1)S(1)}, bf16[4,8,512]{2,1,0:T(8,128)(2,1)S(1)}, u32[]{:S(2)}, u32[]{:S(2)}) collective-permute-start(bf16[4,8,512]{2,1,0:T(8,128)(2,1)S(1)} %get-tuple-element.9), channel_id=1, source_target_pairs={{0,320},{64,384},{128,448},{192,0},{256,64},{320,128},{384,192},{4... | collective-permute-start | bytes 98312 | tf_op jit(solution)/shard_map/ppermute | solution.py:168
  38.7 5.0 %collective-permute-start.8 = (bf16[4,8,512]{2,1,0:T(8,128)(2,1)S(1)}, bf16[4,8,512]{2,1,0:T(8,128)(2,1)S(1)}, u32[]{:S(2)}, u32[]{:S(2)}) collective-permute-start(bf16[4,8,512]{2,1,0:T(8,128)(2,1)S(1)} %get-tuple-element.8), channel_id=1, source_target_pairs={{0,384},{64,448},{128,0},{192,64},{256,128},{320,192},{384,256},{4... | collective-permute-start | bytes 98312 | tf_op jit(solution)/shard_map/ppermute | solution.py:168
  43.7 3.0 %collective-permute-start.9 = (bf16[4,8,512]{2,1,0:T(8,128)(2,1)S(1)}, bf16[4,8,512]{2,1,0:T(8,128)(2,1)S(1)}, u32[]{:S(2)}, u32[]{:S(2)}) collective-permute-start(bf16[4,8,512]{2,1,0:T(8,128)(2,1)S(1)} %get-tuple-element.7), channel_id=1, source_target_pairs={{0,448},{64,0},{128,64},{192,128},{256,192},{320,256},{384,320},{4... | collective-permute-start | bytes 98312 | tf_op jit(solution)/shard_map/ppermute | solution.py:168
  46.8 1.7 collective-permute-done.9
  50.9 14.8 %all-to-all-start = ((bf16[16,8,16,128]{3,1,2,0:T(8,128)(2,1)}), bf16[16,8,16,128]{3,1,2,0:T(8,128)(2,1)S(1)}, u32[]{:S(2)}, u32[]{:S(2)}) async-start(bf16[16,8,16,128]{3,1,2,0:T(8,128)(2,1)} %bitcast.36), calls=%async_computation | async-start | bytes 1048576 | tf_op jit(solution)/shard_map/all_to_all | solution.py:56
  68.4 14.5 %all-to-all-done = bf16[16,8,16,128]{3,1,2,0:T(8,128)(2,1)S(1)} async-done(((bf16[16,8,16,128]{3,1,2,0:T(8,128)(2,1)}), bf16[16,8,16,128]{3,1,2,0:T(8,128)(2,1)S(1)}, u32[]{:S(2)}, u32[]{:S(2)}) %all-to-all-start) | async-done | bytes 524320 | tf_op jit(solution)/shard_map/all_to_all | solution.py:56
  83.0 4.2 %all-to-all-start.1 = ((bf16[16,2,8,16,128]{4,2,3,1,0:T(8,128)(2,1)}), bf16[16,2,8,16,128]{4,2,3,1,0:T(8,128)(2,1)}, u32[]{:S(2)}, u32[]{:S(2)}) async-start(bf16[16,2,8,16,128]{4,2,3,1,0:T(8,128)(2,1)} %copy.158), calls=%async_computation.1 | async-start | bytes 2097152 | tf_op jit(solution)/shard_map/all_to_all | solution.py:55
  90.2 23.8 %all-to-all-done.1 = bf16[16,2,8,16,128]{4,2,3,1,0:T(8,128)(2,1)} async-done(((bf16[16,2,8,16,128]{4,2,3,1,0:T(8,128)(2,1)}), bf16[16,2,8,16,128]{4,2,3,1,0:T(8,128)(2,1)}, u32[]{:S(2)}, u32[]{:S(2)}) %all-to-all-start.1) | async-done | bytes 1048608 | tf_op jit(solution)/shard_map/all_to_all | solution.py:55
  114.0 1.4 copy.159
  121.0 4.1 %all-to-all-start.2 = ((bf16[16,8,16,128]{3,1,2,0:T(8,128)(2,1)}), bf16[16,8,16,128]{3,1,2,0:T(8,128)(2,1)}, u32[]{:S(2)}, u32[]{:S(2)}) async-start(bf16[16,8,16,128]{3,1,2,0:T(8,128)(2,1)} %bitcast.65), calls=%async_computation.2 | async-start | bytes 1048576 | tf_op jit(solution)/shard_map/all_to_all | solution.py:120
  127.2 2.1 %collective-permute-start.10 = (bf16[8,8,2048]{2,1,0:T(8,128)(2,1)S(1)}, bf16[8,8,2048]{2,1,0:T(8,128)(2,1)S(1)}, u32[]{:S(2)}, u32[]{:S(2)}) collective-permute-start(bf16[8,8,2048]{2,1,0:T(8,128)(2,1)S(1)} %get-tuple-element.4), channel_id=1, source_target_pairs={{0,16},{16,32},{32,48},{48,0},{1,17},{17,33},{33,49},{49,1},{2,18}... | collective-permute-start | bytes 786440 | tf_op jit(solution)/shard_map/ppermute | solution.py:118
  129.3 5.3 %collective-permute-start.11 = (bf16[8,8,2048]{2,1,0:T(8,128)(2,1)S(1)}, bf16[8,8,2048]{2,1,0:T(8,128)(2,1)S(1)}, u32[]{:S(2)}, u32[]{:S(2)}) collective-permute-start(bf16[8,8,2048]{2,1,0:T(8,128)(2,1)S(1)} %get-tuple-element.6), channel_id=1, source_target_pairs={{0,32},{16,48},{32,0},{48,16},{1,33},{17,49},{33,1},{49,17},{2,34}... | collective-permute-start | bytes 786440 | tf_op jit(solution)/shard_map/ppermute | solution.py:118
  134.6 1.9 %collective-permute-start.12 = (bf16[8,8,2048]{2,1,0:T(8,128)(2,1)S(1)}, bf16[8,8,2048]{2,1,0:T(8,128)(2,1)}, u32[]{:S(2)}, u32[]{:S(2)}) collective-permute-start(bf16[8,8,2048]{2,1,0:T(8,128)(2,1)S(1)} %get-tuple-element.5), channel_id=1, source_target_pairs={{0,48},{16,0},{32,16},{48,32},{1,49},{17,1},{33,17},{49,33},{2,50}... | collective-permute-start | bytes 786440 | tf_op jit(solution)/shard_map/ppermute | solution.py:118
  136.5 5.3 %all-to-all-done.2 = bf16[16,8,16,128]{3,1,2,0:T(8,128)(2,1)} async-done(((bf16[16,8,16,128]{3,1,2,0:T(8,128)(2,1)}), bf16[16,8,16,128]{3,1,2,0:T(8,128)(2,1)}, u32[]{:S(2)}, u32[]{:S(2)}) %all-to-all-start.2) | async-done | bytes 524320 | tf_op jit(solution)/shard_map/all_to_all | solution.py:120
  144.3 3.6 %all-to-all-start.3 = ((bf16[8,4,8,512]{3,0,2,1:T(8,128)(2,1)}), bf16[8,4,8,512]{3,0,2,1:T(8,128)(2,1)S(1)}, u32[]{:S(2)}, u32[]{:S(2)}) async-start(bf16[8,4,8,512]{3,0,2,1:T(8,128)(2,1)} %copy.171), calls=%async_computation.3 | async-start | bytes 524288 | tf_op jit(solution)/shard_map/all_to_all | solution.py:212
  149.1 5.6 %all-to-all-done.3 = bf16[8,4,8,512]{3,0,2,1:T(8,128)(2,1)S(1)} async-done(((bf16[8,4,8,512]{3,0,2,1:T(8,128)(2,1)}), bf16[8,4,8,512]{3,0,2,1:T(8,128)(2,1)S(1)}, u32[]{:S(2)}, u32[]{:S(2)}) %all-to-all-start.3) | async-done | bytes 262176 | tf_op jit(solution)/shard_map/all_to_all | solution.py:212
  154.8 16.1 %all_to_all.52 = bf16[8,8,2560]{2,1,0:T(8,128)(2,1)S(1)} all-to-all(bf16[8,8,2560]{2,1,0:T(8,128)(2,1)S(1)} %pad_maximum_fusion.1), channel_id=1, replica_groups=mesh['y'=8,'x'=4,'z'=8,'core'=2] {'y'}, dimensions={0} | all-to-all | bytes 655360 | tf_op jit(solution)/shard_map/all_to_all | solution.py:215
  (119 shorter events, 26.3 us)
Async XLA Ops:
  0.6 16.4 %copy-start.8 = (bf16[8,256,64]{1,2,0:T(8,128)(2,1)S(1)}, bf16[8,256,64]{1,2,0:T(8,128)(2,1)}, u32[]{:S(2)}) copy-start(bf16[8,256,64]{1,2,0:T(8,128)(2,1)} %param.14) | copy-start | bytes 786436
  3.4 14.0 %collective-permute-start = (bf16[8,8,512]{2,1,0:T(8,128)(2,1)S(1)}, bf16[8,8,512]{2,1,0:T(8,128)(2,1)S(1)}, u32[]{:S(2)}, u32[]{:S(2)}) collective-permute-start(bf16[8,8,512]{2,1,0:T(8,128)(2,1)S(1)} %get-tuple-element.17), channel_id=1, source_target_pairs={{0,16},{16,32},{32,48},{48,0},{1,17},{17,33},{33,49},{49,1},{2,18}... | collective-permute-start | bytes 196616 | tf_op jit(solution)/shard_map/ppermute | solution.py:162
  7.3 10.1 %collective-permute-start.1 = (bf16[8,8,512]{2,1,0:T(8,128)(2,1)S(1)}, bf16[8,8,512]{2,1,0:T(8,128)(2,1)S(1)}, u32[]{:S(2)}, u32[]{:S(2)}) collective-permute-start(bf16[8,8,512]{2,1,0:T(8,128)(2,1)S(1)} %get-tuple-element.16), channel_id=1, source_target_pairs={{0,32},{16,48},{32,0},{48,16},{1,33},{17,49},{33,1},{49,17},{2,34}... | collective-permute-start | bytes 196616 | tf_op jit(solution)/shard_map/ppermute | solution.py:162
  11.7 5.7 %collective-permute-start.2 = (bf16[8,8,512]{2,1,0:T(8,128)(2,1)S(1)}, bf16[8,8,512]{2,1,0:T(8,128)(2,1)S(1)}, u32[]{:S(2)}, u32[]{:S(2)}) collective-permute-start(bf16[8,8,512]{2,1,0:T(8,128)(2,1)S(1)} %get-tuple-element.15), channel_id=1, source_target_pairs={{0,48},{16,0},{32,16},{48,32},{1,49},{17,1},{33,17},{49,33},{2,50}... | collective-permute-start | bytes 196616 | tf_op jit(solution)/shard_map/ppermute | solution.py:162
  18.2 20.5 %collective-permute-start.3 = (bf16[4,8,512]{2,1,0:T(8,128)(2,1)S(1)}, bf16[4,8,512]{2,1,0:T(8,128)(2,1)S(1)}, u32[]{:S(2)}, u32[]{:S(2)}) collective-permute-start(bf16[4,8,512]{2,1,0:T(8,128)(2,1)S(1)} %get-tuple-element.13), channel_id=1, source_target_pairs={{0,64},{64,128},{128,192},{192,256},{256,320},{320,384},{384,448},... | collective-permute-start | bytes 98312 | tf_op jit(solution)/shard_map/ppermute | solution.py:168
  21.4 22.3 %collective-permute-start.4 = (bf16[4,8,512]{2,1,0:T(8,128)(2,1)S(1)}, bf16[4,8,512]{2,1,0:T(8,128)(2,1)S(1)}, u32[]{:S(2)}, u32[]{:S(2)}) collective-permute-start(bf16[4,8,512]{2,1,0:T(8,128)(2,1)S(1)} %get-tuple-element.12), channel_id=1, source_target_pairs={{0,128},{64,192},{128,256},{192,320},{256,384},{320,448},{384,0},{... | collective-permute-start | bytes 98312 | tf_op jit(solution)/shard_map/ppermute | solution.py:168
  25.6 21.1 %collective-permute-start.5 = (bf16[4,8,512]{2,1,0:T(8,128)(2,1)S(1)}, bf16[4,8,512]{2,1,0:T(8,128)(2,1)S(1)}, u32[]{:S(2)}, u32[]{:S(2)}) collective-permute-start(bf16[4,8,512]{2,1,0:T(8,128)(2,1)S(1)} %get-tuple-element.11), channel_id=1, source_target_pairs={{0,192},{64,256},{128,320},{192,384},{256,448},{320,0},{384,64},{4... | collective-permute-start | bytes 98312 | tf_op jit(solution)/shard_map/ppermute | solution.py:168
  30.3 16.5 %collective-permute-start.6 = (bf16[4,8,512]{2,1,0:T(8,128)(2,1)S(1)}, bf16[4,8,512]{2,1,0:T(8,128)(2,1)S(1)}, u32[]{:S(2)}, u32[]{:S(2)}) collective-permute-start(bf16[4,8,512]{2,1,0:T(8,128)(2,1)S(1)} %get-tuple-element.10), channel_id=1, source_target_pairs={{0,256},{64,320},{128,384},{192,448},{256,0},{320,64},{384,128},{4... | collective-permute-start | bytes 98312 | tf_op jit(solution)/shard_map/ppermute | solution.py:168
  33.8 12.9 %collective-permute-start.7 = (bf16[4,8,512]{2,1,0:T(8,128)(2,1)S(1)}, bf16[4,8,512]{2,1,0:T(8,128)(2,1)S(1)}, u32[]{:S(2)}, u32[]{:S(2)}) collective-permute-start(bf16[4,8,512]{2,1,0:T(8,128)(2,1)S(1)} %get-tuple-element.9), channel_id=1, source_target_pairs={{0,320},{64,384},{128,448},{192,0},{256,64},{320,128},{384,192},{4... | collective-permute-start | bytes 98312 | tf_op jit(solution)/shard_map/ppermute | solution.py:168
  38.7 8.1 %collective-permute-start.8 = (bf16[4,8,512]{2,1,0:T(8,128)(2,1)S(1)}, bf16[4,8,512]{2,1,0:T(8,128)(2,1)S(1)}, u32[]{:S(2)}, u32[]{:S(2)}) collective-permute-start(bf16[4,8,512]{2,1,0:T(8,128)(2,1)S(1)} %get-tuple-element.8), channel_id=1, source_target_pairs={{0,384},{64,448},{128,0},{192,64},{256,128},{320,192},{384,256},{4... | collective-permute-start | bytes 98312 | tf_op jit(solution)/shard_map/ppermute | solution.py:168
  43.7 4.8 %collective-permute-start.9 = (bf16[4,8,512]{2,1,0:T(8,128)(2,1)S(1)}, bf16[4,8,512]{2,1,0:T(8,128)(2,1)S(1)}, u32[]{:S(2)}, u32[]{:S(2)}) collective-permute-start(bf16[4,8,512]{2,1,0:T(8,128)(2,1)S(1)} %get-tuple-element.7), channel_id=1, source_target_pairs={{0,448},{64,0},{128,64},{192,128},{256,192},{320,256},{384,320},{4... | collective-permute-start | bytes 98312 | tf_op jit(solution)/shard_map/ppermute | solution.py:168
  49.1 16.7 %copy-start.11 = (bf16[128,512]{1,0:T(8,128)(2,1)S(1)}, bf16[128,512]{1,0:T(8,128)(2,1)}, u32[]{:S(2)}) copy-start(bf16[128,512]{1,0:T(8,128)(2,1)} %param.10) | copy-start | bytes 393220
  49.2 16.7 %copy-start.9 = (bf16[8,64,256]{2,1,0:T(8,128)(2,1)S(1)}, bf16[8,64,256]{2,1,0:T(8,128)(2,1)}, u32[]{:S(2)}) copy-start(bf16[8,64,256]{2,1,0:T(8,128)(2,1)} %param.12) | copy-start | bytes 786436
  50.9 15.6 %copy-start.10 = (bf16[8,64,256]{2,1,0:T(8,128)(2,1)S(1)}, bf16[8,64,256]{2,1,0:T(8,128)(2,1)}, u32[]{:S(2)}) copy-start(bf16[8,64,256]{2,1,0:T(8,128)(2,1)} %param.15) | copy-start | bytes 786436
  50.9 32.0 %all-to-all-start = ((bf16[16,8,16,128]{3,1,2,0:T(8,128)(2,1)}), bf16[16,8,16,128]{3,1,2,0:T(8,128)(2,1)S(1)}, u32[]{:S(2)}, u32[]{:S(2)}) async-start(bf16[16,8,16,128]{3,1,2,0:T(8,128)(2,1)} %bitcast.36), calls=%async_computation | async-start | bytes 1048576 | tf_op jit(solution)/shard_map/all_to_all | solution.py:56
  67.4 19.9 %copy-start.1 = (bf16[8,256,256]{2,1,0:T(8,128)(2,1)S(1)}, bf16[8,256,256]{2,1,0:T(8,128)(2,1)}, u32[]{:S(2)}) copy-start(bf16[8,256,256]{2,1,0:T(8,128)(2,1)} %param.13) | copy-start | bytes 3145732
  68.4 20.0 %copy-start.4 = (bf16[8,256,256]{2,1,0:T(8,128)(2,1)S(1)}, bf16[8,256,256]{2,1,0:T(8,128)(2,1)}, u32[]{:S(2)}) copy-start(bf16[8,256,256]{2,1,0:T(8,128)(2,1)} %param.16) | copy-start | bytes 3145732
  83.0 31.0 %all-to-all-start.1 = ((bf16[16,2,8,16,128]{4,2,3,1,0:T(8,128)(2,1)}), bf16[16,2,8,16,128]{4,2,3,1,0:T(8,128)(2,1)}, u32[]{:S(2)}, u32[]{:S(2)}) async-start(bf16[16,2,8,16,128]{4,2,3,1,0:T(8,128)(2,1)} %copy.158), calls=%async_computation.1 | async-start | bytes 2097152 | tf_op jit(solution)/shard_map/all_to_all | solution.py:55
  120.0 5.2 %copy-start.3 = (bf16[8,256,128]{1,2,0:T(8,128)(2,1)S(1)}, bf16[8,256,128]{1,2,0:T(8,128)(2,1)}, u32[]{:S(2)}) copy-start(bf16[8,256,128]{1,2,0:T(8,128)(2,1)} %copy-done.2) | copy-start | bytes 1572868
  121.0 20.8 %all-to-all-start.2 = ((bf16[16,8,16,128]{3,1,2,0:T(8,128)(2,1)}), bf16[16,8,16,128]{3,1,2,0:T(8,128)(2,1)}, u32[]{:S(2)}, u32[]{:S(2)}) async-start(bf16[16,8,16,128]{3,1,2,0:T(8,128)(2,1)} %bitcast.65), calls=%async_computation.2 | async-start | bytes 1048576 | tf_op jit(solution)/shard_map/all_to_all | solution.py:120
  127.2 20.8 %collective-permute-start.10 = (bf16[8,8,2048]{2,1,0:T(8,128)(2,1)S(1)}, bf16[8,8,2048]{2,1,0:T(8,128)(2,1)S(1)}, u32[]{:S(2)}, u32[]{:S(2)}) collective-permute-start(bf16[8,8,2048]{2,1,0:T(8,128)(2,1)S(1)} %get-tuple-element.4), channel_id=1, source_target_pairs={{0,16},{16,32},{32,48},{48,0},{1,17},{17,33},{33,49},{49,1},{2,18}... | collective-permute-start | bytes 786440 | tf_op jit(solution)/shard_map/ppermute | solution.py:118
  129.3 18.7 %collective-permute-start.11 = (bf16[8,8,2048]{2,1,0:T(8,128)(2,1)S(1)}, bf16[8,8,2048]{2,1,0:T(8,128)(2,1)S(1)}, u32[]{:S(2)}, u32[]{:S(2)}) collective-permute-start(bf16[8,8,2048]{2,1,0:T(8,128)(2,1)S(1)} %get-tuple-element.6), channel_id=1, source_target_pairs={{0,32},{16,48},{32,0},{48,16},{1,33},{17,49},{33,1},{49,17},{2,34}... | collective-permute-start | bytes 786440 | tf_op jit(solution)/shard_map/ppermute | solution.py:118
  134.6 13.4 %collective-permute-start.12 = (bf16[8,8,2048]{2,1,0:T(8,128)(2,1)S(1)}, bf16[8,8,2048]{2,1,0:T(8,128)(2,1)}, u32[]{:S(2)}, u32[]{:S(2)}) collective-permute-start(bf16[8,8,2048]{2,1,0:T(8,128)(2,1)S(1)} %get-tuple-element.5), channel_id=1, source_target_pairs={{0,48},{16,0},{32,16},{48,32},{1,49},{17,1},{33,17},{49,33},{2,50}... | collective-permute-start | bytes 786440 | tf_op jit(solution)/shard_map/ppermute | solution.py:118
  144.3 10.4 %all-to-all-start.3 = ((bf16[8,4,8,512]{3,0,2,1:T(8,128)(2,1)}), bf16[8,4,8,512]{3,0,2,1:T(8,128)(2,1)S(1)}, u32[]{:S(2)}, u32[]{:S(2)}) async-start(bf16[8,4,8,512]{3,0,2,1:T(8,128)(2,1)} %copy.171), calls=%async_computation.3 | async-start | bytes 524288 | tf_op jit(solution)/shard_map/all_to_all | solution.py:212
  (5 other events, 7.1 us)

commit v11 on v8

--- a/solution.py
+++ b/solution.py
@@ -148,7 +148,7 @@
     doc_span = jnp.sum(mine * doc_lengths, axis=1)
     in_slot = position[None, :] < doc_span[:, None]
     source = jnp.where(in_slot, first_row[:, None] + position[None, :], 0)
-    outgoing = jnp.take(targets, source.reshape(-1), axis=0).reshape(
+    outgoing = targets.at[source.reshape(-1)].get(mode="promise_in_bounds").reshape(
         loaders, slot_rows, feature_cols
     )
     arrived = lax.all_to_all(outgoing, DP, split_axis=0, concat_axis=0, tiled=True)

time: 141 us -> 141 us (level)
  no operation moved by 1% of the time
where the time goes in v11:
time: 141 us; the launch traced here: 140 us
  waiting for transfers between devices  53.7 us (38%)
  starting transfers between devices  40.2 us (29%)
  local copies, waits for them, and re-layouts  18.9 us (13%)
  blocking collectives  16.2 us (11%)
  matrix products  6.29 us (4%)
  other arithmetic  3.45 us (2%)
    all_to_all x1, waiting for transfers between devices, curvature(): mixed = lax.all_to_all(stacked, FE, split_axis=0, concat_axis=3, tiled=True)  35.1 us
    all_to_all x1, blocking collectives, per_device(): lax.all_to_all(row_sums, 'y', split_axis=0, concat_axis=0, tiled=True)  16.2 us
    all_to_all x1, starting transfers between devices, curvature(): mixed = lax.all_to_all(stacked, FE, split_axis=0, concat_axis=3, tiled=True)  12.9 us
    all_to_all x1, starting transfers between devices, per_device(): lax.all_to_all(outgoing, DP, split_axis=0, concat_axis=0, tiled=True)  10.5 us
    ppermute x3, starting transfers between devices, curvature(): lax.ppermute(piece, 'x', [(i, (i + shift) % x_size) for i in range(x_size)])  9.21 us
    all_to_all x1, waiting for transfers between devices, per_device(): lax.all_to_all(outgoing, DP, split_axis=0, concat_axis=0, tiled=True)  7.6 us
    all_to_all x1, waiting for transfers between devices, curvature(): lax.all_to_all(back_merged, FE, split_axis=0, concat_axis=2, tiled=True)  5.96 us
    all_to_all x1, waiting for transfers between devices, per_device(): lax.all_to_all(first_part, 'x', split_axis=1, concat_axis=1, tiled=True)  5.07 us
  transfers between devices with their start and end apart: 7, of which 4 were waited for; matrix products, arithmetic and copies ran while one was open for 9% of the time, Pallas kernels for 0%

profile of v11, /device:TPU:1, one launch (start us, length us, event | category | flops | bytes accessed | tf_op | source)
XLA Modules:
  0.0 139.8 jit_solution(16118984906948226423)
XLA Ops:
  0.7 0.9 select_reduce_fusion.2
  1.8 1.9 %gather_fusion = bf16[256,512]{1,0:T(8,128)(2,1)} fusion(bf16[256,512]{1,0:T(8,128)(2,1)S(1)} %copy-done, s32[1024]{0:T(1024)S(1)} %pad_clamp_fusion), kind=kCustom, calls=%fused_computation | custom fusion | bytes 525312 | tf_op jit(solution)/shard_map/gather | solution.py:151
  3.7 10.5 %all-to-all-start = ((bf16[32,8,512]{2,1,0:T(8,128)(2,1)}), bf16[32,8,512]{2,1,0:T(8,128)(2,1)S(1)}, u32[]{:S(2)}, u32[]{:S(2)}) async-start(bf16[32,8,512]{2,1,0:T(8,128)(2,1)} %bitcast.12), calls=%async_computation | async-start | bytes 524288 | tf_op jit(solution)/shard_map/all_to_all | solution.py:154
  17.9 7.6 %all-to-all-done = bf16[32,8,512]{2,1,0:T(8,128)(2,1)S(1)} async-done(((bf16[32,8,512]{2,1,0:T(8,128)(2,1)}), bf16[32,8,512]{2,1,0:T(8,128)(2,1)S(1)}, u32[]{:S(2)}, u32[]{:S(2)}) %all-to-all-start) | async-done | bytes 262176 | tf_op jit(solution)/shard_map/all_to_all | solution.py:154
  26.6 1.3 copy.149
  27.8 12.9 %all-to-all-start.1 = ((bf16[16,3,8,16,128]{4,2,3,1,0:T(8,128)(2,1)}), bf16[16,3,8,16,128]{4,2,3,1,0:T(8,128)(2,1)S(1)}, u32[]{:S(2)}, u32[]{:S(2)}) async-start(bf16[16,3,8,16,128]{4,2,3,1,0:T(8,128)(2,1)} %copy.149), calls=%async_computation.1 | async-start | bytes 3145728 | tf_op jit(solution)/shard_map/all_to_all | solution.py:56
  40.7 1.2 reshape.139
  42.0 2.2 %reshape.140 = bf16[8,16,8,2,256]{4,3,2,1,0:T(2,128)(2,1)} reshape(bf16[8,256,256]{2,1,0:T(8,128)(2,1)} %param.16) | data formatting | bytes 2097152 | tf_op jit(solution)/shard_map/reshape | solution.py:98
  44.2 35.1 %all-to-all-done.1 = bf16[16,3,8,16,128]{4,2,3,1,0:T(8,128)(2,1)S(1)} async-done(((bf16[16,3,8,16,128]{4,2,3,1,0:T(8,128)(2,1)}), bf16[16,3,8,16,128]{4,2,3,1,0:T(8,128)(2,1)S(1)}, u32[]{:S(2)}, u32[]{:S(2)}) %all-to-all-start.1) | async-done | bytes 1572896 | tf_op jit(solution)/shard_map/all_to_all | solution.py:56
  80.5 1.3 fusion.28
  81.8 1.2 copy.182
  83.1 0.9 fusion.10
  87.6 1.0 copy.158
  88.6 4.1 %all-to-all-start.2 = ((bf16[16,8,16,128]{3,1,2,0:T(8,128)(2,1)}), bf16[16,8,16,128]{3,1,2,0:T(8,128)(2,1)}, u32[]{:S(2)}, u32[]{:S(2)}) async-start(bf16[16,8,16,128]{3,1,2,0:T(8,128)(2,1)} %bitcast.38), calls=%async_computation.2 | async-start | bytes 1048576 | tf_op jit(solution)/shard_map/all_to_all | solution.py:120
  94.9 1.9 %collective-permute-start = (bf16[8,8,2048]{2,1,0:T(8,128)(2,1)S(1)}, bf16[8,8,2048]{2,1,0:T(8,128)(2,1)S(1)}, u32[]{:S(2)}, u32[]{:S(2)}) collective-permute-start(bf16[8,8,2048]{2,1,0:T(8,128)(2,1)S(1)} %get-tuple-element.4), channel_id=1, source_target_pairs={{0,16},{16,32},{32,48},{48,0},{1,17},{17,33},{33,49},{49,1},{2,18}... | collective-permute-start | bytes 786440 | tf_op jit(solution)/shard_map/ppermute | solution.py:118
  96.8 4.2 %collective-permute-start.1 = (bf16[8,8,2048]{2,1,0:T(8,128)(2,1)S(1)}, bf16[8,8,2048]{2,1,0:T(8,128)(2,1)S(1)}, u32[]{:S(2)}, u32[]{:S(2)}) collective-permute-start(bf16[8,8,2048]{2,1,0:T(8,128)(2,1)S(1)} %get-tuple-element.6), channel_id=1, source_target_pairs={{0,32},{16,48},{32,0},{48,16},{1,33},{17,49},{33,1},{49,17},{2,34}... | collective-permute-start | bytes 786440 | tf_op jit(solution)/shard_map/ppermute | solution.py:118
  101.0 3.1 %collective-permute-start.2 = (bf16[8,8,2048]{2,1,0:T(8,128)(2,1)S(1)}, bf16[8,8,2048]{2,1,0:T(8,128)(2,1)}, u32[]{:S(2)}, u32[]{:S(2)}) collective-permute-start(bf16[8,8,2048]{2,1,0:T(8,128)(2,1)S(1)} %get-tuple-element.5), channel_id=1, source_target_pairs={{0,48},{16,0},{32,16},{48,32},{1,49},{17,1},{33,17},{49,33},{2,50}... | collective-permute-start | bytes 786440 | tf_op jit(solution)/shard_map/ppermute | solution.py:118
  104.1 6.0 %all-to-all-done.2 = bf16[16,8,16,128]{3,1,2,0:T(8,128)(2,1)} async-done(((bf16[16,8,16,128]{3,1,2,0:T(8,128)(2,1)}), bf16[16,8,16,128]{3,1,2,0:T(8,128)(2,1)}, u32[]{:S(2)}, u32[]{:S(2)}) %all-to-all-start.2) | async-done | bytes 524320 | tf_op jit(solution)/shard_map/all_to_all | solution.py:120
  110.1 1.1 copy.159
  111.7 0.8 copy.161
  112.6 3.4 %all-to-all-start.3 = ((bf16[8,4,8,512]{3,0,2,1:T(8,128)(2,1)}), bf16[8,4,8,512]{3,0,2,1:T(8,128)(2,1)S(1)}, u32[]{:S(2)}, u32[]{:S(2)}) async-start(bf16[8,4,8,512]{3,0,2,1:T(8,128)(2,1)} %copy.161), calls=%async_computation.3 | async-start | bytes 524288 | tf_op jit(solution)/shard_map/all_to_all | solution.py:197
  116.0 1.1 fusion.23
  117.1 5.1 %all-to-all-done.3 = bf16[8,4,8,512]{3,0,2,1:T(8,128)(2,1)S(1)} async-done(((bf16[8,4,8,512]{3,0,2,1:T(8,128)(2,1)}), bf16[8,4,8,512]{3,0,2,1:T(8,128)(2,1)S(1)}, u32[]{:S(2)}, u32[]{:S(2)}) %all-to-all-start.3) | async-done | bytes 262176 | tf_op jit(solution)/shard_map/all_to_all | solution.py:197
  122.3 16.2 %all_to_all.48 = bf16[8,8,2560]{2,1,0:T(8,128)(2,1)S(1)} all-to-all(bf16[8,8,2560]{2,1,0:T(8,128)(2,1)S(1)} %pad_maximum_fusion.1), channel_id=1, replica_groups=mesh['y'=8,'x'=4,'z'=8,'core'=2] {'y'}, dimensions={0} | all-to-all | bytes 655360 | tf_op jit(solution)/shard_map/all_to_all | solution.py:200
  (76 shorter events, 13.6 us)
Async XLA Ops:
  0.6 1.1 copy-start
  0.6 14.5 %copy-start.13 = (bf16[128,512]{1,0:T(8,128)(2,1)S(1)}, bf16[128,512]{1,0:T(8,128)(2,1)}, u32[]{:S(2)}) copy-start(bf16[128,512]{1,0:T(8,128)(2,1)} %param.10) | copy-start | bytes 393220
  1.8 13.5 %copy-start.10 = (bf16[8,64,256]{2,1,0:T(8,128)(2,1)S(1)}, bf16[8,64,256]{2,1,0:T(8,128)(2,1)}, u32[]{:S(2)}) copy-start(bf16[8,64,256]{2,1,0:T(8,128)(2,1)} %param.15) | copy-start | bytes 786436
  1.8 13.8 %copy-start.11 = (bf16[8,64,256]{2,1,0:T(8,128)(2,1)S(1)}, bf16[8,64,256]{2,1,0:T(8,128)(2,1)}, u32[]{:S(2)}) copy-start(bf16[8,64,256]{2,1,0:T(8,128)(2,1)} %param.12) | copy-start | bytes 786436
  3.7 21.8 %all-to-all-start = ((bf16[32,8,512]{2,1,0:T(8,128)(2,1)}), bf16[32,8,512]{2,1,0:T(8,128)(2,1)S(1)}, u32[]{:S(2)}, u32[]{:S(2)}) async-start(bf16[32,8,512]{2,1,0:T(8,128)(2,1)} %bitcast.12), calls=%async_computation | async-start | bytes 524288 | tf_op jit(solution)/shard_map/all_to_all | solution.py:154
  15.6 1.6 %copy-start.12 = (bf16[8,256,64]{1,2,0:T(8,128)(2,1)S(1)}, bf16[8,256,64]{1,2,0:T(8,128)(2,1)}, u32[]{:S(2)}) copy-start(bf16[8,256,64]{1,2,0:T(8,128)(2,1)} %param.14) | copy-start | bytes 786436
  27.8 12.9 %copy-start.2 = (bf16[8,256,256]{2,1,0:T(8,128)(2,1)S(1)}, bf16[8,256,256]{2,1,0:T(8,128)(2,1)}, u32[]{:S(2)}) copy-start(bf16[8,256,256]{2,1,0:T(8,128)(2,1)} %param.13) | copy-start | bytes 3145732
  27.8 51.4 %all-to-all-start.1 = ((bf16[16,3,8,16,128]{4,2,3,1,0:T(8,128)(2,1)}), bf16[16,3,8,16,128]{4,2,3,1,0:T(8,128)(2,1)S(1)}, u32[]{:S(2)}, u32[]{:S(2)}) async-start(bf16[16,3,8,16,128]{4,2,3,1,0:T(8,128)(2,1)} %copy.149), calls=%async_computation.1 | async-start | bytes 3145728 | tf_op jit(solution)/shard_map/all_to_all | solution.py:56
  79.3 1.2 copy-start.3
  80.5 2.6 %copy-start.4 = (bf16[8,256,256]{2,1,0:T(8,128)(2,1)S(1)}, bf16[8,256,256]{2,1,0:T(8,128)(2,1)}, u32[]{:S(2)}) copy-start(bf16[8,256,256]{2,1,0:T(8,128)(2,1)} %param.13) | copy-start | bytes 3145732
  83.1 1.2 copy-start.6
  83.1 1.5 %copy-start.7 = (f32[8,128,256]{2,1,0:T(8,128)S(1)}, f32[8,128,256]{2,1,0:T(8,128)}, u32[]{:S(2)}) copy-start(f32[8,128,256]{2,1,0:T(8,128)} %fusion.28) | copy-start | bytes 3145732
  84.0 2.3 %copy-start.8 = (bf16[8,256,128]{1,2,0:T(8,128)(2,1)}, bf16[8,256,128]{1,2,0:T(8,128)(2,1)S(1)}, u32[]{:S(2)}) copy-start(bf16[8,256,128]{1,2,0:T(8,128)(2,1)S(1)} %get-tuple-element.10) | copy-start | bytes 1572868
  84.6 1.2 copy-start.5
  85.8 1.2 copy-start.1
  87.6 5.2 %copy-start.9 = (bf16[8,256,128]{1,2,0:T(8,128)(2,1)S(1)}, bf16[8,256,128]{1,2,0:T(8,128)(2,1)}, u32[]{:S(2)}) copy-start(bf16[8,256,128]{1,2,0:T(8,128)(2,1)} %copy-done.8) | copy-start | bytes 1572868
  88.6 21.4 %all-to-all-start.2 = ((bf16[16,8,16,128]{3,1,2,0:T(8,128)(2,1)}), bf16[16,8,16,128]{3,1,2,0:T(8,128)(2,1)}, u32[]{:S(2)}, u32[]{:S(2)}) async-start(bf16[16,8,16,128]{3,1,2,0:T(8,128)(2,1)} %bitcast.38), calls=%async_computation.2 | async-start | bytes 1048576 | tf_op jit(solution)/shard_map/all_to_all | solution.py:120
  94.9 21.1 %collective-permute-start = (bf16[8,8,2048]{2,1,0:T(8,128)(2,1)S(1)}, bf16[8,8,2048]{2,1,0:T(8,128)(2,1)S(1)}, u32[]{:S(2)}, u32[]{:S(2)}) collective-permute-start(bf16[8,8,2048]{2,1,0:T(8,128)(2,1)S(1)} %get-tuple-element.4), channel_id=1, source_target_pairs={{0,16},{16,32},{32,48},{48,0},{1,17},{17,33},{33,49},{49,1},{2,18}... | collective-permute-start | bytes 786440 | tf_op jit(solution)/shard_map/ppermute | solution.py:118
  96.8 19.2 %collective-permute-start.1 = (bf16[8,8,2048]{2,1,0:T(8,128)(2,1)S(1)}, bf16[8,8,2048]{2,1,0:T(8,128)(2,1)S(1)}, u32[]{:S(2)}, u32[]{:S(2)}) collective-permute-start(bf16[8,8,2048]{2,1,0:T(8,128)(2,1)S(1)} %get-tuple-element.6), channel_id=1, source_target_pairs={{0,32},{16,48},{32,0},{48,16},{1,33},{17,49},{33,1},{49,17},{2,34}... | collective-permute-start | bytes 786440 | tf_op jit(solution)/shard_map/ppermute | solution.py:118
  101.0 15.0 %collective-permute-start.2 = (bf16[8,8,2048]{2,1,0:T(8,128)(2,1)S(1)}, bf16[8,8,2048]{2,1,0:T(8,128)(2,1)}, u32[]{:S(2)}, u32[]{:S(2)}) collective-permute-start(bf16[8,8,2048]{2,1,0:T(8,128)(2,1)S(1)} %get-tuple-element.5), channel_id=1, source_target_pairs={{0,48},{16,0},{32,16},{48,32},{1,49},{17,1},{33,17},{49,33},{2,50}... | collective-permute-start | bytes 786440 | tf_op jit(solution)/shard_map/ppermute | solution.py:118
  112.6 9.6 %all-to-all-start.3 = ((bf16[8,4,8,512]{3,0,2,1:T(8,128)(2,1)}), bf16[8,4,8,512]{3,0,2,1:T(8,128)(2,1)S(1)}, u32[]{:S(2)}, u32[]{:S(2)}) async-start(bf16[8,4,8,512]{3,0,2,1:T(8,128)(2,1)} %copy.161), calls=%async_computation.3 | async-start | bytes 524288 | tf_op jit(solution)/shard_map/all_to_all | solution.py:197
